TPU v7x, 32 devices: a whole 2x2x4 slice. The times are simulated.
32 devices in a mesh: tm: 4 (over z), space: 2 (over y), hyp: 4 (over x, core).
Axes of the slice: x: 2, y: 2, z: 4, core: 2. Of those that a mesh axis runs over, the one named last changes fastest.
Arguments:
- log_kappa: float32 [8192], P('space'), may hold values from -0.5 to 0.5
- node_mass: float32 [8192], P('space'), may hold values from 0.5 to 2
- rho_base: float32 [8192], P('space'), may hold values from 1.5 to 4
- edge_weight: float32 [4, 8192], P(None, 'space'), may hold values from 0.05 to 0.3
- offsets: int32 [4, 8192], P(None, 'space'), may hold values from -64 to 64
- roughness: float32 [64, 8192], P('tm', 'space'), may hold values from 0.5 to 1.0002
- coupling: float32 [64, 8192], P('tm', 'space'), may hold values from 0.5 to 1
- obs_weight: float32 [64, 8192], P('tm', 'space'), may hold values from 0.0003 to 0.03
- observed: float32 [64, 8192], P('tm', 'space'), may hold values from -0.3125 to 0.3125
- hyper_params: float32 [4], replicated, may hold values from -0.3 to 0.3
Outputs:
- solution: float32 [64, 8192], P('tm', ('space', 'hyp'))
- log_det_mean: float32 [8192], P('space')
- gradient: float32 [4, 8192], P(None, 'space')
Inputs may be any that keep to these rules, and one draw needn't show every extreme that they name: offsets[k, i] is a band offset from node i to a listed neighbour.
All inputs are finite; a program needn't handle non-finite values.
Results may differ from a plain program's by a relative error of at most 0.0003.
Values sent between devices are 32-bit elements; how exact they have to be, the bound alone decides.
No kernel may reach another device: no remote copies, remote signals or barrier semaphores. Data moves between devices by JAX's collectives and lax.ppermute only.
A program may use at most 64 MiB of HBM per device.

v0:
```python
import jax
import jax.numpy as jnp
from jax import lax
from jax.sharding import PartitionSpec as P

BAND = 64


def with_halo(block, sides, width):
    for axis, dim in sides:
        count = lax.axis_size(axis)
        forward = [(i, i + 1) for i in range(count - 1)]
        backward = [(target, source) for source, target in forward]
        low = lax.ppermute(
            lax.slice_in_dim(block, block.shape[dim] - width, None, axis=dim), axis, forward
        )
        high = lax.ppermute(lax.slice_in_dim(block, 0, width, axis=dim), axis, backward)
        block = jnp.concatenate([low, block, high], axis=dim)
    return block


def prefix(part, axis, combine, identity, reverse):
    count = lax.axis_size(axis)
    place = lax.axis_index(axis)
    ahead = count - 1 - place if reverse else place
    gathered = jax.tree.map(lambda a: lax.all_gather(a, axis), part)
    state = jax.tree.map(lambda a, e: jnp.zeros_like(a) + jnp.asarray(e, a.dtype), part, identity)

    def one(hop, state):
        source = count - 1 - hop if reverse else hop
        return combine(
            state, jax.tree.map(lambda a: lax.dynamic_index_in_dim(a, source, 0, False), gathered)
        )

    return lax.fori_loop(0, ahead, one, state)


def row_terms(scaled, persist, roughness, coupling, obs_weight, nugget_scale, later_rows):
    prior = scaled * (1.0 + persist * persist) * roughness
    nugget = nugget_scale * obs_weight
    diagonal = prior + nugget
    offdiag = -persist * scaled * coupling * later_rows
    slopes = jnp.stack(
        [
            2.0 * prior,
            prior,
            2.0 * persist * (1.0 - persist * persist) * scaled * roughness,
            nugget,
        ],
        axis=-2,
    )
    return (diagonal, offdiag, slopes)


def mobius_join(earlier_part, later_part):
    upper_left = later_part[0] * earlier_part[0] + later_part[1] * earlier_part[2]
    upper_right = later_part[0] * earlier_part[1] + later_part[1] * earlier_part[3]
    lower_left = later_part[2] * earlier_part[0] + later_part[3] * earlier_part[2]
    lower_right = later_part[2] * earlier_part[1] + later_part[3] * earlier_part[3]
    norm_total = (
        jnp.abs(upper_left) + jnp.abs(upper_right) + jnp.abs(lower_left) + jnp.abs(lower_right)
    )
    return (
        upper_left / norm_total,
        upper_right / norm_total,
        lower_left / norm_total,
        lower_right / norm_total,
    )


def affine_join(earlier_part, later_part):
    joined = []
    for index in range(0, len(earlier_part), 2):
        joined.append(later_part[index] * earlier_part[index])
        joined.append(later_part[index] * earlier_part[index + 1] + later_part[index + 1])
    return tuple(joined)


def mobius_step(carried, step_rows):
    diag_row, off_row = step_rows
    step_map = (diag_row, -off_row * off_row, jnp.ones_like(diag_row), jnp.zeros_like(diag_row))
    return (mobius_join(carried, step_map), None)


def per_device(
    log_kappa,
    node_mass,
    rho_base,
    edge_weight,
    offsets,
    roughness,
    coupling,
    obs_weight,
    observed,
    hyper_params,
):
    row_count, full_width = roughness.shape
    kappa_sq = jnp.exp(2.0 * log_kappa)
    padded = with_halo(kappa_sq, (("space", 0),), BAND)
    indices = jnp.arange(full_width, dtype=jnp.int32)[None, :] + BAND + offsets
    nearby = jnp.take(padded, indices)
    spatial = jnp.exp(2.0 * hyper_params[0]) * (
        node_mass * kappa_sq + jnp.sum(edge_weight * nearby, axis=0)
    )
    scaled = jnp.exp(hyper_params[1]) * spatial
    persist = jnp.tanh(hyper_params[2] + rho_base)
    nugget_scale = jnp.exp(hyper_params[3])
    log_slope = jnp.stack(
        [
            2.0 * jnp.ones_like(persist),
            jnp.ones_like(persist),
            (1.0 - persist * persist) / persist,
            jnp.zeros_like(persist),
        ]
    )
    hyp_count = lax.axis_size("hyp")
    hyp_place = lax.axis_index("hyp")
    quarter = full_width // hyp_count
    time_count = lax.axis_size("tm")
    global_rows = jnp.arange(row_count, dtype=jnp.int32) + lax.axis_index("tm") * row_count
    later_rows = (global_rows > 0).astype(jnp.float32)[:, None]
    diagonal, offdiag, slopes = row_terms(
        scaled, persist, roughness, coupling, obs_weight, nugget_scale, later_rows
    )
    slopes = lax.dynamic_index_in_dim(slopes, hyp_place, 1, keepdims=True)
    log_slope = lax.dynamic_index_in_dim(log_slope, hyp_place, 0, keepdims=True)
    ones_row = jnp.ones_like(diagonal[0])
    zeros_row = jnp.zeros_like(diagonal[0])
    zeros_dir = jnp.zeros_like(log_slope)
    identity = (ones_row, zeros_row, zeros_row, ones_row)
    local_map, unused = lax.scan(mobius_step, identity, (diagonal, offdiag))
    before = prefix(local_map, "tm", mobius_join, identity, False)
    inverse_in = before[2] / before[0]

    def forward_step(carried, step_rows):
        inverse, gain_tangent, tangent_loc, gain_solve, solve_loc = carried
        diag_row, off_row, slope_row, observed_row = step_rows
        pivots = diag_row - off_row * off_row * inverse
        ratios = off_row * inverse
        gain_tangent = ratios * ratios * gain_tangent
        tangent_loc = ratios * ratios * tangent_loc + slope_row - 2.0 * log_slope * off_row * ratios
        gain_solve = -ratios * gain_solve
        solve_loc = observed_row - ratios * solve_loc
        return (
            (1.0 / pivots, gain_tangent, tangent_loc, gain_solve, solve_loc),
            (pivots, gain_tangent, tangent_loc, gain_solve, solve_loc),
        )

    start = (inverse_in, ones_row, zeros_dir, ones_row, zeros_row)
    ending, stacked = lax.scan(forward_step, start, (diagonal, offdiag, slopes, observed))
    pivots, gains_tangent, tangent_locs, gains_solve, solve_locs = stacked
    incoming = prefix(
        (ending[1], ending[2], ending[3], ending[4]),
        "tm",
        affine_join,
        (ones_row, zeros_dir, ones_row, zeros_row),
        False,
    )
    tangents = tangent_locs + gains_tangent[:, None, :] * incoming[1][None]
    solveds = solve_locs + gains_solve * incoming[3][None]

    def backward_step(carried, step_rows):
        next_loc, next_gain = carried
        off_row, pivot_row, solved_row = step_rows
        return (
            (off_row * (solved_row - next_loc) / pivot_row, -off_row / pivot_row * next_gain),
            (next_loc, next_gain),
        )

    front, trailing = lax.scan(
        backward_step, (zeros_row, ones_row), (offdiag, pivots, solveds), reverse=True
    )
    next_locs, next_gains = trailing
    after = prefix((front[1], front[0]), "tm", affine_join, (ones_row, zeros_row), True)
    carried_next = next_locs + next_gains * after[1][None]
    solution = (solveds - carried_next) / pivots
    total_rows = row_count * time_count
    scores = jnp.sum(0.5 * tangents / pivots[:, None, :], axis=0)
    quadratic = jnp.sum(
        slopes * (solution * solution)[:, None, :]
        + 2.0 * log_slope[None] * (solution * carried_next)[:, None, :],
        axis=0,
    )
    gradient_part = (scores - 0.5 * quadratic) / total_rows
    logdet_part = jnp.sum(jnp.log(pivots), axis=0) / total_rows
    direction_mask = (jnp.arange(hyp_count, dtype=jnp.int32) == hyp_place).astype(jnp.float32)[
        :, None
    ]
    leader_mask = (hyp_place == 0).astype(jnp.float32)
    placed = jnp.concatenate(
        [(leader_mask * logdet_part)[None], direction_mask * gradient_part], axis=0
    )
    solution_out = lax.dynamic_slice_in_dim(
        solution, hyp_place * quarter, quarter, solution.ndim - 1
    )
    totals = lax.psum(placed, ("tm", "hyp"))
    return (solution_out, totals[0], totals[1:])


def solution(mesh):
    placed = (
        P("space"),
        P("space"),
        P("space"),
        P(None, "space"),
        P(None, "space"),
        P("tm", "space"),
        P("tm", "space"),
        P("tm", "space"),
        P("tm", "space"),
        P(),
    )
    return jax.shard_map(
        per_device,
        mesh=mesh,
        in_specs=placed,
        out_specs=(P("tm", ("space", "hyp")), P("space"), P(None, "space")),
        check_vma=False,
    )
```

profile of v0, /device:TPU:0, one launch (start us, length us, event | category | flops | bytes accessed | tf_op | source)
XLA Modules:
  0.0 406.8 jit_solution(9264937598001699120)
XLA Ops:
  8.0 4.9 %collective-permute-start = (f32[64]{0:T(128)S(1)}, f32[64]{0:T(128)S(1)}, u32[]{:S(2)}, u32[]{:S(2)}) collective-permute-start(f32[64]{0:T(128)S(1)} %get-tuple-element.865), channel_id=1, source_target_pairs={{0,4},{1,5},{2,6},{3,7},{8,12},{9,13},{10,14},{11,15},{16,20},{17,... | collective-permute-start | bytes 776 | tf_op jit(solution)/shard_map/ppermute | solution.py:14
  12.9 1.3 collective-permute-start.1
  18.6 90.5 %gather_fusion = f32[16384]{0:T(1024)S(1)} fusion(f32[4224]{0:T(1024)S(1)} %concatenate.6, s32[16384]{0:T(1024)S(1)} %broadcast_clamp_fusion), kind=kCustom, calls=%fused_computation | custom fusion | bytes 196608 | tf_op jit(solution)/shard_map/jit(_take)/gather | solution.py:101
  110.8 2.1 while.116
  112.9 13.4 %all-gather = f32[16384]{0:T(1024)S(1)} all-gather(f32[4096]{0:T(1024)S(1)} %get-tuple-element.526), channel_id=2, replica_groups=mesh['tm'=4,'space'=2,'hyp'=4] {'tm'}, dimensions={0}, use_global_device_ids=true | all-gather | bytes 81920 | tf_op jit(solution)/shard_map/all_gather | solution.py:26
  126.3 13.2 %all-gather.1 = f32[16384]{0:T(1024)S(1)} all-gather(f32[4096]{0:T(1024)S(1)} %get-tuple-element.527), channel_id=3, replica_groups=mesh['tm'=4,'space'=2,'hyp'=4] {'tm'}, dimensions={0}, use_global_device_ids=true | all-gather | bytes 81920 | tf_op jit(solution)/shard_map/all_gather | solution.py:26
  139.5 13.3 %all-gather.2 = f32[16384]{0:T(1024)S(1)} all-gather(f32[4096]{0:T(1024)S(1)} %get-tuple-element.528), channel_id=4, replica_groups=mesh['tm'=4,'space'=2,'hyp'=4] {'tm'}, dimensions={0}, use_global_device_ids=true | all-gather | bytes 81920 | tf_op jit(solution)/shard_map/all_gather | solution.py:26
  152.8 13.2 %all-gather.3 = f32[16384]{0:T(1024)S(1)} all-gather(f32[4096]{0:T(1024)S(1)} %get-tuple-element.529), channel_id=5, replica_groups=mesh['tm'=4,'space'=2,'hyp'=4] {'tm'}, dimensions={0}, use_global_device_ids=true | all-gather | bytes 81920 | tf_op jit(solution)/shard_map/all_gather | solution.py:26
  167.0 43.2 %while.117 = (s32[]{:T(128)}, f32[4096]{0:T(1024)S(1)}, f32[4096]{0:T(1024)S(1)}, f32[1,4096]{1,0:T(1,128)S(1)}, f32[4096]{0:T(1024)S(1)}, /*index=5*/f32[4096]{...) while((s32[]{:T(128)}, f32[4096]{0:T(1024)S(1)}, ...), condition=%wide.region_6.7_spmd.clone, body=%wide.region_5.6_spmd.clone.sunk | while | flops 86019 | bytes 606413 | solution.py:150
  167.0 0.9 constant_dynamic-slice_fusion.31
  169.7 0.9 constant_dynamic-slice_fusion.31
  172.4 0.9 constant_dynamic-slice_fusion.31
  175.1 0.9 constant_dynamic-slice_fusion.31
  177.8 0.9 constant_dynamic-slice_fusion.31
  180.5 0.9 constant_dynamic-slice_fusion.31
  183.2 0.9 constant_dynamic-slice_fusion.31
  185.9 0.9 constant_dynamic-slice_fusion.31
  188.6 0.9 constant_dynamic-slice_fusion.31
  191.4 0.9 constant_dynamic-slice_fusion.31
  194.1 0.9 constant_dynamic-slice_fusion.31
  196.8 0.9 constant_dynamic-slice_fusion.31
  204.9 0.9 constant_dynamic-slice_fusion.31
  210.3 13.1 %all-gather.4 = f32[16384]{0:T(1024)S(1)} all-gather(f32[4096]{0:T(1024)S(1)} %get-tuple-element.534), channel_id=6, replica_groups=mesh['tm'=4,'space'=2,'hyp'=4] {'tm'}, dimensions={0}, use_global_device_ids=true | all-gather | bytes 81920 | tf_op jit(solution)/shard_map/all_gather | solution.py:26
  223.4 13.1 %all-gather.6 = f32[16384]{0:T(1024)S(1)} all-gather(f32[4096]{0:T(1024)S(1)} %get-tuple-element.536), channel_id=8, replica_groups=mesh['tm'=4,'space'=2,'hyp'=4] {'tm'}, dimensions={0}, use_global_device_ids=true | all-gather | bytes 81920 | tf_op jit(solution)/shard_map/all_gather | solution.py:26
  236.6 13.2 %all-gather.7 = f32[16384]{0:T(1024)S(1)} all-gather(f32[4096]{0:T(1024)S(1)} %get-tuple-element.537), channel_id=9, replica_groups=mesh['tm'=4,'space'=2,'hyp'=4] {'tm'}, dimensions={0}, use_global_device_ids=true | all-gather | bytes 81920 | tf_op jit(solution)/shard_map/all_gather | solution.py:26
  249.8 13.1 %all-gather.10 = f32[4,1,4096]{2,1,0:T(1,128)S(1)} all-gather(f32[1,1,4096]{2,1,0:T(1,128)S(1)} %bitcast.142), channel_id=7, replica_groups=mesh['tm'=4,'space'=2,'hyp'=4] {'tm'}, dimensions={0}, use_global_device_ids=true | all-gather | bytes 81920 | tf_op jit(solution)/shard_map/all_gather | solution.py:26
  263.1 14.6 %while.118 = (s32[]{:T(128)}, f32[4096]{0:T(1024)S(1)}, f32[4096]{0:T(1024)S(1)}, f32[16,4096]{1,0:T(8,128)S(1)}, f32[16,4096]{1,0:T(8,128)S(1)}, /*index=5*/f32...) while((s32[]{:T(128)}, f32[4096]{0:T(1024)S(1)}, ...), condition=%wide.region_10.11_spmd.clone, body=%wide.region_9.10_spmd.clone.sunk | while | flops 32772 | bytes 311443 | solution.py:170
  277.8 13.5 %all-gather.8 = f32[16384]{0:T(1024)S(1)} all-gather(f32[4096]{0:T(1024)S(1)} %get-tuple-element.542), channel_id=10, replica_groups=mesh['tm'=4,'space'=2,'hyp'=4] {'tm'}, dimensions={0}, use_global_device_ids=true | all-gather | bytes 81920 | tf_op jit(solution)/shard_map/all_gather | solution.py:26
  291.3 13.1 %all-gather.9 = f32[16384]{0:T(1024)S(1)} all-gather(f32[4096]{0:T(1024)S(1)} %get-tuple-element.543), channel_id=11, replica_groups=mesh['tm'=4,'space'=2,'hyp'=4] {'tm'}, dimensions={0}, use_global_device_ids=true | all-gather | bytes 81920 | tf_op jit(solution)/shard_map/all_gather | solution.py:26
  306.8 90.1 %all-reduce.2.cloned.1.call-done = f32[5,4096]{1,0:T(8,128)} async-done(((f32[5,4096]{1,0:T(8,128)}), f32[5,4096]{1,0:T(8,128)}) %all-reduce.2.cloned.1.call-update) | async-done | bytes 81936 | tf_op jit(solution)/shard_map/psum | solution.py:196
  396.9 1.6 slice.37
  398.5 1.5 slice.36
  (370 shorter events, 53.0 us)
Async XLA Ops:
  7.2 7.2 %copy-start.3 = (s32[4,4096]{1,0:T(4,128)S(1)}, s32[4,4096]{1,0:T(4,128)}, u32[]{:S(2)}) copy-start(s32[4,4096]{1,0:T(4,128)} %param.26) | copy-start | bytes 196612
  7.2 389.7 %all-reduce.2.cloned.1.call-start = ((), (), s32[]{:S(2)}) async-start(), calls=%async_computation | async-start | bytes 262144 | tf_op jit(solution)/shard_map/psum | solution.py:196
  8.0 10.4 %collective-permute-start = (f32[64]{0:T(128)S(1)}, f32[64]{0:T(128)S(1)}, u32[]{:S(2)}, u32[]{:S(2)}) collective-permute-start(f32[64]{0:T(128)S(1)} %get-tuple-element.865), channel_id=1, source_target_pairs={{0,4},{1,5},{2,6},{3,7},{8,12},{9,13},{10,14},{11,15},{16,20},{17,... | collective-permute-start | bytes 776 | tf_op jit(solution)/shard_map/ppermute | solution.py:14
  12.9 5.5 %collective-permute-start.1 = (f32[64]{0:T(128)S(1)}, f32[64]{0:T(128)S(1)}, u32[]{:S(2)}, u32[]{:S(2)}) collective-permute-start(f32[64]{0:T(128)S(1)} %get-tuple-element.864), channel_id=1, source_target_pairs={{4,0},{5,1},{6,2},{7,3},{12,8},{13,9},{14,10},{15,11},{20,16},{21,... | collective-permute-start | bytes 776 | tf_op jit(solution)/shard_map/ppermute | solution.py:17
  14.4 0.7 copy-start.8
  18.5 90.7 %copy-start.4 = (f32[4,4096]{1,0:T(4,128)S(1)}, f32[4,4096]{1,0:T(4,128)}, u32[]{:S(2)}) copy-start(f32[4,4096]{1,0:T(4,128)} %param.25) | copy-start | bytes 196612
  18.5 90.8 %copy-start.5 = (f32[4096]{0:T(1024)S(1)}, f32[4096]{0:T(1024)}, u32[]{:S(2)}) copy-start(f32[4096]{0:T(1024)} %param.24) | copy-start | bytes 49156
  18.5 90.7 %copy-start.6 = (f32[4096]{0:T(1024)S(1)}, f32[4096]{0:T(1024)}, u32[]{:S(2)}) copy-start(f32[4096]{0:T(1024)} %param.22) | copy-start | bytes 49156
  18.6 90.7 %copy-start.7 = (f32[4096]{0:T(1024)S(1)}, f32[4096]{0:T(1024)}, u32[]{:S(2)}) copy-start(f32[4096]{0:T(1024)} %param.23) | copy-start | bytes 49156
  18.6 92.1 %copy-start.2 = (f32[16,4096]{1,0:T(8,128)S(1)}, f32[16,4096]{1,0:T(8,128)}, u32[]{:S(2)}) copy-start(f32[16,4096]{1,0:T(8,128)} %param.28) | copy-start | bytes 786436
  109.1 1.5 copy-start
  109.1 1.5 copy-start.1
Sparse Core Ops, SparseCore 0:
  306.3 90.5 all-reduce.1
where the time goes:
time: 408 us; the launch traced here: 407 us
  local copies, waits for them, and re-layouts  151 us (37%)
  blocking collectives  132 us (32%)
  waiting for transfers between devices  90.1 us (22%)
  between operations  16.7 us (4%)
  other arithmetic  7.23 us (2%)
  starting transfers between devices  6.22 us (2%)
    all_gather x10, blocking collectives, prefix(): gathered = jax.tree.map(lambda a: lax.all_gather(a, axis), part)  132 us
    gather x2, local copies, waits for them, and re-layouts, per_device(): nearby = jnp.take(padded, indices)  90.6 us
    psum x1, waiting for transfers between devices, per_device(): totals = lax.psum(placed, ('tm', 'hyp'))  90.1 us
    dynamic_update_slice x96, local copies, waits for them, and re-layouts, per_device(): lax.scan(forward_step, start, (diagonal, offdiag, slopes, observed))  37.7 us
    dynamic_slice x80, local copies, waits for them, and re-layouts, per_device(): local_map, unused = lax.scan(mobius_step, identity, (diagonal, offdiag))  16.6 us
  transfers between devices with their start and end apart: 3, of which 1 were waited for; matrix products, arithmetic and copies ran while one was open for 1% of the time, Pallas kernels for 0%

commit v1 on v0

v1 whole, which is shorter than its diff:
```python
import jax
import jax.numpy as jnp
from jax import lax
from jax.experimental import pallas as pl
from jax.experimental.pallas import tpu as pltpu
from jax.sharding import PartitionSpec as P

BAND = 64
INTERPRET = False


def with_halo(block, sides, width):
    for axis, dim in sides:
        count = lax.axis_size(axis)
        forward = [(i, i + 1) for i in range(count - 1)]
        backward = [(target, source) for source, target in forward]
        low = lax.ppermute(
            lax.slice_in_dim(block, block.shape[dim] - width, None, axis=dim), axis, forward
        )
        high = lax.ppermute(lax.slice_in_dim(block, 0, width, axis=dim), axis, backward)
        block = jnp.concatenate([low, block, high], axis=dim)
    return block


def chain_kernel(data_ref, par_ref, sol_ref, stat_ref, piv_ref, slv_ref):
    rows = data_ref.shape[1]
    ns = par_ref[2:3, :]
    ls2 = par_ref[3:4, :]
    sp = par_ref[4:5, :]
    mps = par_ref[5:6, :]
    qs = par_ref[6:7, :]
    two_ls2 = 2.0 * ls2
    zeros = jnp.zeros_like(sp)

    def forward(t, carry):
        inv, t0, t1, t2, t3, solved, c0, c1, c2, c3, logs = carry
        rough = data_ref[0, pl.ds(t, 1), :]
        coup = data_ref[1, pl.ds(t, 1), :]
        weight = data_ref[2, pl.ds(t, 1), :]
        obs = data_ref[3, pl.ds(t, 1), :]
        prior = sp * rough
        nugget = ns * weight
        diagonal = prior + nugget
        offdiag = mps * coup
        pivots = diagonal - offdiag * offdiag * inv
        ratios = offdiag * inv
        rr = ratios * ratios
        t0 = rr * t0 + 2.0 * prior - 4.0 * offdiag * ratios
        t1 = rr * t1 + prior - 2.0 * offdiag * ratios
        t2 = rr * t2 + qs * rough - two_ls2 * offdiag * ratios
        t3 = rr * t3 + nugget
        solved = obs - ratios * solved
        c0 = c0 + 0.5 * t0 / pivots
        c1 = c1 + 0.5 * t1 / pivots
        c2 = c2 + 0.5 * t2 / pivots
        c3 = c3 + 0.5 * t3 / pivots
        logs = logs + jnp.log(pivots)
        piv_ref[pl.ds(t, 1), :] = pivots
        slv_ref[pl.ds(t, 1), :] = solved
        return (1.0 / pivots, t0, t1, t2, t3, solved, c0, c1, c2, c3, logs)

    start = (zeros,) * 11
    ending = lax.fori_loop(0, rows, forward, start, unroll=8)
    c0, c1, c2, c3, logs = ending[6:]

    def backward(i, carry):
        t = rows - 1 - i
        following, q0, q1, q2, q3 = carry
        rough = data_ref[0, pl.ds(t, 1), :]
        coup = data_ref[1, pl.ds(t, 1), :]
        weight = data_ref[2, pl.ds(t, 1), :]
        prior = sp * rough
        nugget = ns * weight
        offdiag = mps * coup
        values = (slv_ref[pl.ds(t, 1), :] - following) / piv_ref[pl.ds(t, 1), :]
        q0 = q0 + 2.0 * prior * values * values + 4.0 * values * following
        q1 = q1 + prior * values * values + 2.0 * values * following
        q2 = q2 + qs * rough * values * values + two_ls2 * values * following
        q3 = q3 + nugget * values * values
        sol_ref[pl.ds(t, 1), :] = values
        return (offdiag * values, q0, q1, q2, q3)

    closing = lax.fori_loop(0, rows, backward, (zeros,) * 5, unroll=8)
    q0, q1, q2, q3 = closing[1:]
    scale = 1.0 / rows
    stat_ref[0:1, :] = logs * scale
    stat_ref[1:2, :] = (c0 - 0.5 * q0) * scale
    stat_ref[2:3, :] = (c1 - 0.5 * q1) * scale
    stat_ref[3:4, :] = (c2 - 0.5 * q2) * scale
    stat_ref[4:5, :] = (c3 - 0.5 * q3) * scale
    stat_ref[5:8, :] = jnp.zeros((3, sp.shape[1]), jnp.float32)


def run_chain(data, params):
    _, rows, width = data.shape
    vmem = pl.BlockSpec(memory_space=pltpu.VMEM)
    return pl.pallas_call(
        chain_kernel,
        out_shape=(
            jax.ShapeDtypeStruct((rows, width), jnp.float32),
            jax.ShapeDtypeStruct((8, width), jnp.float32),
        ),
        in_specs=[vmem, vmem],
        out_specs=(vmem, vmem),
        scratch_shapes=[pltpu.VMEM((rows, width), jnp.float32)] * 2,
        interpret=INTERPRET,
    )(data, params)


def per_device(
    log_kappa,
    node_mass,
    rho_base,
    edge_weight,
    offsets,
    roughness,
    coupling,
    obs_weight,
    observed,
    hyper_params,
):
    row_count, full_width = roughness.shape
    time_count = lax.axis_size("tm")
    hyp_count = lax.axis_size("hyp")
    time_place = lax.axis_index("tm")
    hyp_place = lax.axis_index("hyp")
    quarter = full_width // hyp_count
    chunk = quarter // time_count
    first = hyp_place * quarter + time_place * chunk

    stacked = jnp.stack([roughness, coupling, obs_weight, observed])
    mine = lax.dynamic_slice_in_dim(stacked, hyp_place * quarter, quarter, axis=2)
    data = lax.all_to_all(mine, "tm", 2, 1, tiled=True)

    kappa_sq = jnp.exp(2.0 * log_kappa)
    padded = with_halo(kappa_sq, (("space", 0),), BAND)
    window = lax.dynamic_slice_in_dim(padded, first, chunk + 2 * BAND)
    near_off = lax.dynamic_slice_in_dim(offsets, first, chunk, axis=1)
    weights = lax.dynamic_slice_in_dim(edge_weight, first, chunk, axis=1)
    mass = lax.dynamic_slice_in_dim(node_mass, first, chunk)
    base = lax.dynamic_slice_in_dim(rho_base, first, chunk)
    own_kappa = window[BAND : BAND + chunk]
    nearby = jnp.zeros(near_off.shape, jnp.float32)
    for shift in range(-BAND, BAND + 1):
        nearby = jnp.where(
            near_off == shift, window[None, BAND + shift : BAND + shift + chunk], nearby
        )
    spatial = jnp.exp(2.0 * hyper_params[0]) * (
        mass * own_kappa + jnp.sum(weights * nearby, axis=0)
    )
    scaled = jnp.exp(hyper_params[1]) * spatial
    persist = jnp.tanh(hyper_params[2] + base)
    nugget_scale = jnp.exp(hyper_params[3]) + jnp.zeros_like(persist)
    log_slope = (1.0 - persist * persist) / persist
    params = jnp.stack(
        [
            scaled,
            persist,
            nugget_scale,
            log_slope,
            scaled * (1.0 + persist * persist),
            -persist * scaled,
            2.0 * persist * (1.0 - persist * persist) * scaled,
            jnp.zeros_like(persist),
        ]
    )
    solution_rows, stats = run_chain(data, params)

    parts = solution_rows.reshape(time_count, row_count, chunk)
    payload = jnp.concatenate(
        [parts, jnp.broadcast_to(stats[None], (time_count,) + stats.shape)], axis=1
    )
    received = lax.all_to_all(payload, "tm", 0, 2, tiled=True)[0]
    solution_out = received[:row_count]
    stats_quarter = received[row_count : row_count + 5]
    stats_full = lax.all_gather(stats_quarter, "hyp", axis=1, tiled=True)
    return (solution_out, stats_full[0], stats_full[1:5])


def solution(mesh):
    placed = (
        P("space"),
        P("space"),
        P("space"),
        P(None, "space"),
        P(None, "space"),
        P("tm", "space"),
        P("tm", "space"),
        P("tm", "space"),
        P("tm", "space"),
        P(),
    )
    return jax.shard_map(
        per_device,
        mesh=mesh,
        in_specs=placed,
        out_specs=(P("tm", ("space", "hyp")), P("space"), P(None, "space")),
        check_vma=False,
    )
```

time: 408 us -> 51.9 us (0.13)
  local copies, waits for them, and re-layouts: 151 us -> 11.3 us
  blocking collectives: 132 us -> 16.1 us
  waiting for transfers between devices: 90.1 us -> 1.4 us
  between operations: 16.7 us -> 2.87 us
  starting transfers between devices: 6.22 us -> 11.1 us
    all_gather x10 -> x1, blocking collectives: 132 us -> 5.42 us  [per_device(): stats_full = lax.all_gather(stats_quarter, 'hyp', axis=1, tiled=True)]
    gather x2 -> x0, local copies, waits for them, and re-layouts: 90.6 us -> none  [per_device(): nearby = jnp.take(padded, indices)]
    psum x1 -> x0, waiting for transfers between devices: 90.1 us -> none  [per_device(): totals = lax.psum(placed, ('tm', 'hyp'))]
    dynamic_update_slice x96 -> x0, local copies, waits for them, and re-layouts: 37.7 us -> none  [per_device(): lax.scan(forward_step, start, (diagonal, offdiag, slopes, observed))]
    dynamic_slice x85 -> x1, local copies, waits for them, and re-layouts: 17.9 us -> 0.08 us  [per_device(): window = lax.dynamic_slice_in_dim(padded, first, chunk + 2 * BAND)]
    all_to_all x0 -> x1, blocking collectives: none -> 10.7 us  [per_device(): received = lax.all_to_all(payload, 'tm', 0, 2, tiled=True)[0]]
    all_to_all x0 -> x1, starting transfers between devices: none -> 6.35 us  [per_device(): data = lax.all_to_all(mine, 'tm', 2, 1, tiled=True)]
    unnamed x19 -> x8, local copies, waits for them, and re-layouts: 0.68 us -> 5.26 us
  transfers between devices with their start and end apart: 3 -> 3, of which waited for: 1 -> 1; matrix products, arithmetic and copies ran while one was open for 1% -> 10% of each run, Pallas kernels for 0% -> 0%
where the time goes in v1:
time: 51.9 us; the launch traced here: 51.3 us
  blocking collectives  16.1 us (31%)
  local copies, waits for them, and re-layouts  11.3 us (22%)
  starting transfers between devices  11.1 us (21%)
  other arithmetic  5.98 us (12%)
  between operations  2.87 us (6%)
  Pallas kernels  2.56 us (5%)
  waiting for transfers between devices  1.4 us (3%)
    all_to_all x1, blocking collectives, per_device(): received = lax.all_to_all(payload, 'tm', 0, 2, tiled=True)[0]  10.7 us
    all_to_all x1, starting transfers between devices, per_device(): data = lax.all_to_all(mine, 'tm', 2, 1, tiled=True)  6.35 us
    all_gather x1, blocking collectives, per_device(): stats_full = lax.all_gather(stats_quarter, 'hyp', axis=1, tiled=True)  5.42 us
    unnamed x8, local copies, waits for them, and re-layouts  5.26 us
    ppermute x1, starting transfers between devices, with_halo(): lax.ppermute(lax.slice_in_dim(block, block.shape[dim] - width, None, axis...  3.41 us
    pallas_call x1, Pallas kernels, run_chain(): pl.pallas_call(chain_kernel, out_shape=(jax.ShapeDtypeStruct((rows, width...  2.56 us
    all_to_all x2, local copies, waits for them, and re-layouts, per_device(): data = lax.all_to_all(mine, 'tm', 2, 1, tiled=True)  1.95 us
    mul x1, other arithmetic, per_device(): 2.0 * persist * (1.0 - persist * persist) * scaled  1.47 us
  transfers between devices with their start and end apart: 3, of which 1 were waited for; matrix products, arithmetic and copies ran while one was open for 10% of the time, Pallas kernels for 0%

profile of v1, /device:TPU:0, one launch (start us, length us, event | category | flops | bytes accessed | tf_op | source)
XLA Modules:
  0.0 51.3 jit_solution(7201316284218559526)
XLA Ops:
  0.6 1.0 %fusion.2 = f32[4,16,1024]{2,1,0:T(8,128)S(1)} fusion(s32[]{:T(128)S(6)} %select_n.400, f32[1,16,4096]{2,1,0:T(8,128)} %bitcast.34, f32[1,16,4096]{2,1,0:T(8,128)} %bitcast.35, f32[1,16,4096]{2,1,0:T(8,128)} %bitcast.36, f32[1,16,4096]{2,1,0:T(8,128)} %bitcast.37), kind=kLoop, calls=%fused_computation.6 | loop fusion | flops 196608 | bytes 1310724 | tf_op jit(solution)/shard_map/stack | solution.py:131
  1.6 0.8 %copy.27 = f32[4,16,1024]{1,0,2:T(4,128)S(1)} copy(f32[4,16,1024]{2,1,0:T(8,128)S(1)} %fusion.2) | data formatting | bytes 524288
  2.5 2.3 %reshape.148 = f32[4,1,16384]{2,1,0:T(1,128)} reshape(f32[1024,4,16]{2,1,0:T(4,128)S(1)} %bitcast.29) | data formatting | bytes 524288
  4.7 6.3 %all-to-all-start = ((f32[4,1,16384]{2,1,0:T(1,128)}), f32[4,1,16384]{2,1,0:T(1,128)S(1)}, u32[]{:S(2)}, u32[]{:S(2)}) async-start(f32[4,1,16384]{2,1,0:T(1,128)} %reshape.148), calls=%async_computation | async-start | bytes 524288 | tf_op jit(solution)/shard_map/all_to_all | solution.py:133
  11.2 3.4 %collective-permute-start = (f32[64]{0:T(128)S(1)}, f32[64]{0:T(128)S(1)}, u32[]{:S(2)}, u32[]{:S(2)}) collective-permute-start(f32[64]{0:T(128)S(1)} %get-tuple-element.11), channel_id=1, source_target_pairs={{0,4},{1,5},{2,6},{3,7},{8,12},{9,13},{10,14},{11,15},{16,20},{17,... | collective-permute-start | bytes 776 | tf_op jit(solution)/shard_map/ppermute | solution.py:17
  14.6 1.3 %collective-permute-start.1 = (f32[64]{0:T(128)S(1)}, f32[64]{0:T(128)S(1)}, u32[]{:S(2)}, u32[]{:S(2)}) collective-permute-start(f32[64]{0:T(128)S(1)} %get-tuple-element.10), channel_id=1, source_target_pairs={{4,0},{5,1},{6,2},{7,3},{12,8},{13,9},{14,10},{15,11},{20,16},{21,... | collective-permute-start | bytes 776 | tf_op jit(solution)/shard_map/ppermute | solution.py:20
  15.9 0.7 %fusion.11 = (f32[1]{0:T(128)}, f32[1]{0:T(128)}, f32[1]{0:T(128)}, f32[1]{0:T(128)}) fusion(f32[4]{0:T(128)S(1)} %copy-done.1), kind=kLoop, calls=%fused_computation.153 | loop fusion | bytes 32 | tf_op jit(solution)/shard_map/slice | solution.py:153
  18.7 1.4 %collective-permute-done.1 = f32[64]{0:T(128)S(1)} collective-permute-done((f32[64]{0:T(128)S(1)}, f32[64]{0:T(128)S(1)}, u32[]{:S(2)}, u32[]{:S(2)}) %collective-permute-start.1) | collective-permute-done | bytes 288 | tf_op jit(solution)/shard_map/ppermute | solution.py:20
  20.1 0.1 concatenate.6
  20.1 0.1 dynamic_slice.20
  20.2 0.1 fusion.4
  20.3 0.1 fusion.5
  20.4 0.1 fusion.6
  20.5 0.1 fusion.7
  20.6 0.1 fusion.10
  20.7 0.1 fusion.8
  20.8 0.1 fusion.9
  20.9 1.3 %multiply_reduce_fusion = f32[256]{0:T(256)S(1)} fusion(f32[256]{0:T(256)S(1)} %get-tuple-element.16, f32[256]{0:T(256)S(1)} %get-tuple-element.17, f32[256]{0:T(256)S(1)} %get-tuple-element.18, f32[256]{0:T(256)S(1)} %get-tuple-element.19, f32[256]{0:T(256)S(1)} %get-tuple-element.20, f32[256]{0:T(256)S(1)} %get-tuple-element.21, ...), kind=kLoop, calls=%fused_computation.9 | loop fusion | flops 265984 | bytes 141316 | tf_op jit(solution)/shard_map/reduce_sum | solution.py:149
  22.2 1.5 %multiply_multiply_fusion = (f32[256]{0:T(256)S(1)}, f32[256]{0:T(256)S(1)}, f32[256]{0:T(256)S(1)}) fusion(f32[4096]{0:T(1024)} %param.12, s32[]{:T(128)S(6)} %select_n.401, f32[]{:T(128)} %bitcast.10, f32[256]{0:T(256)S(1)} %multiply_reduce_fusion, f32[384]{0:T(512)S(1)} %dynamic_slice.20, f32[4096]{0:T(1024)} %param.11, f32[]{:T(128)} %bitcast.8, f32[]{:T(128)} %bitcast.7), kind=kLoop, calls=%fused_computation.139 | loop fusion | flops 2560 | bytes 7184 | tf_op jit(solution)/shard_map/mul | solution.py:163
  23.7 0.6 %stack.51.par_ref = f32[8,256]{1,0:T(8,128)} concatenate(f32[1,256]{1,0:T(1,128)S(1)} %bitcast.44, f32[1,256]{1,0:T(1,128)S(1)} %bitcast.43, f32[1,256]{1,0:T(1,128)S(1)} %stack.46, f32[1,256]{1,0:T(1,128)S(1)} %bitcast.48, f32[1,256]{1,0:T(1,128)S(1)} %bitcast.47, f32[1,256]{1,0:T(1,128)S(1)} %bitcast.46, f32[1,256]{1,0:T(1,128)S(1)} %bitcast.45, f32[1,256]{1,0:T(1,128)S(1)} %stack_broadcast_in_dim.3), dimensions={0} | concatenate | bytes 16384 | tf_op jit(solution)/shard_map/stack | solution.py:155
  24.3 0.5 broadcast.139
  24.8 1.4 %reduce = f32[4,16384]{1,0:T(4,128)S(1)} reduce(f32[4,1,16384]{2,1,0:T(1,128)S(1)} %all-to-all-done, f32[]{:T(128)} %broadcast.139), dimensions={1}, to_apply=%all_to_all.24.reduce_sub_computation | reduce | bytes 524292 | tf_op jit(solution)/shard_map/all_to_all | solution.py:133
  26.2 1.5 %reshape.149 = f32[1024,4,16]{2,1,0:T(4,128)S(1)} reshape(f32[4,16384]{1,0:T(4,128)S(1)} %reduce) | data formatting | bytes 524288
  27.7 1.4 %copy.24 = f32[4,16,4,256]{3,1,2,0:T(8,128)} copy(f32[4,16,4,256]{1,0,3,2:T(4,128)S(1)} %bitcast.30) | data formatting | bytes 524288 | tf_op jit(solution)/shard_map/all_to_all | solution.py:133
  29.1 2.6 %shard_map.121 = (f32[64,256]{1,0:T(8,128)}, f32[8,256]{1,0:T(8,128)}) custom-call(f32[4,64,256]{2,1,0:T(8,128)} %bitcast.31, f32[8,256]{1,0:T(8,128)} %stack.51.par_ref), custom_call_target="tpu_custom_call" | custom-call | tf_op jit(solution)/shard_map/pallas_call | solution.py:97
  31.7 0.7 %broadcast_in_dim.916 = f32[4,8,256]{2,1,0:T(8,128)S(1)} broadcast(f32[8,256]{1,0:T(8,128)} %get-tuple-element.6), dimensions={1,2} | broadcast | bytes 40960 | tf_op jit(solution)/shard_map/broadcast_in_dim | solution.py:171
  32.4 0.8 %pad_maximum_fusion = f32[4,24,256]{2,1,0:T(8,128)S(1)} fusion(f32[4,8,256]{2,1,0:T(8,128)S(1)} %broadcast_in_dim.916, f32[4,16,256]{2,1,0:T(8,128)} %bitcast.40), kind=kLoop, calls=%fused_computation.7 | loop fusion | flops 24576 | bytes 196608 | tf_op jit(solution)/shard_map/concatenate | solution.py:170
  33.2 10.7 %all_to_all.33 = f32[4,24,256]{2,1,0:T(8,128)S(1)} all-to-all(f32[4,24,256]{2,1,0:T(8,128)S(1)} %pad_maximum_fusion), channel_id=1, replica_groups=mesh['tm'=4,'space'=2,'hyp'=4] {'tm'}, dimensions={0} | all-to-all | bytes 196608 | tf_op jit(solution)/shard_map/all_to_all | solution.py:173
  44.0 5.4 %all_gather.3 = f32[5,4096]{1,0:T(8,128)S(1)} all-gather(f32[5,1024]{1,0:T(8,128)S(1)} %bitcast.39), channel_id=1, replica_groups=mesh['tm'=4,'space'=2,'hyp'=4] {'hyp'}, dimensions={1}, use_global_device_ids=true | all-gather | bytes 102400 | tf_op jit(solution)/shard_map/all_gather | solution.py:176
  49.4 0.6 %slice.569 = f32[1,4096]{1,0:T(1,128)} slice(f32[5,4096]{1,0:T(8,128)S(1)} %all_gather.3), slice={[0:1], [0:4096]} | slice | bytes 32768 | tf_op jit(solution)/shard_map/slice | solution.py:177
  50.0 0.6 %slice.570 = f32[4,4096]{1,0:T(4,128)} slice(f32[5,4096]{1,0:T(8,128)S(1)} %all_gather.3), slice={[1:5], [0:4096]} | slice | bytes 131072 | tf_op jit(solution)/shard_map/slice | solution.py:177
  50.7 0.6 %copy.28 = f32[2,8,4,256]{3,1,2,0:T(8,128)} copy(f32[2,8,4,256]{3,2,1,0:T(4,128)S(1)} %bitcast.38) | data formatting | bytes 131072
  (15 shorter events, 0.2 us)
Async XLA Ops:
  1.6 9.5 %copy-start = (f32[4096]{0:T(1024)S(1)}, f32[4096]{0:T(1024)}, u32[]{:S(2)}) copy-start(f32[4096]{0:T(1024)} %param.10) | copy-start | bytes 49156
  1.6 14.3 %copy-start.1 = (f32[4]{0:T(128)S(1)}, f32[4]{0:T(128)}, u32[]{:S(2)}) copy-start(f32[4]{0:T(128)} %param.19) | copy-start | bytes 52
  4.7 19.6 %all-to-all-start = ((f32[4,1,16384]{2,1,0:T(1,128)}), f32[4,1,16384]{2,1,0:T(1,128)S(1)}, u32[]{:S(2)}, u32[]{:S(2)}) async-start(f32[4,1,16384]{2,1,0:T(1,128)} %reshape.148), calls=%async_computation | async-start | bytes 524288 | tf_op jit(solution)/shard_map/all_to_all | solution.py:133
  11.2 7.5 %collective-permute-start = (f32[64]{0:T(128)S(1)}, f32[64]{0:T(128)S(1)}, u32[]{:S(2)}, u32[]{:S(2)}) collective-permute-start(f32[64]{0:T(128)S(1)} %get-tuple-element.11), channel_id=1, source_target_pairs={{0,4},{1,5},{2,6},{3,7},{8,12},{9,13},{10,14},{11,15},{16,20},{17,... | collective-permute-start | bytes 776 | tf_op jit(solution)/shard_map/ppermute | solution.py:17
  14.6 5.5 %collective-permute-start.1 = (f32[64]{0:T(128)S(1)}, f32[64]{0:T(128)S(1)}, u32[]{:S(2)}, u32[]{:S(2)}) collective-permute-start(f32[64]{0:T(128)S(1)} %get-tuple-element.10), channel_id=1, source_target_pairs={{4,0},{5,1},{6,2},{7,3},{12,8},{13,9},{14,10},{15,11},{20,16},{21,... | collective-permute-start | bytes 776 | tf_op jit(solution)/shard_map/ppermute | solution.py:20

commit v2 on v1

v2 whole, which is shorter than its diff:
```python
import jax
import jax.numpy as jnp
from jax import lax
from jax.experimental import pallas as pl
from jax.experimental.pallas import tpu as pltpu
from jax.sharding import PartitionSpec as P

BAND = 64
INTERPRET = False


def with_halo(block, sides, width):
    for axis, dim in sides:
        count = lax.axis_size(axis)
        forward = [(i, i + 1) for i in range(count - 1)]
        backward = [(target, source) for source, target in forward]
        low = lax.ppermute(
            lax.slice_in_dim(block, block.shape[dim] - width, None, axis=dim), axis, forward
        )
        high = lax.ppermute(lax.slice_in_dim(block, 0, width, axis=dim), axis, backward)
        block = jnp.concatenate([low, block, high], axis=dim)
    return block


def chain_kernel(data_ref, par_ref, out_ref, piv_ref, slv_ref):
    blocks, _, rows, width = data_ref.shape
    ns = par_ref[2:3, :]
    ls2 = par_ref[3:4, :]
    sp = par_ref[4:5, :]
    mps = par_ref[5:6, :]
    qs = par_ref[6:7, :]
    two_ls2 = 2.0 * ls2
    zeros = jnp.zeros_like(sp)
    carry = (zeros,) * 11
    for block in range(blocks):

        def forward(t, carry):
            inv, t0, t1, t2, t3, solved, c0, c1, c2, c3, logs = carry
            rough = data_ref[block, 0, pl.ds(t, 1), :]
            coup = data_ref[block, 1, pl.ds(t, 1), :]
            weight = data_ref[block, 2, pl.ds(t, 1), :]
            obs = data_ref[block, 3, pl.ds(t, 1), :]
            prior = sp * rough
            nugget = ns * weight
            diagonal = prior + nugget
            offdiag = mps * coup
            pivots = diagonal - offdiag * offdiag * inv
            ratios = offdiag * inv
            rr = ratios * ratios
            t0 = rr * t0 + 2.0 * prior - 4.0 * offdiag * ratios
            t1 = rr * t1 + prior - 2.0 * offdiag * ratios
            t2 = rr * t2 + qs * rough - two_ls2 * offdiag * ratios
            t3 = rr * t3 + nugget
            solved = obs - ratios * solved
            c0 = c0 + 0.5 * t0 / pivots
            c1 = c1 + 0.5 * t1 / pivots
            c2 = c2 + 0.5 * t2 / pivots
            c3 = c3 + 0.5 * t3 / pivots
            logs = logs + jnp.log(pivots)
            piv_ref[block, pl.ds(t, 1), :] = pivots
            slv_ref[block, pl.ds(t, 1), :] = solved
            return (1.0 / pivots, t0, t1, t2, t3, solved, c0, c1, c2, c3, logs)

        carry = lax.fori_loop(0, rows, forward, carry, unroll=8)
    c0, c1, c2, c3, logs = carry[6:]
    closing = (zeros,) * 5
    for block in reversed(range(blocks)):

        def backward(i, carry):
            t = rows - 1 - i
            following, q0, q1, q2, q3 = carry
            rough = data_ref[block, 0, pl.ds(t, 1), :]
            coup = data_ref[block, 1, pl.ds(t, 1), :]
            weight = data_ref[block, 2, pl.ds(t, 1), :]
            prior = sp * rough
            nugget = ns * weight
            offdiag = mps * coup
            values = (slv_ref[block, pl.ds(t, 1), :] - following) / piv_ref[block, pl.ds(t, 1), :]
            q0 = q0 + 2.0 * prior * values * values + 4.0 * values * following
            q1 = q1 + prior * values * values + 2.0 * values * following
            q2 = q2 + qs * rough * values * values + two_ls2 * values * following
            q3 = q3 + nugget * values * values
            out_ref[block, pl.ds(t, 1), :] = values
            return (offdiag * values, q0, q1, q2, q3)

        closing = lax.fori_loop(0, rows, backward, closing, unroll=8)
    q0, q1, q2, q3 = closing[1:]
    scale = 1.0 / (rows * blocks)
    stats = jnp.concatenate(
        [
            logs * scale,
            (c0 - 0.5 * q0) * scale,
            (c1 - 0.5 * q1) * scale,
            (c2 - 0.5 * q2) * scale,
            (c3 - 0.5 * q3) * scale,
            jnp.zeros((3, width), jnp.float32),
        ],
        axis=0,
    )
    for block in range(blocks):
        out_ref[block, rows : rows + 8, :] = stats


def run_chain(data, params):
    blocks, _, rows, width = data.shape
    vmem = pl.BlockSpec(memory_space=pltpu.VMEM)
    return pl.pallas_call(
        chain_kernel,
        out_shape=jax.ShapeDtypeStruct((blocks, rows + 8, width), jnp.float32),
        in_specs=[vmem, vmem],
        out_specs=vmem,
        scratch_shapes=[pltpu.VMEM((blocks, rows, width), jnp.float32)] * 2,
        interpret=INTERPRET,
    )(data, params)


def per_device(
    log_kappa,
    node_mass,
    rho_base,
    edge_weight,
    offsets,
    roughness,
    coupling,
    obs_weight,
    observed,
    hyper_params,
):
    row_count, full_width = roughness.shape
    time_count = lax.axis_size("tm")
    hyp_count = lax.axis_size("hyp")
    time_place = lax.axis_index("tm")
    hyp_place = lax.axis_index("hyp")
    quarter = full_width // hyp_count
    chunk = quarter // time_count
    first = hyp_place * quarter + time_place * chunk

    stacked = jnp.stack([roughness, coupling, obs_weight, observed])
    mine = lax.dynamic_slice_in_dim(stacked, hyp_place * quarter, quarter, axis=2)
    pieces = mine.reshape(4, row_count, time_count, chunk).transpose(2, 0, 1, 3)
    data = lax.all_to_all(pieces, "tm", 0, 0, tiled=True)

    kappa_sq = jnp.exp(2.0 * log_kappa)
    padded = with_halo(kappa_sq, (("space", 0),), BAND)
    window = lax.dynamic_slice_in_dim(padded, first, chunk + 2 * BAND)
    near_off = lax.dynamic_slice_in_dim(offsets, first, chunk, axis=1)
    weights = lax.dynamic_slice_in_dim(edge_weight, first, chunk, axis=1)
    mass = lax.dynamic_slice_in_dim(node_mass, first, chunk)
    base = lax.dynamic_slice_in_dim(rho_base, first, chunk)
    own_kappa = window[BAND : BAND + chunk]
    nearby = jnp.zeros(near_off.shape, jnp.float32)
    for shift in range(-BAND, BAND + 1):
        nearby = jnp.where(
            near_off == shift, window[None, BAND + shift : BAND + shift + chunk], nearby
        )
    spatial = jnp.exp(2.0 * hyper_params[0]) * (
        mass * own_kappa + jnp.sum(weights * nearby, axis=0)
    )
    scaled = jnp.exp(hyper_params[1]) * spatial
    persist = jnp.tanh(hyper_params[2] + base)
    nugget_scale = jnp.exp(hyper_params[3]) + jnp.zeros_like(persist)
    log_slope = (1.0 - persist * persist) / persist
    params = jnp.stack(
        [
            scaled,
            persist,
            nugget_scale,
            log_slope,
            scaled * (1.0 + persist * persist),
            -persist * scaled,
            2.0 * persist * (1.0 - persist * persist) * scaled,
            jnp.zeros_like(persist),
        ]
    )
    payload = run_chain(data, params)
    received = lax.all_to_all(payload, "tm", 0, 0, tiled=True)
    solution_out = received[:, :row_count].transpose(1, 0, 2).reshape(row_count, quarter)
    stats_quarter = received[:, row_count : row_count + 5].transpose(1, 0, 2).reshape(5, quarter)
    stats_full = lax.all_gather(stats_quarter, "hyp", axis=1, tiled=True)
    return (solution_out, stats_full[0], stats_full[1:5])


def solution(mesh):
    placed = (
        P("space"),
        P("space"),
        P("space"),
        P(None, "space"),
        P(None, "space"),
        P("tm", "space"),
        P("tm", "space"),
        P("tm", "space"),
        P("tm", "space"),
        P(),
    )
    return jax.shard_map(
        per_device,
        mesh=mesh,
        in_specs=placed,
        out_specs=(P("tm", ("space", "hyp")), P("space"), P(None, "space")),
        check_vma=False,
    )
```

time: 51.9 us -> 44.9 us (0.87)
  local copies, waits for them, and re-layouts: 11.3 us -> 7.36 us
  other arithmetic: 5.98 us -> 3.17 us
  waiting for transfers between devices: 1.4 us -> 0.83 us
    unnamed x8 -> x11, local copies, waits for them, and re-layouts: 5.26 us -> 2.03 us
    all_to_all x2 -> x0, local copies, waits for them, and re-layouts: 1.95 us -> none  [per_device(): data = lax.all_to_all(mine, 'tm', 2, 1, tiled=True)]
    all_to_all x1 -> x0, other arithmetic: 1.37 us -> none  [per_device(): data = lax.all_to_all(mine, 'tm', 2, 1, tiled=True)]
    reshape x0 -> x2, local copies, waits for them, and re-layouts: none -> 1.35 us  [the longest x1 0.72 us: per_device(): pieces = mine.reshape(4, row_count, time_count, chunk).transpose(2, 0, 1, 3)]
    concatenate x1 -> x0, other arithmetic: 0.85 us -> none  [per_device(): jnp.concatenate([parts, jnp.broadcast_to(stats[None], (time_count,) + sta...]
    broadcast_in_dim x1 -> x0, local copies, waits for them, and re-layouts: 0.7 us -> none  [per_device(): jnp.broadcast_to(stats[None], (time_count,) + stats.shape)]
    slice x8 -> x9, local copies, waits for them, and re-layouts: 0.59 us -> 1.26 us  [per_device(): window[None, BAND + shift:BAND + shift + chunk]]
    ppermute x1, waiting for transfers between devices: 1.4 us -> 0.82 us  [with_halo(): lax.ppermute(lax.slice_in_dim(block, 0, width, axis=dim), axis, backward)]
where the time goes in v2:
time: 44.9 us; the launch traced here: 44.3 us
  blocking collectives  16.3 us (36%)
  starting transfers between devices  11.2 us (25%)
  local copies, waits for them, and re-layouts  7.36 us (16%)
  other arithmetic  3.17 us (7%)
  between operations  2.85 us (6%)
  Pallas kernels  2.56 us (6%)
  waiting for transfers between devices  0.83 us (2%)
    all_to_all x1, blocking collectives, per_device(): received = lax.all_to_all(payload, 'tm', 0, 0, tiled=True)  10.9 us
    all_to_all x1, starting transfers between devices, per_device(): data = lax.all_to_all(pieces, 'tm', 0, 0, tiled=True)  6.48 us
    all_gather x1, blocking collectives, per_device(): stats_full = lax.all_gather(stats_quarter, 'hyp', axis=1, tiled=True)  5.4 us
    ppermute x1, starting transfers between devices, with_halo(): lax.ppermute(lax.slice_in_dim(block, block.shape[dim] - width, None, axis...  3.41 us
    pallas_call x1, Pallas kernels, run_chain(): pl.pallas_call(chain_kernel, out_shape=jax.ShapeDtypeStruct((blocks, rows...  2.56 us
    unnamed x11, local copies, waits for them, and re-layouts  2.03 us
    mul x1, other arithmetic, per_device(): 2.0 * persist * (1.0 - persist * persist) * scaled  1.34 us
    ppermute x1, starting transfers between devices, with_halo(): lax.ppermute(lax.slice_in_dim(block, 0, width, axis=dim), axis, backward)  1.29 us
  transfers between devices with their start and end apart: 3, of which 1 were waited for; matrix products, arithmetic and copies ran while one was open for 10% of the time, Pallas kernels for 0%

profile of v2, /device:TPU:0, one launch (start us, length us, event | category | flops | bytes accessed | tf_op | source)
XLA Modules:
  0.0 44.3 jit_solution(17812290364893774955)
XLA Ops:
  0.6 1.0 %fusion.2 = f32[4,16,1024]{2,1,0:T(8,128)S(1)} fusion(s32[]{:T(128)S(6)} %select_n.400, f32[1,16,4096]{2,1,0:T(8,128)} %bitcast.30, f32[1,16,4096]{2,1,0:T(8,128)} %bitcast.31, f32[1,16,4096]{2,1,0:T(8,128)} %bitcast.32, f32[1,16,4096]{2,1,0:T(8,128)} %bitcast.33), kind=kLoop, calls=%fused_computation.6 | loop fusion | flops 196608 | bytes 1310724 | tf_op jit(solution)/shard_map/stack | solution.py:138
  1.6 0.7 %copy.18 = f32[4,2,4,8,256]{4,3,1,0,2:T(8,128)} copy(f32[4,2,4,8,256]{4,3,2,1,0:T(8,128)S(1)} %bitcast.29) | data formatting | bytes 524288 | tf_op jit(solution)/shard_map/reshape | solution.py:140
  2.3 6.5 %all-to-all-start = ((f32[4,4,16,256]{3,2,1,0:T(8,128)}), f32[4,4,16,256]{3,2,1,0:T(8,128)S(1)}, u32[]{:S(2)}, u32[]{:S(2)}) async-start(f32[4,4,16,256]{3,2,1,0:T(8,128)} %bitcast.28), calls=%async_computation | async-start | bytes 524288 | tf_op jit(solution)/shard_map/all_to_all | solution.py:141
  8.8 0.1 fusion.3
  8.9 3.4 %collective-permute-start = (f32[64]{0:T(128)S(1)}, f32[64]{0:T(128)S(1)}, u32[]{:S(2)}, u32[]{:S(2)}) collective-permute-start(f32[64]{0:T(128)S(1)} %get-tuple-element.7), channel_id=1, source_target_pairs={{0,4},{1,5},{2,6},{3,7},{8,12},{9,13},{10,14},{11,15},{16,20},{17,... | collective-permute-start | bytes 776 | tf_op jit(solution)/shard_map/ppermute | solution.py:17
  12.3 1.3 %collective-permute-start.1 = (f32[64]{0:T(128)S(1)}, f32[64]{0:T(128)S(1)}, u32[]{:S(2)}, u32[]{:S(2)}) collective-permute-start(f32[64]{0:T(128)S(1)} %get-tuple-element.6), channel_id=1, source_target_pairs={{4,0},{5,1},{6,2},{7,3},{12,8},{13,9},{14,10},{15,11},{20,16},{21,... | collective-permute-start | bytes 776 | tf_op jit(solution)/shard_map/ppermute | solution.py:20
  13.6 0.0 copy-start.4
  13.6 0.6 %copy-done.4 = f32[4]{0:T(128)S(1)} copy-done((f32[4]{0:T(128)S(1)}, f32[4]{0:T(128)}, u32[]{:S(2)}) %copy-start.4) | copy-done | bytes 40
  14.3 0.6 %fusion.11 = (f32[1]{0:T(128)}, f32[1]{0:T(128)}, f32[1]{0:T(128)}, f32[1]{0:T(128)}) fusion(f32[4]{0:T(128)S(1)} %copy-done.4), kind=kLoop, calls=%fused_computation.154 | loop fusion | bytes 32 | tf_op jit(solution)/shard_map/slice | solution.py:161
  16.9 0.8 %collective-permute-done.1 = f32[64]{0:T(128)S(1)} collective-permute-done((f32[64]{0:T(128)S(1)}, f32[64]{0:T(128)S(1)}, u32[]{:S(2)}, u32[]{:S(2)}) %collective-permute-start.1) | collective-permute-done | bytes 288 | tf_op jit(solution)/shard_map/ppermute | solution.py:20
  17.8 0.1 concatenate.3
  17.9 0.1 dynamic_slice.20
  17.9 0.1 fusion.4
  18.0 0.1 fusion.5
  18.1 0.1 fusion.6
  18.2 0.1 fusion.7
  18.3 0.1 fusion.10
  18.4 0.1 fusion.8
  18.5 0.1 fusion.9
  18.6 0.0 slice-start
  18.6 0.7 %slice-done = f32[256]{0:T(256)S(1)} async-done(((f32[384]{0:T(512)}), f32[256]{0:T(256)S(1)}, s32[]{:S(2)}) %slice-start) | async-done | bytes 1048 | tf_op jit(solution)/shard_map/slice | solution.py:154
  19.3 0.8 %multiply_reduce_fusion = f32[256]{0:T(256)S(1)} fusion(f32[256]{0:T(256)S(1)} %get-tuple-element.12, f32[256]{0:T(256)S(1)} %get-tuple-element.13, f32[256]{0:T(256)S(1)} %get-tuple-element.14, f32[256]{0:T(256)S(1)} %get-tuple-element.15, f32[256]{0:T(256)S(1)} %get-tuple-element.16, f32[256]{0:T(256)S(1)} %get-tuple-element.17, ...), kind=kLoop, calls=%fused_computation.10 | loop fusion | flops 265984 | bytes 141316 | tf_op jit(solution)/shard_map/reduce_sum | solution.py:157
  20.1 0.7 %copy-done.1 = f32[384]{0:T(512)S(1)} copy-done((f32[384]{0:T(512)S(1)}, f32[384]{0:T(512)}, u32[]{:S(2)}) %copy-start.1) | copy-done | bytes 1560
  20.8 1.3 %multiply_multiply_fusion = (f32[256]{0:T(256)S(1)}, f32[256]{0:T(256)S(1)}, f32[256]{0:T(256)S(1)}) fusion(f32[4096]{0:T(1024)} %param.12, s32[]{:T(128)S(6)} %select_n.401, f32[]{:T(128)} %bitcast.8, f32[256]{0:T(256)S(1)} %multiply_reduce_fusion, f32[384]{0:T(512)S(1)} %copy-done.1, f32[4096]{0:T(1024)} %param.11, f32[]{:T(128)} %bitcast.6, f32[]{:T(128)} %bitcast.5), kind=kLoop, calls=%fused_computation.140 | loop fusion | flops 2560 | bytes 7184 | tf_op jit(solution)/shard_map/mul | solution.py:171
  22.2 0.6 %stack.51.par_ref = f32[8,256]{1,0:T(8,128)} concatenate(f32[1,256]{1,0:T(1,128)S(1)} %bitcast.38, f32[1,256]{1,0:T(1,128)S(1)} %bitcast.37, f32[1,256]{1,0:T(1,128)S(1)} %stack.46, f32[1,256]{1,0:T(1,128)S(1)} %bitcast.42, f32[1,256]{1,0:T(1,128)S(1)} %bitcast.41, f32[1,256]{1,0:T(1,128)S(1)} %bitcast.40, f32[1,256]{1,0:T(1,128)S(1)} %bitcast.39, f32[1,256]{1,0:T(1,128)S(1)} %stack_broadcast_in_dim.3), dimensions={0} | concatenate | bytes 16384 | tf_op jit(solution)/shard_map/stack | solution.py:163
  22.8 0.7 %copy-done.2 = f32[4,4,16,256]{3,2,1,0:T(8,128)} copy-done((f32[4,4,16,256]{3,2,1,0:T(8,128)}, f32[4,4,16,256]{3,2,1,0:T(8,128)S(1)}, u32[]{:S(2)}) %copy-start.2) | copy-done | bytes 262168
  23.5 2.6 %shard_map.121 = f32[4,24,256]{2,1,0:T(8,128)} custom-call(f32[4,4,16,256]{3,2,1,0:T(8,128)} %copy-done.2, f32[8,256]{1,0:T(8,128)} %stack.51.par_ref), custom_call_target="tpu_custom_call" | custom-call | tf_op jit(solution)/shard_map/pallas_call | solution.py:107
  26.0 10.9 %all_to_all.10 = f32[4,24,256]{2,1,0:T(8,128)S(1)} all-to-all(f32[4,24,256]{2,1,0:T(8,128)} %shard_map.121), channel_id=1, replica_groups=mesh['tm'=4,'space'=2,'hyp'=4] {'tm'}, dimensions={0} | all-to-all | bytes 196608 | tf_op jit(solution)/shard_map/all_to_all | solution.py:176
  37.0 5.4 %all_gather.3 = f32[5,4096]{1,0:T(8,128)S(1)} all-gather(f32[5,1024]{1,0:T(8,128)S(1)} %bitcast.34), channel_id=1, replica_groups=mesh['tm'=4,'space'=2,'hyp'=4] {'hyp'}, dimensions={1}, use_global_device_ids=true | all-gather | bytes 102400 | tf_op jit(solution)/shard_map/all_gather | solution.py:179
  42.4 0.6 %slice.561 = f32[1,4096]{1,0:T(1,128)} slice(f32[5,4096]{1,0:T(8,128)S(1)} %all_gather.3), slice={[0:1], [0:4096]} | slice | bytes 32768 | tf_op jit(solution)/shard_map/slice | solution.py:180
  43.0 0.6 %slice.562 = f32[4,4096]{1,0:T(4,128)} slice(f32[5,4096]{1,0:T(8,128)S(1)} %all_gather.3), slice={[1:5], [0:4096]} | slice | bytes 131072 | tf_op jit(solution)/shard_map/slice | solution.py:180
  43.6 0.6 %copy.16 = f32[4,2,8,256]{3,2,0,1:T(8,128)} copy(f32[4,2,8,256]{3,2,1,0:T(8,128)S(1)} %slice_bitcast_fusion) | data formatting | bytes 131072 | tf_op jit(solution)/shard_map/reshape | solution.py:177
  (14 shorter events, 0.0 us)
Async XLA Ops:
  2.3 6.5 %copy-start.3 = (f32[4096]{0:T(1024)S(1)}, f32[4096]{0:T(1024)}, u32[]{:S(2)}) copy-start(f32[4096]{0:T(1024)} %param.10) | copy-start | bytes 49156
  2.3 20.5 %all-to-all-start = ((f32[4,4,16,256]{3,2,1,0:T(8,128)}), f32[4,4,16,256]{3,2,1,0:T(8,128)S(1)}, u32[]{:S(2)}, u32[]{:S(2)}) async-start(f32[4,4,16,256]{3,2,1,0:T(8,128)} %bitcast.28), calls=%async_computation | async-start | bytes 524288 | tf_op jit(solution)/shard_map/all_to_all | solution.py:141
  8.9 8.1 %collective-permute-start = (f32[64]{0:T(128)S(1)}, f32[64]{0:T(128)S(1)}, u32[]{:S(2)}, u32[]{:S(2)}) collective-permute-start(f32[64]{0:T(128)S(1)} %get-tuple-element.7), channel_id=1, source_target_pairs={{0,4},{1,5},{2,6},{3,7},{8,12},{9,13},{10,14},{11,15},{16,20},{17,... | collective-permute-start | bytes 776 | tf_op jit(solution)/shard_map/ppermute | solution.py:17
  12.3 5.5 %collective-permute-start.1 = (f32[64]{0:T(128)S(1)}, f32[64]{0:T(128)S(1)}, u32[]{:S(2)}, u32[]{:S(2)}) collective-permute-start(f32[64]{0:T(128)S(1)} %get-tuple-element.6), channel_id=1, source_target_pairs={{4,0},{5,1},{6,2},{7,3},{12,8},{13,9},{14,10},{15,11},{20,16},{21,... | collective-permute-start | bytes 776 | tf_op jit(solution)/shard_map/ppermute | solution.py:20
  13.6 0.7 %copy-start.4 = (f32[4]{0:T(128)S(1)}, f32[4]{0:T(128)}, u32[]{:S(2)}) copy-start(f32[4]{0:T(128)} %param.19) | copy-start | bytes 52
  17.9 0.6 %copy-start = (f32[384]{0:T(512)}, f32[384]{0:T(512)S(1)}, u32[]{:S(2)}) copy-start(f32[384]{0:T(512)S(1)} %dynamic_slice.20) | copy-start | bytes 4612
  18.6 0.7 %slice-start = ((f32[384]{0:T(512)}), f32[256]{0:T(256)S(1)}, s32[]{:S(2)}) async-start(f32[384]{0:T(512)} %copy-done), calls=%async_computation.2 | async-start | bytes 2048 | tf_op jit(solution)/shard_map/slice | solution.py:154
  20.1 0.7 %copy-start.1 = (f32[384]{0:T(512)S(1)}, f32[384]{0:T(512)}, u32[]{:S(2)}) copy-start(f32[384]{0:T(512)} %copy-done) | copy-start | bytes 4612
  22.8 0.7 %copy-start.2 = (f32[4,4,16,256]{3,2,1,0:T(8,128)}, f32[4,4,16,256]{3,2,1,0:T(8,128)S(1)}, u32[]{:S(2)}) copy-start(f32[4,4,16,256]{3,2,1,0:T(8,128)S(1)} %all-to-all-done.data_ref) | copy-start | bytes 786436

commit v3 on v2

--- a/solution.py
+++ b/solution.py
@@ -22,8 +22,9 @@
     return block
 
 
-def chain_kernel(data_ref, par_ref, out_ref, piv_ref, slv_ref):
+def chain_kernel(place_ref, data_ref, par_ref, out_ref, piv_ref, slv_ref):
     blocks, _, rows, width = data_ref.shape
+    place = place_ref[0]
     ns = par_ref[2:3, :]
     ls2 = par_ref[3:4, :]
     sp = par_ref[4:5, :]
@@ -33,13 +34,14 @@
     zeros = jnp.zeros_like(sp)
     carry = (zeros,) * 11
     for block in range(blocks):
+        slot = lax.rem(place - block + blocks, blocks)
 
         def forward(t, carry):
             inv, t0, t1, t2, t3, solved, c0, c1, c2, c3, logs = carry
-            rough = data_ref[block, 0, pl.ds(t, 1), :]
-            coup = data_ref[block, 1, pl.ds(t, 1), :]
-            weight = data_ref[block, 2, pl.ds(t, 1), :]
-            obs = data_ref[block, 3, pl.ds(t, 1), :]
+            rough = data_ref[slot, 0, pl.ds(t, 1), :]
+            coup = data_ref[slot, 1, pl.ds(t, 1), :]
+            weight = data_ref[slot, 2, pl.ds(t, 1), :]
+            obs = data_ref[slot, 3, pl.ds(t, 1), :]
             prior = sp * rough
             nugget = ns * weight
             diagonal = prior + nugget
@@ -65,13 +67,14 @@
     c0, c1, c2, c3, logs = carry[6:]
     closing = (zeros,) * 5
     for block in reversed(range(blocks)):
+        slot = lax.rem(place - block + blocks, blocks)
 
         def backward(i, carry):
             t = rows - 1 - i
             following, q0, q1, q2, q3 = carry
-            rough = data_ref[block, 0, pl.ds(t, 1), :]
-            coup = data_ref[block, 1, pl.ds(t, 1), :]
-            weight = data_ref[block, 2, pl.ds(t, 1), :]
+            rough = data_ref[slot, 0, pl.ds(t, 1), :]
+            coup = data_ref[slot, 1, pl.ds(t, 1), :]
+            weight = data_ref[slot, 2, pl.ds(t, 1), :]
             prior = sp * rough
             nugget = ns * weight
             offdiag = mps * coup
@@ -101,17 +104,18 @@
         out_ref[block, rows : rows + 8, :] = stats
 
 
-def run_chain(data, params):
+def run_chain(place, data, params):
     blocks, _, rows, width = data.shape
     vmem = pl.BlockSpec(memory_space=pltpu.VMEM)
+    smem = pl.BlockSpec(memory_space=pltpu.SMEM)
     return pl.pallas_call(
         chain_kernel,
         out_shape=jax.ShapeDtypeStruct((blocks, rows + 8, width), jnp.float32),
-        in_specs=[vmem, vmem],
+        in_specs=[smem, vmem, vmem],
         out_specs=vmem,
         scratch_shapes=[pltpu.VMEM((blocks, rows, width), jnp.float32)] * 2,
         interpret=INTERPRET,
-    )(data, params)
+    )(place, data, params)
 
 
 def per_device(
@@ -136,9 +140,25 @@
     first = hyp_place * quarter + time_place * chunk
 
     stacked = jnp.stack([roughness, coupling, obs_weight, observed])
-    mine = lax.dynamic_slice_in_dim(stacked, hyp_place * quarter, quarter, axis=2)
-    pieces = mine.reshape(4, row_count, time_count, chunk).transpose(2, 0, 1, 3)
-    data = lax.all_to_all(pieces, "tm", 0, 0, tiled=True)
+    pieces = [
+        lax.dynamic_slice_in_dim(
+            stacked,
+            hyp_place * quarter + lax.rem(time_place + shift, time_count) * chunk,
+            chunk,
+            axis=2,
+        )
+        for shift in range(time_count)
+    ]
+    arrived = [pieces[0]] + [
+        lax.ppermute(
+            pieces[shift],
+            "tm",
+            [(i, (i + shift) % time_count) for i in range(time_count)],
+        )
+        for shift in range(1, time_count)
+    ]
+    data = jnp.stack(arrived)
+    place = time_place.astype(jnp.int32).reshape(1)
 
     kappa_sq = jnp.exp(2.0 * log_kappa)
     padded = with_halo(kappa_sq, (("space", 0),), BAND)
@@ -172,7 +192,7 @@
             jnp.zeros_like(persist),
         ]
     )
-    payload = run_chain(data, params)
+    payload = run_chain(place, data, params)
     received = lax.all_to_all(payload, "tm", 0, 0, tiled=True)
     solution_out = received[:, :row_count].transpose(1, 0, 2).reshape(row_count, quarter)
     stats_quarter = received[:, row_count : row_count + 5].transpose(1, 0, 2).reshape(5, quarter)

time: 44.9 us -> 43.1 us (0.960)
  local copies, waits for them, and re-layouts: 7.36 us -> 6.02 us
  other arithmetic: 3.17 us -> 4.19 us
  blocking collectives: 16.3 us -> 15.3 us
    all_to_all x1 -> x0, starting transfers between devices: 6.48 us -> none  [per_device(): data = lax.all_to_all(pieces, 'tm', 0, 0, tiled=True)]
    ppermute x0 -> x3, starting transfers between devices: none -> 6.14 us  [per_device(): lax.ppermute(pieces[shift], 'tm', [(i, (i + shift) % time_count) for i in...]
    all_to_all x1, blocking collectives: 10.9 us -> 9.91 us  [per_device(): received = lax.all_to_all(payload, 'tm', 0, 0, tiled=True)]
    another operation x0 -> x1, other arithmetic: none -> 0.72 us  [per_device(): data = jnp.stack(arrived)]
    reshape x1 -> x0, local copies, waits for them, and re-layouts: 0.72 us -> none  [per_device(): pieces = mine.reshape(4, row_count, time_count, chunk).transpose(2, 0, 1, 3)]
    unnamed x11 -> x9, local copies, waits for them, and re-layouts: 2.03 us -> 1.34 us
  transfers between devices with their start and end apart: 3 -> 5, of which waited for: 1 -> 1; matrix products, arithmetic and copies ran while one was open for 10% -> 10% of each run, Pallas kernels for 0% -> 0%
where the time goes in v3:
time: 43.1 us; the launch traced here: 42.6 us
  blocking collectives  15.3 us (35%)
  starting transfers between devices  10.8 us (25%)
  local copies, waits for them, and re-layouts  6.02 us (14%)
  other arithmetic  4.19 us (10%)
  between operations  2.88 us (7%)
  Pallas kernels  2.56 us (6%)
  waiting for transfers between devices  0.82 us (2%)
    all_to_all x1, blocking collectives, per_device(): received = lax.all_to_all(payload, 'tm', 0, 0, tiled=True)  9.91 us
    ppermute x3, starting transfers between devices, per_device(): lax.ppermute(pieces[shift], 'tm', [(i, (i + shift) % time_count) for i in...  6.14 us
    all_gather x1, blocking collectives, per_device(): stats_full = lax.all_gather(stats_quarter, 'hyp', axis=1, tiled=True)  5.4 us
    ppermute x1, starting transfers between devices, with_halo(): lax.ppermute(lax.slice_in_dim(block, block.shape[dim] - width, None, axis...  3.41 us
    pallas_call x1, Pallas kernels, run_chain(): pl.pallas_call(chain_kernel, out_shape=jax.ShapeDtypeStruct((blocks, rows...  2.56 us
    mul x1, other arithmetic, per_device(): 2.0 * persist * (1.0 - persist * persist) * scaled  1.34 us
    unnamed x9, local copies, waits for them, and re-layouts  1.34 us
    ppermute x1, starting transfers between devices, with_halo(): lax.ppermute(lax.slice_in_dim(block, 0, width, axis=dim), axis, backward)  1.29 us
  transfers between devices with their start and end apart: 5, of which 1 were waited for; matrix products, arithmetic and copies ran while one was open for 10% of the time, Pallas kernels for 0%

profile of v3, /device:TPU:0, one launch (start us, length us, event | category | flops | bytes accessed | tf_op | source)
XLA Modules:
  0.0 42.6 jit_solution(750677099272885344)
XLA Ops:
  0.7 1.3 %pad_maximum_fusion = f32[4,16,4096]{2,1,0:T(8,128)S(1)} fusion(f32[1,16,4096]{2,1,0:T(8,128)} %bitcast.28, f32[1,16,4096]{2,1,0:T(8,128)} %bitcast.29, f32[1,16,4096]{2,1,0:T(8,128)} %bitcast.30, f32[1,16,4096]{2,1,0:T(8,128)} %bitcast.31), kind=kLoop, calls=%fused_computation | loop fusion | flops 786432 | bytes 2097152 | tf_op jit(solution)/shard_map/stack | solution.py:142
  2.0 5.1 %collective-permute-start.2 = (f32[4,16,256]{2,1,0:T(8,128)S(1)}, f32[4,16,256]{2,1,0:T(8,128)S(1)}, u32[]{:S(2)}, u32[]{:S(2)}) collective-permute-start(f32[4,16,256]{2,1,0:T(8,128)S(1)} %get-tuple-element.7), channel_id=1, source_target_pairs={{0,24},{8,0},{16,8},{24,16},{1,25},{9,1},{17,9},{25,17},{2,26},{10... | collective-permute-start | bytes 196616 | tf_op jit(solution)/shard_map/ppermute | solution.py:153
  7.1 1.0 %collective-permute-start = (f32[4,16,256]{2,1,0:T(8,128)S(1)}, f32[4,16,256]{2,1,0:T(8,128)S(1)}, u32[]{:S(2)}, u32[]{:S(2)}) collective-permute-start(f32[4,16,256]{2,1,0:T(8,128)S(1)} %get-tuple-element.9), channel_id=1, source_target_pairs={{0,8},{8,16},{16,24},{24,0},{1,9},{9,17},{17,25},{25,1},{2,10},{10... | collective-permute-start | bytes 196616 | tf_op jit(solution)/shard_map/ppermute | solution.py:153
  8.1 0.1 fusion
  8.2 3.4 %collective-permute-start.3 = (f32[64]{0:T(128)S(1)}, f32[64]{0:T(128)S(1)}, u32[]{:S(2)}, u32[]{:S(2)}) collective-permute-start(f32[64]{0:T(128)S(1)} %get-tuple-element.11), channel_id=1, source_target_pairs={{0,4},{1,5},{2,6},{3,7},{8,12},{9,13},{10,14},{11,15},{16,20},{17,... | collective-permute-start | bytes 776 | tf_op jit(solution)/shard_map/ppermute | solution.py:17
  11.6 1.3 %collective-permute-start.4 = (f32[64]{0:T(128)S(1)}, f32[64]{0:T(128)S(1)}, u32[]{:S(2)}, u32[]{:S(2)}) collective-permute-start(f32[64]{0:T(128)S(1)} %get-tuple-element.10), channel_id=1, source_target_pairs={{4,0},{5,1},{6,2},{7,3},{12,8},{13,9},{14,10},{15,11},{20,16},{21,... | collective-permute-start | bytes 776 | tf_op jit(solution)/shard_map/ppermute | solution.py:20
  12.9 0.0 copy-start.3
  13.0 0.6 %copy-done.3 = f32[4]{0:T(128)S(1)} copy-done((f32[4]{0:T(128)S(1)}, f32[4]{0:T(128)}, u32[]{:S(2)}) %copy-start.3) | copy-done | bytes 40
  13.6 0.6 %fusion.8 = (f32[1]{0:T(128)}, f32[1]{0:T(128)}, f32[1]{0:T(128)}, f32[1]{0:T(128)}) fusion(f32[4]{0:T(128)S(1)} %copy-done.3), kind=kLoop, calls=%fused_computation.152 | loop fusion | bytes 32 | tf_op jit(solution)/shard_map/slice | solution.py:181
  16.3 0.8 %collective-permute-done.4 = f32[64]{0:T(128)S(1)} collective-permute-done((f32[64]{0:T(128)S(1)}, f32[64]{0:T(128)S(1)}, u32[]{:S(2)}, u32[]{:S(2)}) %collective-permute-start.4) | collective-permute-done | bytes 288 | tf_op jit(solution)/shard_map/ppermute | solution.py:20
  17.1 0.1 concatenate.3
  17.2 0.1 dynamic_slice.32
  17.3 0.1 fusion.1
  17.3 0.1 fusion.2
  17.4 0.1 fusion.3
  17.5 0.1 fusion.4
  17.6 0.1 fusion.7
  17.7 0.1 fusion.5
  17.8 0.1 fusion.6
  17.9 0.0 slice-start
  17.9 0.7 %slice-done = f32[256]{0:T(256)S(1)} async-done(((f32[384]{0:T(512)}), f32[256]{0:T(256)S(1)}, s32[]{:S(2)}) %slice-start) | async-done | bytes 1048 | tf_op jit(solution)/shard_map/slice | solution.py:174
  18.6 0.8 %multiply_reduce_fusion = f32[256]{0:T(256)S(1)} fusion(f32[256]{0:T(256)S(1)} %get-tuple-element.16, f32[256]{0:T(256)S(1)} %get-tuple-element.17, f32[256]{0:T(256)S(1)} %get-tuple-element.18, f32[256]{0:T(256)S(1)} %get-tuple-element.19, f32[256]{0:T(256)S(1)} %get-tuple-element.20, f32[256]{0:T(256)S(1)} %get-tuple-element.21, ...), kind=kLoop, calls=%fused_computation.5 | loop fusion | flops 265984 | bytes 141316 | tf_op jit(solution)/shard_map/reduce_sum | solution.py:177
  19.4 0.7 %copy-done.1 = f32[384]{0:T(512)S(1)} copy-done((f32[384]{0:T(512)S(1)}, f32[384]{0:T(512)}, u32[]{:S(2)}) %copy-start.1) | copy-done | bytes 1560
  20.1 1.3 %multiply_multiply_fusion = (f32[256]{0:T(256)S(1)}, f32[256]{0:T(256)S(1)}, f32[256]{0:T(256)S(1)}) fusion(f32[4096]{0:T(1024)} %param.12, s32[]{:T(128)S(6)} %select_n.413, f32[]{:T(128)} %bitcast.12, f32[256]{0:T(256)S(1)} %multiply_reduce_fusion, f32[384]{0:T(512)S(1)} %copy-done.1, f32[4096]{0:T(1024)} %param.11, f32[]{:T(128)} %bitcast.10, f32[]{:T(128)} %bitcast.9), kind=kLoop, calls=%fused_computation.138 | loop fusion | flops 2560 | bytes 7184 | tf_op jit(solution)/shard_map/mul | solution.py:191
  21.5 0.6 %stack.71.par_ref = f32[8,256]{1,0:T(8,128)} concatenate(f32[1,256]{1,0:T(1,128)S(1)} %bitcast.39, f32[1,256]{1,0:T(1,128)S(1)} %bitcast.38, f32[1,256]{1,0:T(1,128)S(1)} %stack.66, f32[1,256]{1,0:T(1,128)S(1)} %bitcast.43, f32[1,256]{1,0:T(1,128)S(1)} %bitcast.42, f32[1,256]{1,0:T(1,128)S(1)} %bitcast.41, f32[1,256]{1,0:T(1,128)S(1)} %bitcast.40, f32[1,256]{1,0:T(1,128)S(1)} %stack_broadcast_in_dim.3), dimensions={0} | concatenate | bytes 16384 | tf_op jit(solution)/shard_map/stack | solution.py:183
  22.1 0.7 %pad_maximum_fusion.1.data_ref = f32[4,4,16,256]{3,2,1,0:T(8,128)} fusion(f32[1,4,16,256]{3,2,1,0:T(8,128)S(1)} %bitcast.34, f32[1,4,16,256]{3,2,1,0:T(8,128)S(1)} %bitcast.35, f32[1,4,16,256]{3,2,1,0:T(8,128)S(1)} %bitcast.36, f32[1,4,16,256]{3,2,1,0:T(8,128)S(1)} %get-tuple-element.6), kind=kLoop, calls=%fused_computation.1 | loop fusion | flops 196608 | bytes 524288 | tf_op jit(solution)/shard_map/stack | solution.py:160
  22.8 2.6 %shard_map.121 = f32[4,24,256]{2,1,0:T(8,128)} custom-call(s32[1]{0:T(128)} %bitcast.place_ref, f32[4,4,16,256]{3,2,1,0:T(8,128)} %pad_maximum_fusion.1.data_ref, f32[8,256]{1,0:T(8,128)} %stack.71.par_ref), custom_call_target="tpu_custom_call" | custom-call | tf_op jit(solution)/shard_map/pallas_call | solution.py:111
  25.4 9.9 %all_to_all.5 = f32[4,24,256]{2,1,0:T(8,128)S(1)} all-to-all(f32[4,24,256]{2,1,0:T(8,128)} %shard_map.121), channel_id=1, replica_groups=mesh['tm'=4,'space'=2,'hyp'=4] {'tm'}, dimensions={0} | all-to-all | bytes 196608 | tf_op jit(solution)/shard_map/all_to_all | solution.py:196
  35.3 5.4 %all_gather.3 = f32[5,4096]{1,0:T(8,128)S(1)} all-gather(f32[5,1024]{1,0:T(8,128)S(1)} %bitcast.32), channel_id=1, replica_groups=mesh['tm'=4,'space'=2,'hyp'=4] {'hyp'}, dimensions={1}, use_global_device_ids=true | all-gather | bytes 102400 | tf_op jit(solution)/shard_map/all_gather | solution.py:199
  40.7 0.6 %slice.561 = f32[1,4096]{1,0:T(1,128)} slice(f32[5,4096]{1,0:T(8,128)S(1)} %all_gather.3), slice={[0:1], [0:4096]} | slice | bytes 32768 | tf_op jit(solution)/shard_map/slice | solution.py:200
  41.3 0.6 %slice.562 = f32[4,4096]{1,0:T(4,128)} slice(f32[5,4096]{1,0:T(8,128)S(1)} %all_gather.3), slice={[1:5], [0:4096]} | slice | bytes 131072 | tf_op jit(solution)/shard_map/slice | solution.py:200
  42.0 0.6 %copy.14 = f32[4,2,8,256]{3,2,0,1:T(8,128)} copy(f32[4,2,8,256]{3,2,1,0:T(8,128)S(1)} %slice_bitcast_fusion) | data formatting | bytes 131072 | tf_op jit(solution)/shard_map/reshape | solution.py:197
  (17 shorter events, 0.1 us)
Async XLA Ops:
  1.9 6.2 %copy-start.2 = (f32[4096]{0:T(1024)S(1)}, f32[4096]{0:T(1024)}, u32[]{:S(2)}) copy-start(f32[4096]{0:T(1024)} %param.10) | copy-start | bytes 49156
  2.0 20.1 %collective-permute-start.2 = (f32[4,16,256]{2,1,0:T(8,128)S(1)}, f32[4,16,256]{2,1,0:T(8,128)S(1)}, u32[]{:S(2)}, u32[]{:S(2)}) collective-permute-start(f32[4,16,256]{2,1,0:T(8,128)S(1)} %get-tuple-element.7), channel_id=1, source_target_pairs={{0,24},{8,0},{16,8},{24,16},{1,25},{9,1},{17,9},{25,17},{2,26},{10... | collective-permute-start | bytes 196616 | tf_op jit(solution)/shard_map/ppermute | solution.py:153
  7.1 15.0 %collective-permute-start.1 = (f32[4,16,256]{2,1,0:T(8,128)S(1)}, f32[4,16,256]{2,1,0:T(8,128)S(1)}, u32[]{:S(2)}, u32[]{:S(2)}) collective-permute-start(f32[4,16,256]{2,1,0:T(8,128)S(1)} %get-tuple-element.8), channel_id=1, source_target_pairs={{0,16},{8,24},{16,0},{24,8},{1,17},{9,25},{17,1},{25,9},{2,18},{10... | collective-permute-start | bytes 196616 | tf_op jit(solution)/shard_map/ppermute | solution.py:153
  7.1 15.0 %collective-permute-start = (f32[4,16,256]{2,1,0:T(8,128)S(1)}, f32[4,16,256]{2,1,0:T(8,128)S(1)}, u32[]{:S(2)}, u32[]{:S(2)}) collective-permute-start(f32[4,16,256]{2,1,0:T(8,128)S(1)} %get-tuple-element.9), channel_id=1, source_target_pairs={{0,8},{8,16},{16,24},{24,0},{1,9},{9,17},{17,25},{25,1},{2,10},{10... | collective-permute-start | bytes 196616 | tf_op jit(solution)/shard_map/ppermute | solution.py:153
  8.2 8.1 %collective-permute-start.3 = (f32[64]{0:T(128)S(1)}, f32[64]{0:T(128)S(1)}, u32[]{:S(2)}, u32[]{:S(2)}) collective-permute-start(f32[64]{0:T(128)S(1)} %get-tuple-element.11), channel_id=1, source_target_pairs={{0,4},{1,5},{2,6},{3,7},{8,12},{9,13},{10,14},{11,15},{16,20},{17,... | collective-permute-start | bytes 776 | tf_op jit(solution)/shard_map/ppermute | solution.py:17
  11.6 5.5 %collective-permute-start.4 = (f32[64]{0:T(128)S(1)}, f32[64]{0:T(128)S(1)}, u32[]{:S(2)}, u32[]{:S(2)}) collective-permute-start(f32[64]{0:T(128)S(1)} %get-tuple-element.10), channel_id=1, source_target_pairs={{4,0},{5,1},{6,2},{7,3},{12,8},{13,9},{14,10},{15,11},{20,16},{21,... | collective-permute-start | bytes 776 | tf_op jit(solution)/shard_map/ppermute | solution.py:20
  12.9 0.7 %copy-start.3 = (f32[4]{0:T(128)S(1)}, f32[4]{0:T(128)}, u32[]{:S(2)}) copy-start(f32[4]{0:T(128)} %param.19) | copy-start | bytes 52
  17.3 0.6 %copy-start = (f32[384]{0:T(512)}, f32[384]{0:T(512)S(1)}, u32[]{:S(2)}) copy-start(f32[384]{0:T(512)S(1)} %dynamic_slice.32) | copy-start | bytes 4612
  17.9 0.7 %slice-start = ((f32[384]{0:T(512)}), f32[256]{0:T(256)S(1)}, s32[]{:S(2)}) async-start(f32[384]{0:T(512)} %copy-done), calls=%async_computation.1 | async-start | bytes 2048 | tf_op jit(solution)/shard_map/slice | solution.py:174
  19.4 0.7 %copy-start.1 = (f32[384]{0:T(512)S(1)}, f32[384]{0:T(512)}, u32[]{:S(2)}) copy-start(f32[384]{0:T(512)} %copy-done) | copy-start | bytes 4612

commit v4 on v3

--- a/solution.py
+++ b/solution.py
@@ -9,17 +9,20 @@
 INTERPRET = False
 
 
-def with_halo(block, sides, width):
-    for axis, dim in sides:
-        count = lax.axis_size(axis)
+def with_halo(block, axis, width):
+    count = lax.axis_size(axis)
+    if count == 2:
+        place = lax.axis_index(axis)
+        send = jnp.where(place == 0, block[-width:], block[:width])
+        got = lax.ppermute(send, axis, [(0, 1), (1, 0)])
+        low = jnp.where(place == 1, got, jnp.zeros_like(got))
+        high = jnp.where(place == 0, got, jnp.zeros_like(got))
+    else:
         forward = [(i, i + 1) for i in range(count - 1)]
         backward = [(target, source) for source, target in forward]
-        low = lax.ppermute(
-            lax.slice_in_dim(block, block.shape[dim] - width, None, axis=dim), axis, forward
-        )
-        high = lax.ppermute(lax.slice_in_dim(block, 0, width, axis=dim), axis, backward)
-        block = jnp.concatenate([low, block, high], axis=dim)
-    return block
+        low = lax.ppermute(block[-width:], axis, forward)
+        high = lax.ppermute(block[:width], axis, backward)
+    return jnp.concatenate([low, block, high])
 
 
 def chain_kernel(place_ref, data_ref, par_ref, out_ref, piv_ref, slv_ref):
@@ -118,7 +121,7 @@
     )(place, data, params)
 
 
-def per_device(
+def per_device_body(
     log_kappa,
     node_mass,
     rho_base,
@@ -138,6 +141,9 @@
     quarter = full_width // hyp_count
     chunk = quarter // time_count
     first = hyp_place * quarter + time_place * chunk
+
+    kappa_sq = jnp.exp(2.0 * log_kappa)
+    padded = with_halo(kappa_sq, "space", BAND)
 
     stacked = jnp.stack([roughness, coupling, obs_weight, observed])
     pieces = [
@@ -160,8 +166,6 @@
     data = jnp.stack(arrived)
     place = time_place.astype(jnp.int32).reshape(1)
 
-    kappa_sq = jnp.exp(2.0 * log_kappa)
-    padded = with_halo(kappa_sq, (("space", 0),), BAND)
     window = lax.dynamic_slice_in_dim(padded, first, chunk + 2 * BAND)
     near_off = lax.dynamic_slice_in_dim(offsets, first, chunk, axis=1)
     weights = lax.dynamic_slice_in_dim(edge_weight, first, chunk, axis=1)
@@ -214,7 +218,7 @@
         P(),
     )
     return jax.shard_map(
-        per_device,
+        per_device_body,
         mesh=mesh,
         in_specs=placed,
         out_specs=(P("tm", ("space", "hyp")), P("space"), P(None, "space")),

time: 43.1 us -> 39.2 us (0.910)
  starting transfers between devices: 10.8 us -> 7.67 us
  waiting for transfers between devices: 0.82 us -> 0.01 us
    ppermute x5 -> x4, starting transfers between devices: 10.8 us -> 7.67 us  [the longest x3 6.14 us: per_device_body(): lax.ppermute(pieces[shift], 'tm', [(i, (i + shift) % time_count) for i in...]
    ppermute x5 -> x4, waiting for transfers between devices: 0.82 us -> 0.01 us  [the longest x3 0.01 us: per_device_body(): lax.ppermute(pieces[shift], 'tm', [(i, (i + shift) % time_count) for i in...]
    slice x14 -> x13, local copies, waits for them, and re-layouts: 3.23 us -> 3.19 us  [the longest x2 1.26 us: per_device_body(): return (solution_out, stats_full[0], stats_full[1:5])]
  transfers between devices with their start and end apart: 5 -> 4, of which waited for: 1 -> 0; matrix products, arithmetic and copies ran while one was open for 10% -> 11% of each run, Pallas kernels for 0% -> 0%
where the time goes in v4:
time: 39.2 us; the launch traced here: 38.8 us
  blocking collectives  15.3 us (39%)
  starting transfers between devices  7.67 us (20%)
  local copies, waits for them, and re-layouts  5.99 us (15%)
  other arithmetic  4.39 us (11%)
  between operations  2.85 us (7%)
  Pallas kernels  2.56 us (7%)
    all_to_all x1, blocking collectives, per_device_body(): received = lax.all_to_all(payload, 'tm', 0, 0, tiled=True)  9.91 us
    ppermute x3, starting transfers between devices, per_device_body(): lax.ppermute(pieces[shift], 'tm', [(i, (i + shift) % time_count) for i in...  6.14 us
    all_gather x1, blocking collectives, per_device_body(): stats_full = lax.all_gather(stats_quarter, 'hyp', axis=1, tiled=True)  5.4 us
    pallas_call x1, Pallas kernels, run_chain(): pl.pallas_call(chain_kernel, out_shape=jax.ShapeDtypeStruct((blocks, rows...  2.56 us
    ppermute x1, starting transfers between devices, with_halo(): got = lax.ppermute(send, axis, [(0, 1), (1, 0)])  1.53 us
    mul x1, other arithmetic, per_device_body(): 2.0 * persist * (1.0 - persist * persist) * scaled  1.48 us
    unnamed x9, local copies, waits for them, and re-layouts  1.35 us
    slice x2, local copies, waits for them, and re-layouts, per_device_body(): return (solution_out, stats_full[0], stats_full[1:5])  1.26 us
  transfers between devices with their start and end apart: 4, of which 0 were waited for; matrix products, arithmetic and copies ran while one was open for 11% of the time, Pallas kernels for 0%

profile of v4, /device:TPU:0, one launch (start us, length us, event | category | flops | bytes accessed | tf_op | source)
XLA Modules:
  0.0 38.8 jit_solution(3105578873558068890)
XLA Ops:
  0.7 1.3 %pad_maximum_fusion = f32[4,16,4096]{2,1,0:T(8,128)S(1)} fusion(f32[1,16,4096]{2,1,0:T(8,128)} %bitcast.28, f32[1,16,4096]{2,1,0:T(8,128)} %bitcast.29, f32[1,16,4096]{2,1,0:T(8,128)} %bitcast.30, f32[1,16,4096]{2,1,0:T(8,128)} %bitcast.31), kind=kLoop, calls=%fused_computation | loop fusion | flops 786432 | bytes 2097152 | tf_op jit(solution)/shard_map/stack | solution.py:148
  1.9 0.0 copy-start.2
  2.0 5.1 %collective-permute-start.2 = (f32[4,16,256]{2,1,0:T(8,128)S(1)}, f32[4,16,256]{2,1,0:T(8,128)S(1)}, u32[]{:S(2)}, u32[]{:S(2)}) collective-permute-start(f32[4,16,256]{2,1,0:T(8,128)S(1)} %get-tuple-element.7), channel_id=1, source_target_pairs={{0,24},{8,0},{16,8},{24,16},{1,25},{9,1},{17,9},{25,17},{2,26},{10... | collective-permute-start | bytes 196616 | tf_op jit(solution)/shard_map/ppermute | solution.py:159
  7.1 1.0 %collective-permute-start = (f32[4,16,256]{2,1,0:T(8,128)S(1)}, f32[4,16,256]{2,1,0:T(8,128)S(1)}, u32[]{:S(2)}, u32[]{:S(2)}) collective-permute-start(f32[4,16,256]{2,1,0:T(8,128)S(1)} %get-tuple-element.9), channel_id=1, source_target_pairs={{0,8},{8,16},{16,24},{24,0},{1,9},{9,17},{17,25},{25,1},{2,10},{10... | collective-permute-start | bytes 196616 | tf_op jit(solution)/shard_map/ppermute | solution.py:159
  8.1 0.1 broadcast_select_fusion.1
  8.2 1.5 %collective-permute-start.3 = (f32[64]{0:T(128)S(1)}, f32[64]{0:T(128)S(1)}, u32[]{:S(2)}, u32[]{:S(2)}) collective-permute-start(f32[64]{0:T(128)S(1)} %broadcast_select_fusion.1), channel_id=1, source_target_pairs={{0,4},{4,0},{1,5},{5,1},{2,6},{6,2},{3,7},{7,3},{8,12},{12,8},{9,1... | collective-permute-start | bytes 776 | tf_op jit(solution)/shard_map/ppermute | solution.py:17
  9.7 0.7 %copy-done.3 = f32[4]{0:T(128)S(1)} copy-done((f32[4]{0:T(128)S(1)}, f32[4]{0:T(128)}, u32[]{:S(2)}) %copy-start.3) | copy-done | bytes 40
  10.4 0.7 %fusion.7 = (f32[1]{0:T(128)}, f32[1]{0:T(128)}, f32[1]{0:T(128)}, f32[1]{0:T(128)}) fusion(f32[4]{0:T(128)S(1)} %copy-done.3), kind=kLoop, calls=%fused_computation.154 | loop fusion | bytes 32 | tf_op jit(solution)/shard_map/slice | solution.py:185
  13.1 0.1 concatenate.3
  13.2 0.1 dynamic_slice.32
  13.3 0.1 fusion
  13.4 0.1 fusion.1
  13.5 0.1 fusion.2
  13.6 0.1 fusion.3
  13.6 0.1 fusion.6
  13.7 0.1 fusion.4
  13.8 0.1 fusion.5
  13.9 0.0 slice-start
  13.9 0.7 %slice-done = f32[256]{0:T(256)S(1)} async-done(((f32[384]{0:T(512)}), f32[256]{0:T(256)S(1)}, s32[]{:S(2)}) %slice-start) | async-done | bytes 1048 | tf_op jit(solution)/shard_map/slice | solution.py:178
  14.6 0.8 %multiply_reduce_fusion = f32[256]{0:T(256)S(1)} fusion(f32[256]{0:T(256)S(1)} %get-tuple-element.14, f32[256]{0:T(256)S(1)} %get-tuple-element.15, f32[256]{0:T(256)S(1)} %get-tuple-element.16, f32[256]{0:T(256)S(1)} %get-tuple-element.17, f32[256]{0:T(256)S(1)} %get-tuple-element.18, f32[256]{0:T(256)S(1)} %get-tuple-element.19, ...), kind=kLoop, calls=%fused_computation.5 | loop fusion | flops 265984 | bytes 141316 | tf_op jit(solution)/shard_map/reduce_sum | solution.py:181
  15.5 0.7 %copy-done.1 = f32[384]{0:T(512)S(1)} copy-done((f32[384]{0:T(512)S(1)}, f32[384]{0:T(512)}, u32[]{:S(2)}) %copy-start.1) | copy-done | bytes 1560
  16.1 1.5 %multiply_multiply_fusion = (f32[256]{0:T(256)S(1)}, f32[256]{0:T(256)S(1)}, f32[256]{0:T(256)S(1)}) fusion(f32[4096]{0:T(1024)} %param.12, s32[]{:T(128)S(6)} %select_n.431, f32[]{:T(128)} %bitcast.12, f32[256]{0:T(256)S(1)} %multiply_reduce_fusion, f32[384]{0:T(512)S(1)} %copy-done.1, f32[4096]{0:T(1024)} %param.11, f32[]{:T(128)} %bitcast.10, f32[]{:T(128)} %bitcast.9), kind=kLoop, calls=%fused_computation.138 | loop fusion | flops 2560 | bytes 7184 | tf_op jit(solution)/shard_map/mul | solution.py:195
  17.6 0.6 %stack.71.par_ref = f32[8,256]{1,0:T(8,128)} concatenate(f32[1,256]{1,0:T(1,128)S(1)} %bitcast.39, f32[1,256]{1,0:T(1,128)S(1)} %bitcast.38, f32[1,256]{1,0:T(1,128)S(1)} %stack.66, f32[1,256]{1,0:T(1,128)S(1)} %bitcast.43, f32[1,256]{1,0:T(1,128)S(1)} %bitcast.42, f32[1,256]{1,0:T(1,128)S(1)} %bitcast.41, f32[1,256]{1,0:T(1,128)S(1)} %bitcast.40, f32[1,256]{1,0:T(1,128)S(1)} %stack_broadcast_in_dim.3), dimensions={0} | concatenate | bytes 16384 | tf_op jit(solution)/shard_map/stack | solution.py:187
  18.3 0.0 collective-permute-done.2
  18.3 0.0 collective-permute-done.1
  18.3 0.7 %pad_maximum_fusion.1.data_ref = f32[4,4,16,256]{3,2,1,0:T(8,128)} fusion(f32[1,4,16,256]{3,2,1,0:T(8,128)S(1)} %bitcast.34, f32[1,4,16,256]{3,2,1,0:T(8,128)S(1)} %bitcast.35, f32[1,4,16,256]{3,2,1,0:T(8,128)S(1)} %bitcast.36, f32[1,4,16,256]{3,2,1,0:T(8,128)S(1)} %get-tuple-element.6), kind=kLoop, calls=%fused_computation.1 | loop fusion | flops 196608 | bytes 524288 | tf_op jit(solution)/shard_map/stack | solution.py:166
  19.0 2.6 %shard_map.121 = f32[4,24,256]{2,1,0:T(8,128)} custom-call(s32[1]{0:T(128)} %bitcast.place_ref, f32[4,4,16,256]{3,2,1,0:T(8,128)} %pad_maximum_fusion.1.data_ref, f32[8,256]{1,0:T(8,128)} %stack.71.par_ref), custom_call_target="tpu_custom_call" | custom-call | tf_op jit(solution)/shard_map/pallas_call | solution.py:114
  21.6 9.9 %all_to_all.5 = f32[4,24,256]{2,1,0:T(8,128)S(1)} all-to-all(f32[4,24,256]{2,1,0:T(8,128)} %shard_map.121), channel_id=1, replica_groups=mesh['tm'=4,'space'=2,'hyp'=4] {'tm'}, dimensions={0} | all-to-all | bytes 196608 | tf_op jit(solution)/shard_map/all_to_all | solution.py:200
  31.5 5.4 %all_gather.3 = f32[5,4096]{1,0:T(8,128)S(1)} all-gather(f32[5,1024]{1,0:T(8,128)S(1)} %bitcast.32), channel_id=1, replica_groups=mesh['tm'=4,'space'=2,'hyp'=4] {'hyp'}, dimensions={1}, use_global_device_ids=true | all-gather | bytes 102400 | tf_op jit(solution)/shard_map/all_gather | solution.py:203
  36.9 0.6 %slice.561 = f32[1,4096]{1,0:T(1,128)} slice(f32[5,4096]{1,0:T(8,128)S(1)} %all_gather.3), slice={[0:1], [0:4096]} | slice | bytes 32768 | tf_op jit(solution)/shard_map/slice | solution.py:204
  37.5 0.6 %slice.562 = f32[4,4096]{1,0:T(4,128)} slice(f32[5,4096]{1,0:T(8,128)S(1)} %all_gather.3), slice={[1:5], [0:4096]} | slice | bytes 131072 | tf_op jit(solution)/shard_map/slice | solution.py:204
  38.1 0.6 %copy.14 = f32[4,2,8,256]{3,2,0,1:T(8,128)} copy(f32[4,2,8,256]{3,2,1,0:T(8,128)S(1)} %slice_bitcast_fusion) | data formatting | bytes 131072 | tf_op jit(solution)/shard_map/reshape | solution.py:201
  (16 shorter events, 0.1 us)
Async XLA Ops:
  1.9 6.2 %copy-start.2 = (f32[4096]{0:T(1024)S(1)}, f32[4096]{0:T(1024)}, u32[]{:S(2)}) copy-start(f32[4096]{0:T(1024)} %param.10) | copy-start | bytes 49156
  2.0 16.3 %collective-permute-start.2 = (f32[4,16,256]{2,1,0:T(8,128)S(1)}, f32[4,16,256]{2,1,0:T(8,128)S(1)}, u32[]{:S(2)}, u32[]{:S(2)}) collective-permute-start(f32[4,16,256]{2,1,0:T(8,128)S(1)} %get-tuple-element.7), channel_id=1, source_target_pairs={{0,24},{8,0},{16,8},{24,16},{1,25},{9,1},{17,9},{25,17},{2,26},{10... | collective-permute-start | bytes 196616 | tf_op jit(solution)/shard_map/ppermute | solution.py:159
  7.1 11.2 %collective-permute-start.1 = (f32[4,16,256]{2,1,0:T(8,128)S(1)}, f32[4,16,256]{2,1,0:T(8,128)S(1)}, u32[]{:S(2)}, u32[]{:S(2)}) collective-permute-start(f32[4,16,256]{2,1,0:T(8,128)S(1)} %get-tuple-element.8), channel_id=1, source_target_pairs={{0,16},{8,24},{16,0},{24,8},{1,17},{9,25},{17,1},{25,9},{2,18},{10... | collective-permute-start | bytes 196616 | tf_op jit(solution)/shard_map/ppermute | solution.py:159
  7.1 11.2 %collective-permute-start = (f32[4,16,256]{2,1,0:T(8,128)S(1)}, f32[4,16,256]{2,1,0:T(8,128)S(1)}, u32[]{:S(2)}, u32[]{:S(2)}) collective-permute-start(f32[4,16,256]{2,1,0:T(8,128)S(1)} %get-tuple-element.9), channel_id=1, source_target_pairs={{0,8},{8,16},{16,24},{24,0},{1,9},{9,17},{17,25},{25,1},{2,10},{10... | collective-permute-start | bytes 196616 | tf_op jit(solution)/shard_map/ppermute | solution.py:159
  8.2 4.9 %collective-permute-start.3 = (f32[64]{0:T(128)S(1)}, f32[64]{0:T(128)S(1)}, u32[]{:S(2)}, u32[]{:S(2)}) collective-permute-start(f32[64]{0:T(128)S(1)} %broadcast_select_fusion.1), channel_id=1, source_target_pairs={{0,4},{4,0},{1,5},{5,1},{2,6},{6,2},{3,7},{7,3},{8,12},{12,8},{9,1... | collective-permute-start | bytes 776 | tf_op jit(solution)/shard_map/ppermute | solution.py:17
  9.7 0.7 %copy-start.3 = (f32[4]{0:T(128)S(1)}, f32[4]{0:T(128)}, u32[]{:S(2)}) copy-start(f32[4]{0:T(128)} %param.19) | copy-start | bytes 52
  13.3 0.6 %copy-start = (f32[384]{0:T(512)}, f32[384]{0:T(512)S(1)}, u32[]{:S(2)}) copy-start(f32[384]{0:T(512)S(1)} %dynamic_slice.32) | copy-start | bytes 4612
  13.9 0.7 %slice-start = ((f32[384]{0:T(512)}), f32[256]{0:T(256)S(1)}, s32[]{:S(2)}) async-start(f32[384]{0:T(512)} %copy-done), calls=%async_computation.1 | async-start | bytes 2048 | tf_op jit(solution)/shard_map/slice | solution.py:178
  15.5 0.7 %copy-start.1 = (f32[384]{0:T(512)S(1)}, f32[384]{0:T(512)}, u32[]{:S(2)}) copy-start(f32[384]{0:T(512)} %copy-done) | copy-start | bytes 4612

commit v5 on v4

--- a/solution.py
+++ b/solution.py
@@ -25,14 +25,37 @@
     return jnp.concatenate([low, block, high])
 
 
-def chain_kernel(place_ref, data_ref, par_ref, out_ref, piv_ref, slv_ref):
+def chain_kernel(
+    place_ref, hyper_ref, window_ref, offsets_ref, weights_ref, node_ref, data_ref,
+    out_ref, piv_ref, slv_ref,
+):
     blocks, _, rows, width = data_ref.shape
     place = place_ref[0]
-    ns = par_ref[2:3, :]
-    ls2 = par_ref[3:4, :]
-    sp = par_ref[4:5, :]
-    mps = par_ref[5:6, :]
-    qs = par_ref[6:7, :]
+    window = window_ref[...]
+    span = window.shape[1]
+    near_off = offsets_ref[...]
+    nearby = jnp.zeros(near_off.shape, jnp.float32)
+    own_kappa = None
+    for shift in range(-BAND, BAND + 1):
+        moved = pltpu.roll(window, (span - BAND - shift) % span, 1)[:, :width]
+        if shift == 0:
+            own_kappa = moved
+        nearby = jnp.where(near_off == shift, moved, nearby)
+    weights = weights_ref[...]
+    edge_sum = (
+        weights[0:1] * nearby[0:1]
+        + weights[1:2] * nearby[1:2]
+        + weights[2:3] * nearby[2:3]
+        + weights[3:4] * nearby[3:4]
+    )
+    spatial = hyper_ref[0] * (node_ref[0:1, :] * own_kappa + edge_sum)
+    scaled = hyper_ref[1] * spatial
+    persist = jnp.tanh(hyper_ref[2] + node_ref[1:2, :])
+    ns = jnp.zeros_like(persist) + hyper_ref[3]
+    ls2 = (1.0 - persist * persist) / persist
+    sp = scaled * (1.0 + persist * persist)
+    mps = -persist * scaled
+    qs = 2.0 * persist * (1.0 - persist * persist) * scaled
     two_ls2 = 2.0 * ls2
     zeros = jnp.zeros_like(sp)
     carry = (zeros,) * 11
@@ -107,18 +130,18 @@
         out_ref[block, rows : rows + 8, :] = stats
 
 
-def run_chain(place, data, params):
+def run_chain(place, hyper, window, near_off, weights, node, data):
     blocks, _, rows, width = data.shape
     vmem = pl.BlockSpec(memory_space=pltpu.VMEM)
     smem = pl.BlockSpec(memory_space=pltpu.SMEM)
     return pl.pallas_call(
         chain_kernel,
         out_shape=jax.ShapeDtypeStruct((blocks, rows + 8, width), jnp.float32),
-        in_specs=[smem, vmem, vmem],
+        in_specs=[smem, smem, vmem, vmem, vmem, vmem, vmem],
         out_specs=vmem,
         scratch_shapes=[pltpu.VMEM((blocks, rows, width), jnp.float32)] * 2,
         interpret=INTERPRET,
-    )(place, data, params)
+    )(place, hyper, window, near_off, weights, node, data)
 
 
 def per_device_body(
@@ -166,37 +189,19 @@
     data = jnp.stack(arrived)
     place = time_place.astype(jnp.int32).reshape(1)
 
-    window = lax.dynamic_slice_in_dim(padded, first, chunk + 2 * BAND)
+    window = lax.dynamic_slice_in_dim(padded, first, chunk + 2 * BAND)[None]
     near_off = lax.dynamic_slice_in_dim(offsets, first, chunk, axis=1)
     weights = lax.dynamic_slice_in_dim(edge_weight, first, chunk, axis=1)
-    mass = lax.dynamic_slice_in_dim(node_mass, first, chunk)
-    base = lax.dynamic_slice_in_dim(rho_base, first, chunk)
-    own_kappa = window[BAND : BAND + chunk]
-    nearby = jnp.zeros(near_off.shape, jnp.float32)
-    for shift in range(-BAND, BAND + 1):
-        nearby = jnp.where(
-            near_off == shift, window[None, BAND + shift : BAND + shift + chunk], nearby
-        )
-    spatial = jnp.exp(2.0 * hyper_params[0]) * (
-        mass * own_kappa + jnp.sum(weights * nearby, axis=0)
-    )
-    scaled = jnp.exp(hyper_params[1]) * spatial
-    persist = jnp.tanh(hyper_params[2] + base)
-    nugget_scale = jnp.exp(hyper_params[3]) + jnp.zeros_like(persist)
-    log_slope = (1.0 - persist * persist) / persist
-    params = jnp.stack(
+    node = lax.dynamic_slice_in_dim(jnp.stack([node_mass, rho_base]), first, chunk, axis=1)
+    hyper = jnp.stack(
         [
-            scaled,
-            persist,
-            nugget_scale,
-            log_slope,
-            scaled * (1.0 + persist * persist),
-            -persist * scaled,
-            2.0 * persist * (1.0 - persist * persist) * scaled,
-            jnp.zeros_like(persist),
+            jnp.exp(2.0 * hyper_params[0]),
+            jnp.exp(hyper_params[1]),
+            hyper_params[2],
+            jnp.exp(hyper_params[3]),
         ]
     )
-    payload = run_chain(place, data, params)
+    payload = run_chain(place, hyper, window, near_off, weights, node, data)
     received = lax.all_to_all(payload, "tm", 0, 0, tiled=True)
     solution_out = received[:, :row_count].transpose(1, 0, 2).reshape(row_count, quarter)
     stats_quarter = received[:, row_count : row_count + 5].transpose(1, 0, 2).reshape(5, quarter)

time: 39.2 us -> 38.9 us (level)
  local copies, waits for them, and re-layouts: 5.99 us -> 5.25 us
  blocking collectives: 15.3 us -> 15.9 us
  Pallas kernels: 2.56 us -> 3.1 us
  other arithmetic: 4.39 us -> 3.93 us
    dynamic_slice x1 -> x3, local copies, waits for them, and re-layouts: 0.08 us -> 1.96 us  [the longest x1 1.29 us: per_device_body(): near_off = lax.dynamic_slice_in_dim(offsets, first, chunk, axis=1)]
    another operation x0 -> x2, other arithmetic: none -> 1.86 us  [the longest x1 1.2 us: per_device_body(): jnp.stack([jnp.exp(2.0 * hyper_params[0]), jnp.exp(hyper_params[1]), hype...]
    mul x2 -> x0, other arithmetic: 1.48 us -> none  [the longest x1 1.48 us: per_device_body(): 2.0 * persist * (1.0 - persist * persist) * scaled]
    unnamed x9 -> x11, local copies, waits for them, and re-layouts: 1.35 us -> 0.03 us
    slice x10 -> x1, local copies, waits for them, and re-layouts: 1.93 us -> 0.65 us  [per_device_body(): hyper_params[0]]
    reduce_sum x1 -> x0, other arithmetic: 0.85 us -> none  [per_device_body(): jnp.sum(weights * nearby, axis=0)]
    another operation x3 -> x0, local copies, waits for them, and re-layouts: 0.63 us -> none  [per_device_body(): jnp.stack([scaled, persist, nugget_scale, log_slope, scaled * (1.0 + pers...]
    broadcast_in_dim x0 -> x1, local copies, waits for them, and re-layouts: none -> 0.59 us  [per_device_body(): window = lax.dynamic_slice_in_dim(padded, first, chunk + 2 * BAND)[None]]
  transfers between devices with their start and end apart: 4 -> 4, of which waited for: 0 -> 0; matrix products, arithmetic and copies ran while one was open for 11% -> 14% of each run, Pallas kernels for 0% -> 0%
where the time goes in v5:
time: 38.9 us; the launch traced here: 38.5 us
  blocking collectives  15.9 us (41%)
  starting transfers between devices  7.67 us (20%)
  local copies, waits for them, and re-layouts  5.25 us (13%)
  other arithmetic  3.93 us (10%)
  Pallas kernels  3.1 us (8%)
  between operations  2.71 us (7%)
    all_to_all x1, blocking collectives, per_device_body(): received = lax.all_to_all(payload, 'tm', 0, 0, tiled=True)  10.5 us
    ppermute x3, starting transfers between devices, per_device_body(): lax.ppermute(pieces[shift], 'tm', [(i, (i + shift) % time_count) for i in...  6.14 us
    all_gather x1, blocking collectives, per_device_body(): stats_full = lax.all_gather(stats_quarter, 'hyp', axis=1, tiled=True)  5.4 us
    pallas_call x1, Pallas kernels, run_chain(): pl.pallas_call(chain_kernel, out_shape=jax.ShapeDtypeStruct((blocks, rows...  3.1 us
    ppermute x1, starting transfers between devices, with_halo(): got = lax.ppermute(send, axis, [(0, 1), (1, 0)])  1.53 us
    dynamic_slice x1, local copies, waits for them, and re-layouts, per_device_body(): near_off = lax.dynamic_slice_in_dim(offsets, first, chunk, axis=1)  1.29 us
    slice x2, local copies, waits for them, and re-layouts, per_device_body(): return (solution_out, stats_full[0], stats_full[1:5])  1.26 us
    another operation x1, other arithmetic, per_device_body(): stacked = jnp.stack([roughness, coupling, obs_weight, observed])  1.26 us
  transfers between devices with their start and end apart: 4, of which 0 were waited for; matrix products, arithmetic and copies ran while one was open for 14% of the time, Pallas kernels for 0%

profile of v5, /device:TPU:0, one launch (start us, length us, event | category | flops | bytes accessed | tf_op | source)
XLA Modules:
  0.0 38.5 jit_solution(6059916794710155021)
XLA Ops:
  0.6 0.0 copy-start
  0.7 1.3 %pad_maximum_fusion = f32[4,16,4096]{2,1,0:T(8,128)S(1)} fusion(f32[1,16,4096]{2,1,0:T(8,128)} %bitcast.20, f32[1,16,4096]{2,1,0:T(8,128)} %bitcast.21, f32[1,16,4096]{2,1,0:T(8,128)} %bitcast.22, f32[1,16,4096]{2,1,0:T(8,128)} %bitcast.23), kind=kLoop, calls=%fused_computation | loop fusion | flops 786432 | bytes 2097152 | tf_op jit(solution)/shard_map/stack | solution.py:171
  1.9 0.0 copy-start.1
  2.0 5.1 %collective-permute-start.3 = (f32[4,16,256]{2,1,0:T(8,128)S(1)}, f32[4,16,256]{2,1,0:T(8,128)S(1)}, u32[]{:S(2)}, u32[]{:S(2)}) collective-permute-start(f32[4,16,256]{2,1,0:T(8,128)S(1)} %get-tuple-element.4), channel_id=1, source_target_pairs={{0,24},{8,0},{16,8},{24,16},{1,25},{9,1},{17,9},{25,17},{2,26},{10... | collective-permute-start | bytes 196616 | tf_op jit(solution)/shard_map/ppermute | solution.py:182
  7.1 0.0 collective-permute-start.1
  7.1 1.0 %collective-permute-start.2 = (f32[4,16,256]{2,1,0:T(8,128)S(1)}, f32[4,16,256]{2,1,0:T(8,128)S(1)}, u32[]{:S(2)}, u32[]{:S(2)}) collective-permute-start(f32[4,16,256]{2,1,0:T(8,128)S(1)} %get-tuple-element.5), channel_id=1, source_target_pairs={{0,16},{8,24},{16,0},{24,8},{1,17},{9,25},{17,1},{25,9},{2,18},{10... | collective-permute-start | bytes 196616 | tf_op jit(solution)/shard_map/ppermute | solution.py:182
  8.1 0.0 copy-done.1
  8.2 0.0 copy-start.4
  8.2 0.1 broadcast_select_fusion.1
  8.2 1.5 %collective-permute-start = (f32[64]{0:T(128)S(1)}, f32[64]{0:T(128)S(1)}, u32[]{:S(2)}, u32[]{:S(2)}) collective-permute-start(f32[64]{0:T(128)S(1)} %broadcast_select_fusion.1), channel_id=1, source_target_pairs={{0,4},{4,0},{1,5},{5,1},{2,6},{6,2},{3,7},{7,3},{8,12},{12,8},{9,1... | collective-permute-start | bytes 776 | tf_op jit(solution)/shard_map/ppermute | solution.py:17
  9.8 0.0 copy-done
  9.8 0.6 %constant_dynamic-slice_fusion.3.weights_ref = f32[4,256]{1,0:T(4,128)} fusion(f32[4,4096]{1,0:T(4,128)S(1)} %copy-done, s32[]{:T(128)S(6)} %select_n.44), kind=kLoop, calls=%fused_computation.11 | loop fusion | bytes 8196 | tf_op jit(solution)/shard_map/dynamic_slice | solution.py:194
  10.4 1.3 %constant_dynamic-slice_fusion.4.offsets_ref = s32[4,256]{1,0:T(4,128)} fusion(s32[4,4096]{1,0:T(4,128)} %param.14, s32[]{:T(128)S(6)} %select_n.44), kind=kLoop, calls=%fused_computation.12 | loop fusion | bytes 8196 | tf_op jit(solution)/shard_map/dynamic_slice | solution.py:193
  11.7 0.0 copy-done.4
  11.7 0.7 %fusion.1 = (f32[1]{0:T(128)}, f32[1]{0:T(128)}, f32[1]{0:T(128)}, f32[1]{0:T(128)}) fusion(f32[4]{0:T(128)S(1)} %copy-done.4), kind=kLoop, calls=%fused_computation.17 | loop fusion | bytes 32 | tf_op jit(solution)/shard_map/slice | solution.py:198
  14.3 0.0 copy-done.3
  14.3 0.7 %fusion.node_ref = f32[2,256]{1,0:T(2,128)} fusion(s32[]{:T(128)S(6)} %select_n.44, f32[1,4096]{1,0:T(1,128)S(1)} %bitcast.29, f32[1,4096]{1,0:T(1,128)S(1)} %bitcast.30), kind=kLoop, calls=%fused_computation.7 | loop fusion | flops 512 | bytes 34820 | tf_op jit(solution)/shard_map/stack | solution.py:195
  15.0 1.2 %pad_maximum_fusion.2.hyper_ref = f32[4]{0:T(128)} fusion(f32[1]{0:T(128)S(6)} %exp.17, f32[1]{0:T(128)} %get-tuple-element.12, f32[1]{0:T(128)S(6)} %exp.16, f32[1]{0:T(128)S(6)} %exp.15), kind=kLoop, calls=%fused_computation.16 | loop fusion | flops 12 | bytes 32 | tf_op jit(solution)/shard_map/stack | solution.py:196
  16.2 0.0 collective-permute-done
  16.2 0.1 concatenate.3
  16.3 0.1 dynamic_slice.24
  16.3 0.6 %broadcast_in_dim.3.window_ref = f32[1,384]{1,0:T(1,128)} reshape(f32[384]{0:T(512)S(1)} %dynamic_slice.24) | data formatting | bytes 3072 | tf_op jit(solution)/shard_map/broadcast_in_dim | solution.py:192
  16.9 0.0 collective-permute-done.3
  16.9 0.0 collective-permute-done.1
  16.9 0.0 collective-permute-done.2
  16.9 0.7 %pad_maximum_fusion.1.data_ref = f32[4,4,16,256]{3,2,1,0:T(8,128)} fusion(f32[1,4,16,256]{3,2,1,0:T(8,128)S(1)} %bitcast.26, f32[1,4,16,256]{3,2,1,0:T(8,128)S(1)} %bitcast.28, f32[1,4,16,256]{3,2,1,0:T(8,128)S(1)} %bitcast.27, f32[1,4,16,256]{3,2,1,0:T(8,128)S(1)} %get-tuple-element.3), kind=kLoop, calls=%fused_computation.1 | loop fusion | flops 196608 | bytes 524288 | tf_op jit(solution)/shard_map/stack | solution.py:189
  17.7 3.1 %shard_map.121 = f32[4,24,256]{2,1,0:T(8,128)} custom-call(s32[1]{0:T(128)} %bitcast.place_ref, f32[4]{0:T(128)} %pad_maximum_fusion.2.hyper_ref, f32[1,384]{1,0:T(1,128)} %broadcast_in_dim.3.window_ref, s32[4,256]{1,0:T(4,128)} %constant_dynamic-slice_fusion.4.offsets_ref, f32[4,256]{1,0:T(4,128)} %constant_dynamic-slice_fusion.3.weights_ref, ...), custom_call_target="tpu_custom_call" | custom-call | tf_op jit(solution)/shard_map/pallas_call | solution.py:137
  20.8 10.5 %all_to_all.5 = f32[4,24,256]{2,1,0:T(8,128)S(1)} all-to-all(f32[4,24,256]{2,1,0:T(8,128)} %shard_map.121), channel_id=1, replica_groups=mesh['tm'=4,'space'=2,'hyp'=4] {'tm'}, dimensions={0} | all-to-all | bytes 196608 | tf_op jit(solution)/shard_map/all_to_all | solution.py:205
  31.2 5.4 %all_gather.3 = f32[5,4096]{1,0:T(8,128)S(1)} all-gather(f32[5,1024]{1,0:T(8,128)S(1)} %bitcast.24), channel_id=1, replica_groups=mesh['tm'=4,'space'=2,'hyp'=4] {'hyp'}, dimensions={1}, use_global_device_ids=true | all-gather | bytes 102400 | tf_op jit(solution)/shard_map/all_gather | solution.py:208
  36.6 0.6 %slice.45 = f32[4,4096]{1,0:T(4,128)} slice(f32[5,4096]{1,0:T(8,128)S(1)} %all_gather.3), slice={[1:5], [0:4096]} | slice | bytes 131072 | tf_op jit(solution)/shard_map/slice | solution.py:209
  37.3 0.6 %slice.44 = f32[1,4096]{1,0:T(1,128)} slice(f32[5,4096]{1,0:T(8,128)S(1)} %all_gather.3), slice={[0:1], [0:4096]} | slice | bytes 32768 | tf_op jit(solution)/shard_map/slice | solution.py:209
  37.9 0.6 %copy.14 = f32[4,2,8,256]{3,2,0,1:T(8,128)} copy(f32[4,2,8,256]{3,2,1,0:T(8,128)S(1)} %slice_bitcast_fusion) | data formatting | bytes 131072 | tf_op jit(solution)/shard_map/reshape | solution.py:206
  (8 shorter events, 0.1 us)
Async XLA Ops:
  0.6 9.1 %copy-start = (f32[4,4096]{1,0:T(4,128)S(1)}, f32[4,4096]{1,0:T(4,128)}, u32[]{:S(2)}) copy-start(f32[4,4096]{1,0:T(4,128)} %param.13) | copy-start | bytes 196612
  1.9 6.2 %copy-start.1 = (f32[4096]{0:T(1024)S(1)}, f32[4096]{0:T(1024)}, u32[]{:S(2)}) copy-start(f32[4096]{0:T(1024)} %param.10) | copy-start | bytes 49156
  2.0 14.9 %collective-permute-start.3 = (f32[4,16,256]{2,1,0:T(8,128)S(1)}, f32[4,16,256]{2,1,0:T(8,128)S(1)}, u32[]{:S(2)}, u32[]{:S(2)}) collective-permute-start(f32[4,16,256]{2,1,0:T(8,128)S(1)} %get-tuple-element.4), channel_id=1, source_target_pairs={{0,24},{8,0},{16,8},{24,16},{1,25},{9,1},{17,9},{25,17},{2,26},{10... | collective-permute-start | bytes 196616 | tf_op jit(solution)/shard_map/ppermute | solution.py:182
  7.1 9.8 %collective-permute-start.1 = (f32[4,16,256]{2,1,0:T(8,128)S(1)}, f32[4,16,256]{2,1,0:T(8,128)S(1)}, u32[]{:S(2)}, u32[]{:S(2)}) collective-permute-start(f32[4,16,256]{2,1,0:T(8,128)S(1)} %get-tuple-element.6), channel_id=1, source_target_pairs={{0,8},{8,16},{16,24},{24,0},{1,9},{9,17},{17,25},{25,1},{2,10},{10... | collective-permute-start | bytes 196616 | tf_op jit(solution)/shard_map/ppermute | solution.py:182
  7.1 9.8 %collective-permute-start.2 = (f32[4,16,256]{2,1,0:T(8,128)S(1)}, f32[4,16,256]{2,1,0:T(8,128)S(1)}, u32[]{:S(2)}, u32[]{:S(2)}) collective-permute-start(f32[4,16,256]{2,1,0:T(8,128)S(1)} %get-tuple-element.5), channel_id=1, source_target_pairs={{0,16},{8,24},{16,0},{24,8},{1,17},{9,25},{17,1},{25,9},{2,18},{10... | collective-permute-start | bytes 196616 | tf_op jit(solution)/shard_map/ppermute | solution.py:182
  8.2 3.5 %copy-start.4 = (f32[4]{0:T(128)S(1)}, f32[4]{0:T(128)}, u32[]{:S(2)}) copy-start(f32[4]{0:T(128)} %param.19) | copy-start | bytes 52
  8.2 7.9 %collective-permute-start = (f32[64]{0:T(128)S(1)}, f32[64]{0:T(128)S(1)}, u32[]{:S(2)}, u32[]{:S(2)}) collective-permute-start(f32[64]{0:T(128)S(1)} %broadcast_select_fusion.1), channel_id=1, source_target_pairs={{0,4},{4,0},{1,5},{5,1},{2,6},{6,2},{3,7},{7,3},{8,12},{12,8},{9,1... | collective-permute-start | bytes 776 | tf_op jit(solution)/shard_map/ppermute | solution.py:17
  9.8 4.5 %copy-start.3 = (f32[4096]{0:T(1024)S(1)}, f32[4096]{0:T(1024)}, u32[]{:S(2)}) copy-start(f32[4096]{0:T(1024)} %param.12) | copy-start | bytes 49156
  10.4 3.9 %copy-start.2 = (f32[4096]{0:T(1024)S(1)}, f32[4096]{0:T(1024)}, u32[]{:S(2)}) copy-start(f32[4096]{0:T(1024)} %param.11) | copy-start | bytes 49156

commit v6 on v5

--- a/solution.py
+++ b/solution.py
@@ -1,3 +1,5 @@
+import functools
+
 import jax
 import jax.numpy as jnp
 from jax import lax
@@ -25,15 +27,29 @@
     return jnp.concatenate([low, block, high])
 
 
-def chain_kernel(
-    place_ref, hyper_ref, window_ref, offsets_ref, weights_ref, node_ref, data_ref,
-    out_ref, piv_ref, slv_ref,
-):
-    blocks, _, rows, width = data_ref.shape
+def chain_kernel(*refs, aligned):
+    place_ref, hyper_ref, window_ref, nodes_hbm, offsets_hbm = refs[:5]
+    blocks = len(refs) - 12
+    pieces = refs[5 : 5 + blocks]
+    out_ref, piv_ref, slv_ref, data_ref, nodes_ref, offsets_ref, sems = refs[5 + blocks :]
+    _, _, rows, width = data_ref.shape
+    first = pl.multiple_of(place_ref[1], 128) if aligned else 0
+    node_copy = pltpu.make_async_copy(nodes_hbm.at[:, pl.ds(first, width)], nodes_ref, sems.at[0])
+    offsets_copy = pltpu.make_async_copy(
+        offsets_hbm.at[:, pl.ds(first, width)], offsets_ref, sems.at[1]
+    )
+    node_copy.start()
+    offsets_copy.start()
+    for shift in range(blocks):
+        data_ref[shift] = pieces[shift][...]
+    node_copy.wait()
+    offsets_copy.wait()
+
     place = place_ref[0]
     window = window_ref[...]
     span = window.shape[1]
     near_off = offsets_ref[...]
+    ones = jnp.ones((1, width), jnp.float32)
     nearby = jnp.zeros(near_off.shape, jnp.float32)
     own_kappa = None
     for shift in range(-BAND, BAND + 1):
@@ -41,17 +57,17 @@
         if shift == 0:
             own_kappa = moved
         nearby = jnp.where(near_off == shift, moved, nearby)
-    weights = weights_ref[...]
+    weights = nodes_ref[2:6, :]
     edge_sum = (
         weights[0:1] * nearby[0:1]
         + weights[1:2] * nearby[1:2]
         + weights[2:3] * nearby[2:3]
         + weights[3:4] * nearby[3:4]
     )
-    spatial = hyper_ref[0] * (node_ref[0:1, :] * own_kappa + edge_sum)
-    scaled = hyper_ref[1] * spatial
-    persist = jnp.tanh(hyper_ref[2] + node_ref[1:2, :])
-    ns = jnp.zeros_like(persist) + hyper_ref[3]
+    spatial = jnp.exp(2.0 * hyper_ref[0] * ones) * (nodes_ref[0:1, :] * own_kappa + edge_sum)
+    scaled = jnp.exp(hyper_ref[1] * ones) * spatial
+    persist = jnp.tanh(hyper_ref[2] + nodes_ref[1:2, :])
+    ns = jnp.exp(hyper_ref[3] * ones)
     ls2 = (1.0 - persist * persist) / persist
     sp = scaled * (1.0 + persist * persist)
     mps = -persist * scaled
@@ -130,18 +146,27 @@
         out_ref[block, rows : rows + 8, :] = stats
 
 
-def run_chain(place, hyper, window, near_off, weights, node, data):
-    blocks, _, rows, width = data.shape
+def run_chain(place, hyper, window, nodes, offsets, pieces):
+    blocks = len(pieces)
+    _, rows, width = pieces[0].shape
     vmem = pl.BlockSpec(memory_space=pltpu.VMEM)
     smem = pl.BlockSpec(memory_space=pltpu.SMEM)
+    hbm = pl.BlockSpec(memory_space=pl.ANY)
     return pl.pallas_call(
-        chain_kernel,
+        functools.partial(chain_kernel, aligned=nodes.shape[1] != width),
         out_shape=jax.ShapeDtypeStruct((blocks, rows + 8, width), jnp.float32),
-        in_specs=[smem, smem, vmem, vmem, vmem, vmem, vmem],
+        in_specs=[smem, smem, vmem, hbm, hbm] + [vmem] * blocks,
         out_specs=vmem,
-        scratch_shapes=[pltpu.VMEM((blocks, rows, width), jnp.float32)] * 2,
+        scratch_shapes=[
+            pltpu.VMEM((blocks, rows, width), jnp.float32),
+            pltpu.VMEM((blocks, rows, width), jnp.float32),
+            pltpu.VMEM((blocks, 4, rows, width), jnp.float32),
+            pltpu.VMEM((6, width), jnp.float32),
+            pltpu.VMEM((4, width), jnp.int32),
+            pltpu.SemaphoreType.DMA((2,)),
+        ],
         interpret=INTERPRET,
-    )(place, hyper, window, near_off, weights, node, data)
+    )(place, hyper, window, nodes, offsets, *pieces)
 
 
 def per_device_body(
@@ -186,22 +211,14 @@
         )
         for shift in range(1, time_count)
     ]
-    data = jnp.stack(arrived)
-    place = time_place.astype(jnp.int32).reshape(1)
-
+    place = jnp.stack([time_place, first]).astype(jnp.int32)
     window = lax.dynamic_slice_in_dim(padded, first, chunk + 2 * BAND)[None]
-    near_off = lax.dynamic_slice_in_dim(offsets, first, chunk, axis=1)
-    weights = lax.dynamic_slice_in_dim(edge_weight, first, chunk, axis=1)
-    node = lax.dynamic_slice_in_dim(jnp.stack([node_mass, rho_base]), first, chunk, axis=1)
-    hyper = jnp.stack(
-        [
-            jnp.exp(2.0 * hyper_params[0]),
-            jnp.exp(hyper_params[1]),
-            hyper_params[2],
-            jnp.exp(hyper_params[3]),
-        ]
-    )
-    payload = run_chain(place, hyper, window, near_off, weights, node, data)
+    nodes = jnp.concatenate([node_mass[None], rho_base[None], edge_weight], axis=0)
+    near_off = offsets
+    if chunk % 128:
+        nodes = lax.dynamic_slice_in_dim(nodes, first, chunk, axis=1)
+        near_off = lax.dynamic_slice_in_dim(offsets, first, chunk, axis=1)
+    payload = run_chain(place, hyper_params, window, nodes, near_off, arrived)
     received = lax.all_to_all(payload, "tm", 0, 0, tiled=True)
     solution_out = received[:, :row_count].transpose(1, 0, 2).reshape(row_count, quarter)
     stats_quarter = received[:, row_count : row_count + 5].transpose(1, 0, 2).reshape(5, quarter)

time: 38.9 us -> 35.3 us (0.907)
  between operations: 2.71 us -> 0.74 us
  blocking collectives: 15.9 us -> 14.5 us
  local copies, waits for them, and re-layouts: 5.25 us -> 3.95 us
  other arithmetic: 3.93 us -> 2.66 us
  starting transfers between devices: 7.67 us -> 8.52 us
  waiting for transfers between devices: 0.01 us -> 0.74 us
  Pallas kernels: 3.1 us -> 3.8 us
    another operation x3 -> x1, other arithmetic: 2.59 us -> 0.62 us  [per_device_body(): place = jnp.stack([time_place, first]).astype(jnp.int32)]
    all_to_all x1, blocking collectives: 10.5 us -> 9.12 us  [per_device_body(): received = lax.all_to_all(payload, 'tm', 0, 0, tiled=True)]
    dynamic_slice x2 -> x1, local copies, waits for them, and re-layouts: 1.89 us -> 0.66 us  [per_device_body(): lax.dynamic_slice_in_dim(stacked, hyp_place * quarter + lax.rem(time_plac...]
    ppermute x3, starting transfers between devices: 6.14 us -> 6.99 us  [per_device_body(): lax.ppermute(pieces[shift], 'tm', [(i, (i + shift) % time_count) for i in...]
    ppermute x1, waiting for transfers between devices: 0.01 us -> 0.73 us  [with_halo(): got = lax.ppermute(send, axis, [(0, 1), (1, 0)])]
    pallas_call x1, Pallas kernels: 3.1 us -> 3.8 us  [run_chain(): pl.pallas_call(functools.partial(chain_kernel, aligned=nodes.shape[1] !=...]
    concatenate x0 -> x1, other arithmetic: none -> 0.7 us  [per_device_body(): jnp.concatenate([node_mass[None], rho_base[None], edge_weight], axis=0)]
    slice x1 -> x0, local copies, waits for them, and re-layouts: 0.65 us -> none  [per_device_body(): hyper_params[0]]
  transfers between devices with their start and end apart: 4 -> 4, of which waited for: 0 -> 1; matrix products, arithmetic and copies ran while one was open for 14% -> 6% of each run, Pallas kernels for 0% -> 0%
where the time goes in v6:
time: 35.3 us; the launch traced here: 34.9 us
  blocking collectives  14.5 us (41%)
  starting transfers between devices  8.52 us (24%)
  local copies, waits for them, and re-layouts  3.95 us (11%)
  Pallas kernels  3.8 us (11%)
  other arithmetic  2.66 us (8%)
  waiting for transfers between devices  0.74 us (2%)
  between operations  0.74 us (2%)
    all_to_all x1, blocking collectives, per_device_body(): received = lax.all_to_all(payload, 'tm', 0, 0, tiled=True)  9.12 us
    ppermute x3, starting transfers between devices, per_device_body(): lax.ppermute(pieces[shift], 'tm', [(i, (i + shift) % time_count) for i in...  6.99 us
    all_gather x1, blocking collectives, per_device_body(): stats_full = lax.all_gather(stats_quarter, 'hyp', axis=1, tiled=True)  5.4 us
    pallas_call x1, Pallas kernels, run_chain(): pl.pallas_call(functools.partial(chain_kernel, aligned=nodes.shape[1] !=...  3.8 us
    ppermute x1, starting transfers between devices, with_halo(): got = lax.ppermute(send, axis, [(0, 1), (1, 0)])  1.53 us
    slice x2, local copies, waits for them, and re-layouts, per_device_body(): return (solution_out, stats_full[0], stats_full[1:5])  1.26 us
    another operation x1, other arithmetic, per_device_body(): stacked = jnp.stack([roughness, coupling, obs_weight, observed])  1.26 us
    ppermute x1, waiting for transfers between devices, with_halo(): got = lax.ppermute(send, axis, [(0, 1), (1, 0)])  0.73 us
  transfers between devices with their start and end apart: 4, of which 1 were waited for; matrix products, arithmetic and copies ran while one was open for 6% of the time, Pallas kernels for 0%

profile of v6, /device:TPU:0, one launch (start us, length us, event | category | flops | bytes accessed | tf_op | source)
XLA Modules:
  0.0 34.9 jit_solution(8145858506923467282)
XLA Ops:
  0.7 1.3 %pad_maximum_fusion = f32[4,16,4096]{2,1,0:T(8,128)S(1)} fusion(f32[1,16,4096]{2,1,0:T(8,128)} %bitcast.16, f32[1,16,4096]{2,1,0:T(8,128)} %bitcast.17, f32[1,16,4096]{2,1,0:T(8,128)} %bitcast.18, f32[1,16,4096]{2,1,0:T(8,128)} %bitcast.19), kind=kLoop, calls=%fused_computation | loop fusion | flops 786432 | bytes 2097152 | tf_op jit(solution)/shard_map/stack | solution.py:196
  1.9 0.0 copy-start.6
  1.9 0.0 copy-start
  2.0 0.7 %constant_dynamic-slice_fusion = (f32[4,16,256]{2,1,0:T(8,128)S(1)}, f32[4,16,256]{2,1,0:T(8,128)S(1)}, f32[4,16,256]{2,1,0:T(8,128)S(1)}, f32[4,16,256]{2,1,0:T(8,128)}) fusion(f32[4,16,4096]{2,1,0:T(8,128)S(1)} %pad_maximum_fusion, s32[]{:T(128)S(6)} %select_n.42, s32[]{:T(128)S(6)} %select_n.41, s32[]{:T(128)S(6)} %select_n.40, s32[]{:T(128)S(6)} %select_n.39), kind=kLoop, calls=%fused_computation.4 | loop fusion | bytes 524304 | tf_op jit(solution)/shard_map/dynamic_slice | solution.py:198
  2.6 3.1 %collective-permute-start.1 = (f32[4,16,256]{2,1,0:T(8,128)S(1)}, f32[4,16,256]{2,1,0:T(8,128)S(1)}, u32[]{:S(2)}, u32[]{:S(2)}) collective-permute-start(f32[4,16,256]{2,1,0:T(8,128)S(1)} %get-tuple-element.5), channel_id=1, source_target_pairs={{0,8},{8,16},{16,24},{24,0},{1,9},{9,17},{17,25},{25,1},{2,10},{10... | collective-permute-start | bytes 196616 | tf_op jit(solution)/shard_map/ppermute | solution.py:207
  5.7 2.6 %collective-permute-start.2 = (f32[4,16,256]{2,1,0:T(8,128)S(1)}, f32[4,16,256]{2,1,0:T(8,128)S(1)}, u32[]{:S(2)}, u32[]{:S(2)}) collective-permute-start(f32[4,16,256]{2,1,0:T(8,128)S(1)} %get-tuple-element.4), channel_id=1, source_target_pairs={{0,16},{8,24},{16,0},{24,8},{1,17},{9,25},{17,1},{25,9},{2,18},{10... | collective-permute-start | bytes 196616 | tf_op jit(solution)/shard_map/ppermute | solution.py:207
  8.3 1.3 %collective-permute-start.3 = (f32[4,16,256]{2,1,0:T(8,128)S(1)}, f32[4,16,256]{2,1,0:T(8,128)S(1)}, u32[]{:S(2)}, u32[]{:S(2)}) collective-permute-start(f32[4,16,256]{2,1,0:T(8,128)S(1)} %get-tuple-element.3), channel_id=1, source_target_pairs={{0,24},{8,0},{16,8},{24,16},{1,25},{9,1},{17,9},{25,17},{2,26},{10... | collective-permute-start | bytes 196616 | tf_op jit(solution)/shard_map/ppermute | solution.py:207
  9.6 0.0 copy-done.6
  9.6 0.1 broadcast_select_fusion.1
  9.7 1.5 %collective-permute-start = (f32[64]{0:T(128)S(1)}, f32[64]{0:T(128)S(1)}, u32[]{:S(2)}, u32[]{:S(2)}) collective-permute-start(f32[64]{0:T(128)S(1)} %broadcast_select_fusion.1), channel_id=1, source_target_pairs={{0,4},{4,0},{1,5},{5,1},{2,6},{6,2},{3,7},{7,3},{8,12},{12,8},{9,1... | collective-permute-start | bytes 776 | tf_op jit(solution)/shard_map/ppermute | solution.py:19
  11.2 0.6 %pad_add_fusion.refs_0_ = s32[2]{0:T(128)} fusion(s32[1]{0:T(128)} %bitcast.1, s32[1]{0:T(128)} %bitcast), kind=kLoop, calls=%fused_computation.11 | loop fusion | flops 2 | bytes 16 | tf_op jit(solution)/shard_map/stack | solution.py:214
  11.8 0.0 copy-done
  11.8 0.0 copy-done.4
  11.8 0.0 copy-done.5
  11.9 0.7 %pad_maximum_fusion.1.refs_3_ = f32[6,4096]{1,0:T(8,128)} fusion(f32[4,4096]{1,0:T(4,128)S(1)} %copy-done, f32[1,4096]{1,0:T(1,128)S(1)} %bitcast.22, f32[1,4096]{1,0:T(1,128)S(1)} %bitcast.23), kind=kLoop, calls=%fused_computation.1 | loop fusion | flops 49152 | bytes 196608 | tf_op jit(solution)/shard_map/concatenate | solution.py:216
  12.5 0.7 %collective-permute-done = f32[64]{0:T(128)S(1)} collective-permute-done((f32[64]{0:T(128)S(1)}, f32[64]{0:T(128)S(1)}, u32[]{:S(2)}, u32[]{:S(2)}) %collective-permute-start) | collective-permute-done | bytes 288 | tf_op jit(solution)/shard_map/ppermute | solution.py:19
  13.3 0.1 concatenate.6
  13.4 0.1 dynamic_slice.15
  13.4 0.6 %broadcast_in_dim.9.refs_2_ = f32[1,384]{1,0:T(1,128)} reshape(f32[384]{0:T(512)S(1)} %dynamic_slice.15) | data formatting | bytes 3072 | tf_op jit(solution)/shard_map/broadcast_in_dim | solution.py:215
  14.0 0.0 collective-permute-done.1.refs_6_
  14.0 0.0 collective-permute-done.2.refs_7_
  14.0 0.0 copy-start.2
  14.0 0.0 collective-permute-done.3.refs_8_
  14.1 0.6 %copy-done.1 = f32[4,16,256]{2,1,0:T(8,128)} copy-done((f32[4,16,256]{2,1,0:T(8,128)}, f32[4,16,256]{2,1,0:T(8,128)S(1)}, u32[]{:S(2)}) %copy-start.1) | copy-done | bytes 65560
  14.6 0.0 copy-done.2
  14.7 0.0 copy-done.3
  14.7 3.8 %shard_map.121 = f32[4,24,256]{2,1,0:T(8,128)} custom-call(s32[2]{0:T(128)} %pad_add_fusion.refs_0_, f32[4]{0:T(128)} %refs_1_.1, f32[1,384]{1,0:T(1,128)} %broadcast_in_dim.9.refs_2_, f32[6,4096]{1,0:T(8,128)} %pad_maximum_fusion.1.refs_3_, s32[4,4096]{1,0:T(4,128)} %refs_4_.1, f32[4,16,256]{2,1,0:T(8,128)} %get-tuple-element.6.refs_5_, ...), custom_call_target="tpu_custom_call" | custom-call | tf_op jit(solution)/shard_map/pallas_call | solution.py:155
  18.5 9.1 %all_to_all.5 = f32[4,24,256]{2,1,0:T(8,128)S(1)} all-to-all(f32[4,24,256]{2,1,0:T(8,128)} %shard_map.121), channel_id=1, replica_groups=mesh['tm'=4,'space'=2,'hyp'=4] {'tm'}, dimensions={0} | all-to-all | bytes 196608 | tf_op jit(solution)/shard_map/all_to_all | solution.py:222
  27.6 5.4 %all_gather.3 = f32[5,4096]{1,0:T(8,128)S(1)} all-gather(f32[5,1024]{1,0:T(8,128)S(1)} %bitcast.20), channel_id=1, replica_groups=mesh['tm'=4,'space'=2,'hyp'=4] {'hyp'}, dimensions={1}, use_global_device_ids=true | all-gather | bytes 102400 | tf_op jit(solution)/shard_map/all_gather | solution.py:225
  33.0 0.6 %slice.29 = f32[4,4096]{1,0:T(4,128)} slice(f32[5,4096]{1,0:T(8,128)S(1)} %all_gather.3), slice={[1:5], [0:4096]} | slice | bytes 131072 | tf_op jit(solution)/shard_map/slice | solution.py:226
  33.7 0.6 %slice.28 = f32[1,4096]{1,0:T(1,128)} slice(f32[5,4096]{1,0:T(8,128)S(1)} %all_gather.3), slice={[0:1], [0:4096]} | slice | bytes 32768 | tf_op jit(solution)/shard_map/slice | solution.py:226
  34.3 0.6 %copy.14 = f32[4,2,8,256]{3,2,0,1:T(8,128)} copy(f32[4,2,8,256]{3,2,1,0:T(8,128)S(1)} %slice_bitcast_fusion) | data formatting | bytes 131072 | tf_op jit(solution)/shard_map/reshape | solution.py:223
  (8 shorter events, 0.0 us)
Async XLA Ops:
  1.9 7.7 %copy-start.6 = (f32[4096]{0:T(1024)S(1)}, f32[4096]{0:T(1024)}, u32[]{:S(2)}) copy-start(f32[4096]{0:T(1024)} %param.10) | copy-start | bytes 49156
  1.9 9.9 %copy-start = (f32[4,4096]{1,0:T(4,128)S(1)}, f32[4,4096]{1,0:T(4,128)}, u32[]{:S(2)}) copy-start(f32[4,4096]{1,0:T(4,128)} %param.13) | copy-start | bytes 196612
  2.6 11.4 %collective-permute-start.1 = (f32[4,16,256]{2,1,0:T(8,128)S(1)}, f32[4,16,256]{2,1,0:T(8,128)S(1)}, u32[]{:S(2)}, u32[]{:S(2)}) collective-permute-start(f32[4,16,256]{2,1,0:T(8,128)S(1)} %get-tuple-element.5), channel_id=1, source_target_pairs={{0,8},{8,16},{16,24},{24,0},{1,9},{9,17},{17,25},{25,1},{2,10},{10... | collective-permute-start | bytes 196616 | tf_op jit(solution)/shard_map/ppermute | solution.py:207
  5.7 8.3 %collective-permute-start.2 = (f32[4,16,256]{2,1,0:T(8,128)S(1)}, f32[4,16,256]{2,1,0:T(8,128)S(1)}, u32[]{:S(2)}, u32[]{:S(2)}) collective-permute-start(f32[4,16,256]{2,1,0:T(8,128)S(1)} %get-tuple-element.4), channel_id=1, source_target_pairs={{0,16},{8,24},{16,0},{24,8},{1,17},{9,25},{17,1},{25,9},{2,18},{10... | collective-permute-start | bytes 196616 | tf_op jit(solution)/shard_map/ppermute | solution.py:207
  8.3 5.8 %collective-permute-start.3 = (f32[4,16,256]{2,1,0:T(8,128)S(1)}, f32[4,16,256]{2,1,0:T(8,128)S(1)}, u32[]{:S(2)}, u32[]{:S(2)}) collective-permute-start(f32[4,16,256]{2,1,0:T(8,128)S(1)} %get-tuple-element.3), channel_id=1, source_target_pairs={{0,24},{8,0},{16,8},{24,16},{1,25},{9,1},{17,9},{25,17},{2,26},{10... | collective-permute-start | bytes 196616 | tf_op jit(solution)/shard_map/ppermute | solution.py:207
  9.6 2.2 %copy-start.4 = (f32[4096]{0:T(1024)S(1)}, f32[4096]{0:T(1024)}, u32[]{:S(2)}) copy-start(f32[4096]{0:T(1024)} %param.12) | copy-start | bytes 49156
  9.6 2.2 %copy-start.5 = (f32[4096]{0:T(1024)S(1)}, f32[4096]{0:T(1024)}, u32[]{:S(2)}) copy-start(f32[4096]{0:T(1024)} %param.11) | copy-start | bytes 49156
  9.7 3.6 %collective-permute-start = (f32[64]{0:T(128)S(1)}, f32[64]{0:T(128)S(1)}, u32[]{:S(2)}, u32[]{:S(2)}) collective-permute-start(f32[64]{0:T(128)S(1)} %broadcast_select_fusion.1), channel_id=1, source_target_pairs={{0,4},{4,0},{1,5},{5,1},{2,6},{6,2},{3,7},{7,3},{8,12},{12,8},{9,1... | collective-permute-start | bytes 776 | tf_op jit(solution)/shard_map/ppermute | solution.py:19
  14.0 0.6 %copy-start.1 = (f32[4,16,256]{2,1,0:T(8,128)}, f32[4,16,256]{2,1,0:T(8,128)S(1)}, u32[]{:S(2)}) copy-start(f32[4,16,256]{2,1,0:T(8,128)S(1)} %collective-permute-done.1.refs_6_) | copy-start | bytes 196612
  14.0 0.6 %copy-start.2 = (f32[4,16,256]{2,1,0:T(8,128)}, f32[4,16,256]{2,1,0:T(8,128)S(1)}, u32[]{:S(2)}) copy-start(f32[4,16,256]{2,1,0:T(8,128)S(1)} %collective-permute-done.2.refs_7_) | copy-start | bytes 196612
  14.0 0.6 %copy-start.3 = (f32[4,16,256]{2,1,0:T(8,128)}, f32[4,16,256]{2,1,0:T(8,128)S(1)}, u32[]{:S(2)}) copy-start(f32[4,16,256]{2,1,0:T(8,128)S(1)} %collective-permute-done.3.refs_8_) | copy-start | bytes 196612

commit v7 on v6

--- a/solution.py
+++ b/solution.py
@@ -29,19 +29,23 @@
 
 def chain_kernel(*refs, aligned):
     place_ref, hyper_ref, window_ref, nodes_hbm, offsets_hbm = refs[:5]
-    blocks = len(refs) - 12
+    blocks = len(refs) - 13
     pieces = refs[5 : 5 + blocks]
-    out_ref, piv_ref, slv_ref, data_ref, nodes_ref, offsets_ref, sems = refs[5 + blocks :]
+    out_ref, piv_ref, slv_ref, data_ref, nodes_ref, offsets_ref, sems, piece_sems = refs[5 + blocks :]
     _, _, rows, width = data_ref.shape
     first = pl.multiple_of(place_ref[1], 128) if aligned else 0
     node_copy = pltpu.make_async_copy(nodes_hbm.at[:, pl.ds(first, width)], nodes_ref, sems.at[0])
     offsets_copy = pltpu.make_async_copy(
         offsets_hbm.at[:, pl.ds(first, width)], offsets_ref, sems.at[1]
     )
+    piece_copies = [
+        pltpu.make_async_copy(pieces[shift], data_ref.at[shift], piece_sems.at[shift])
+        for shift in range(blocks)
+    ]
     node_copy.start()
     offsets_copy.start()
-    for shift in range(blocks):
-        data_ref[shift] = pieces[shift][...]
+    for copy in piece_copies:
+        copy.start()
     node_copy.wait()
     offsets_copy.wait()
 
@@ -75,6 +79,8 @@
     two_ls2 = 2.0 * ls2
     zeros = jnp.zeros_like(sp)
     carry = (zeros,) * 11
+    for copy in piece_copies:
+        copy.wait()
     for block in range(blocks):
         slot = lax.rem(place - block + blocks, blocks)
 
@@ -96,14 +102,15 @@
             t2 = rr * t2 + qs * rough - two_ls2 * offdiag * ratios
             t3 = rr * t3 + nugget
             solved = obs - ratios * solved
-            c0 = c0 + 0.5 * t0 / pivots
-            c1 = c1 + 0.5 * t1 / pivots
-            c2 = c2 + 0.5 * t2 / pivots
-            c3 = c3 + 0.5 * t3 / pivots
+            inv = 1.0 / pivots
+            c0 = c0 + 0.5 * t0 * inv
+            c1 = c1 + 0.5 * t1 * inv
+            c2 = c2 + 0.5 * t2 * inv
+            c3 = c3 + 0.5 * t3 * inv
             logs = logs + jnp.log(pivots)
-            piv_ref[block, pl.ds(t, 1), :] = pivots
+            piv_ref[block, pl.ds(t, 1), :] = inv
             slv_ref[block, pl.ds(t, 1), :] = solved
-            return (1.0 / pivots, t0, t1, t2, t3, solved, c0, c1, c2, c3, logs)
+            return (inv, t0, t1, t2, t3, solved, c0, c1, c2, c3, logs)
 
         carry = lax.fori_loop(0, rows, forward, carry, unroll=8)
     c0, c1, c2, c3, logs = carry[6:]
@@ -120,7 +127,7 @@
             prior = sp * rough
             nugget = ns * weight
             offdiag = mps * coup
-            values = (slv_ref[block, pl.ds(t, 1), :] - following) / piv_ref[block, pl.ds(t, 1), :]
+            values = (slv_ref[block, pl.ds(t, 1), :] - following) * piv_ref[block, pl.ds(t, 1), :]
             q0 = q0 + 2.0 * prior * values * values + 4.0 * values * following
             q1 = q1 + prior * values * values + 2.0 * values * following
             q2 = q2 + qs * rough * values * values + two_ls2 * values * following
@@ -155,7 +162,7 @@
     return pl.pallas_call(
         functools.partial(chain_kernel, aligned=nodes.shape[1] != width),
         out_shape=jax.ShapeDtypeStruct((blocks, rows + 8, width), jnp.float32),
-        in_specs=[smem, smem, vmem, hbm, hbm] + [vmem] * blocks,
+        in_specs=[smem, smem, vmem, hbm, hbm] + [hbm] * blocks,
         out_specs=vmem,
         scratch_shapes=[
             pltpu.VMEM((blocks, rows, width), jnp.float32),
@@ -164,6 +171,7 @@
             pltpu.VMEM((6, width), jnp.float32),
             pltpu.VMEM((4, width), jnp.int32),
             pltpu.SemaphoreType.DMA((2,)),
+            pltpu.SemaphoreType.DMA((blocks,)),
         ],
         interpret=INTERPRET,
     )(place, hyper, window, nodes, offsets, *pieces)

time: 35.3 us -> 35.1 us (level)
  no operation moved by 1% of the time
where the time goes in v7:
time: 35.1 us; the launch traced here: 34.7 us
  blocking collectives  14.5 us (41%)
  starting transfers between devices  8.52 us (24%)
  local copies, waits for them, and re-layouts  3.95 us (11%)
  Pallas kernels  3.63 us (10%)
  other arithmetic  2.66 us (8%)
  waiting for transfers between devices  0.74 us (2%)
  between operations  0.74 us (2%)
    all_to_all x1, blocking collectives, per_device_body(): received = lax.all_to_all(payload, 'tm', 0, 0, tiled=True)  9.12 us
    ppermute x3, starting transfers between devices, per_device_body(): lax.ppermute(pieces[shift], 'tm', [(i, (i + shift) % time_count) for i in...  6.99 us
    all_gather x1, blocking collectives, per_device_body(): stats_full = lax.all_gather(stats_quarter, 'hyp', axis=1, tiled=True)  5.4 us
    pallas_call x1, Pallas kernels, run_chain(): pl.pallas_call(functools.partial(chain_kernel, aligned=nodes.shape[1] !=...  3.63 us
    ppermute x1, starting transfers between devices, with_halo(): got = lax.ppermute(send, axis, [(0, 1), (1, 0)])  1.53 us
    slice x2, local copies, waits for them, and re-layouts, per_device_body(): return (solution_out, stats_full[0], stats_full[1:5])  1.26 us
    another operation x1, other arithmetic, per_device_body(): stacked = jnp.stack([roughness, coupling, obs_weight, observed])  1.26 us
    ppermute x1, waiting for transfers between devices, with_halo(): got = lax.ppermute(send, axis, [(0, 1), (1, 0)])  0.73 us
  transfers between devices with their start and end apart: 4, of which 1 were waited for; matrix products, arithmetic and copies ran while one was open for 6% of the time, Pallas kernels for 0%

profile of v7, /device:TPU:0, one launch (start us, length us, event | category | flops | bytes accessed | tf_op | source)
XLA Modules:
  0.0 34.7 jit_solution(16351256473613875990)
XLA Ops:
  0.7 1.3 %pad_maximum_fusion = f32[4,16,4096]{2,1,0:T(8,128)S(1)} fusion(f32[1,16,4096]{2,1,0:T(8,128)} %bitcast.16, f32[1,16,4096]{2,1,0:T(8,128)} %bitcast.17, f32[1,16,4096]{2,1,0:T(8,128)} %bitcast.18, f32[1,16,4096]{2,1,0:T(8,128)} %bitcast.19), kind=kLoop, calls=%fused_computation | loop fusion | flops 786432 | bytes 2097152 | tf_op jit(solution)/shard_map/stack | solution.py:204
  1.9 0.0 copy-start.6
  1.9 0.0 copy-start
  2.0 0.7 %constant_dynamic-slice_fusion = (f32[4,16,256]{2,1,0:T(8,128)S(1)}, f32[4,16,256]{2,1,0:T(8,128)S(1)}, f32[4,16,256]{2,1,0:T(8,128)S(1)}, f32[4,16,256]{2,1,0:T(8,128)}) fusion(f32[4,16,4096]{2,1,0:T(8,128)S(1)} %pad_maximum_fusion, s32[]{:T(128)S(6)} %select_n.42, s32[]{:T(128)S(6)} %select_n.41, s32[]{:T(128)S(6)} %select_n.40, s32[]{:T(128)S(6)} %select_n.39), kind=kLoop, calls=%fused_computation.4 | loop fusion | bytes 524304 | tf_op jit(solution)/shard_map/dynamic_slice | solution.py:206
  2.6 3.1 %collective-permute-start.1 = (f32[4,16,256]{2,1,0:T(8,128)S(1)}, f32[4,16,256]{2,1,0:T(8,128)S(1)}, u32[]{:S(2)}, u32[]{:S(2)}) collective-permute-start(f32[4,16,256]{2,1,0:T(8,128)S(1)} %get-tuple-element.5), channel_id=1, source_target_pairs={{0,8},{8,16},{16,24},{24,0},{1,9},{9,17},{17,25},{25,1},{2,10},{10... | collective-permute-start | bytes 196616 | tf_op jit(solution)/shard_map/ppermute | solution.py:215
  5.7 2.6 %collective-permute-start.2 = (f32[4,16,256]{2,1,0:T(8,128)S(1)}, f32[4,16,256]{2,1,0:T(8,128)S(1)}, u32[]{:S(2)}, u32[]{:S(2)}) collective-permute-start(f32[4,16,256]{2,1,0:T(8,128)S(1)} %get-tuple-element.4), channel_id=1, source_target_pairs={{0,16},{8,24},{16,0},{24,8},{1,17},{9,25},{17,1},{25,9},{2,18},{10... | collective-permute-start | bytes 196616 | tf_op jit(solution)/shard_map/ppermute | solution.py:215
  8.3 1.3 %collective-permute-start.3 = (f32[4,16,256]{2,1,0:T(8,128)S(1)}, f32[4,16,256]{2,1,0:T(8,128)S(1)}, u32[]{:S(2)}, u32[]{:S(2)}) collective-permute-start(f32[4,16,256]{2,1,0:T(8,128)S(1)} %get-tuple-element.3), channel_id=1, source_target_pairs={{0,24},{8,0},{16,8},{24,16},{1,25},{9,1},{17,9},{25,17},{2,26},{10... | collective-permute-start | bytes 196616 | tf_op jit(solution)/shard_map/ppermute | solution.py:215
  9.6 0.0 copy-done.6
  9.6 0.1 broadcast_select_fusion.1
  9.7 1.5 %collective-permute-start = (f32[64]{0:T(128)S(1)}, f32[64]{0:T(128)S(1)}, u32[]{:S(2)}, u32[]{:S(2)}) collective-permute-start(f32[64]{0:T(128)S(1)} %broadcast_select_fusion.1), channel_id=1, source_target_pairs={{0,4},{4,0},{1,5},{5,1},{2,6},{6,2},{3,7},{7,3},{8,12},{12,8},{9,1... | collective-permute-start | bytes 776 | tf_op jit(solution)/shard_map/ppermute | solution.py:19
  11.2 0.6 %pad_add_fusion.refs_0_ = s32[2]{0:T(128)} fusion(s32[1]{0:T(128)} %bitcast.1, s32[1]{0:T(128)} %bitcast), kind=kLoop, calls=%fused_computation.11 | loop fusion | flops 2 | bytes 16 | tf_op jit(solution)/shard_map/stack | solution.py:222
  11.8 0.0 copy-done
  11.8 0.0 copy-done.4
  11.8 0.0 copy-done.5
  11.9 0.7 %pad_maximum_fusion.1.refs_3_ = f32[6,4096]{1,0:T(8,128)} fusion(f32[4,4096]{1,0:T(4,128)S(1)} %copy-done, f32[1,4096]{1,0:T(1,128)S(1)} %bitcast.22, f32[1,4096]{1,0:T(1,128)S(1)} %bitcast.23), kind=kLoop, calls=%fused_computation.1 | loop fusion | flops 49152 | bytes 196608 | tf_op jit(solution)/shard_map/concatenate | solution.py:224
  12.5 0.7 %collective-permute-done = f32[64]{0:T(128)S(1)} collective-permute-done((f32[64]{0:T(128)S(1)}, f32[64]{0:T(128)S(1)}, u32[]{:S(2)}, u32[]{:S(2)}) %collective-permute-start) | collective-permute-done | bytes 288 | tf_op jit(solution)/shard_map/ppermute | solution.py:19
  13.3 0.1 concatenate.6
  13.4 0.1 dynamic_slice.15
  13.4 0.6 %broadcast_in_dim.9.refs_2_ = f32[1,384]{1,0:T(1,128)} reshape(f32[384]{0:T(512)S(1)} %dynamic_slice.15) | data formatting | bytes 3072 | tf_op jit(solution)/shard_map/broadcast_in_dim | solution.py:223
  14.0 0.0 collective-permute-done.1.refs_6_
  14.0 0.0 collective-permute-done.2.refs_7_
  14.0 0.0 copy-start.2
  14.0 0.0 collective-permute-done.3.refs_8_
  14.1 0.6 %copy-done.1 = f32[4,16,256]{2,1,0:T(8,128)} copy-done((f32[4,16,256]{2,1,0:T(8,128)}, f32[4,16,256]{2,1,0:T(8,128)S(1)}, u32[]{:S(2)}) %copy-start.1) | copy-done | bytes 65560
  14.6 0.0 copy-done.2
  14.7 0.0 copy-done.3
  14.7 3.6 %shard_map.121 = f32[4,24,256]{2,1,0:T(8,128)} custom-call(s32[2]{0:T(128)} %pad_add_fusion.refs_0_, f32[4]{0:T(128)} %refs_1_.1, f32[1,384]{1,0:T(1,128)} %broadcast_in_dim.9.refs_2_, f32[6,4096]{1,0:T(8,128)} %pad_maximum_fusion.1.refs_3_, s32[4,4096]{1,0:T(4,128)} %refs_4_.1, f32[4,16,256]{2,1,0:T(8,128)} %get-tuple-element.6.refs_5_, ...), custom_call_target="tpu_custom_call" | custom-call | tf_op jit(solution)/shard_map/pallas_call | solution.py:162
  18.3 9.1 %all_to_all.5 = f32[4,24,256]{2,1,0:T(8,128)S(1)} all-to-all(f32[4,24,256]{2,1,0:T(8,128)} %shard_map.121), channel_id=1, replica_groups=mesh['tm'=4,'space'=2,'hyp'=4] {'tm'}, dimensions={0} | all-to-all | bytes 196608 | tf_op jit(solution)/shard_map/all_to_all | solution.py:230
  27.4 5.4 %all_gather.3 = f32[5,4096]{1,0:T(8,128)S(1)} all-gather(f32[5,1024]{1,0:T(8,128)S(1)} %bitcast.20), channel_id=1, replica_groups=mesh['tm'=4,'space'=2,'hyp'=4] {'hyp'}, dimensions={1}, use_global_device_ids=true | all-gather | bytes 102400 | tf_op jit(solution)/shard_map/all_gather | solution.py:233
  32.8 0.6 %slice.29 = f32[4,4096]{1,0:T(4,128)} slice(f32[5,4096]{1,0:T(8,128)S(1)} %all_gather.3), slice={[1:5], [0:4096]} | slice | bytes 131072 | tf_op jit(solution)/shard_map/slice | solution.py:234
  33.5 0.6 %slice.28 = f32[1,4096]{1,0:T(1,128)} slice(f32[5,4096]{1,0:T(8,128)S(1)} %all_gather.3), slice={[0:1], [0:4096]} | slice | bytes 32768 | tf_op jit(solution)/shard_map/slice | solution.py:234
  34.1 0.6 %copy.14 = f32[4,2,8,256]{3,2,0,1:T(8,128)} copy(f32[4,2,8,256]{3,2,1,0:T(8,128)S(1)} %slice_bitcast_fusion) | data formatting | bytes 131072 | tf_op jit(solution)/shard_map/reshape | solution.py:231
  (8 shorter events, 0.0 us)
Async XLA Ops:
  1.9 7.7 %copy-start.6 = (f32[4096]{0:T(1024)S(1)}, f32[4096]{0:T(1024)}, u32[]{:S(2)}) copy-start(f32[4096]{0:T(1024)} %param.10) | copy-start | bytes 49156
  1.9 9.9 %copy-start = (f32[4,4096]{1,0:T(4,128)S(1)}, f32[4,4096]{1,0:T(4,128)}, u32[]{:S(2)}) copy-start(f32[4,4096]{1,0:T(4,128)} %param.13) | copy-start | bytes 196612
  2.6 11.4 %collective-permute-start.1 = (f32[4,16,256]{2,1,0:T(8,128)S(1)}, f32[4,16,256]{2,1,0:T(8,128)S(1)}, u32[]{:S(2)}, u32[]{:S(2)}) collective-permute-start(f32[4,16,256]{2,1,0:T(8,128)S(1)} %get-tuple-element.5), channel_id=1, source_target_pairs={{0,8},{8,16},{16,24},{24,0},{1,9},{9,17},{17,25},{25,1},{2,10},{10... | collective-permute-start | bytes 196616 | tf_op jit(solution)/shard_map/ppermute | solution.py:215
  5.7 8.3 %collective-permute-start.2 = (f32[4,16,256]{2,1,0:T(8,128)S(1)}, f32[4,16,256]{2,1,0:T(8,128)S(1)}, u32[]{:S(2)}, u32[]{:S(2)}) collective-permute-start(f32[4,16,256]{2,1,0:T(8,128)S(1)} %get-tuple-element.4), channel_id=1, source_target_pairs={{0,16},{8,24},{16,0},{24,8},{1,17},{9,25},{17,1},{25,9},{2,18},{10... | collective-permute-start | bytes 196616 | tf_op jit(solution)/shard_map/ppermute | solution.py:215
  8.3 5.8 %collective-permute-start.3 = (f32[4,16,256]{2,1,0:T(8,128)S(1)}, f32[4,16,256]{2,1,0:T(8,128)S(1)}, u32[]{:S(2)}, u32[]{:S(2)}) collective-permute-start(f32[4,16,256]{2,1,0:T(8,128)S(1)} %get-tuple-element.3), channel_id=1, source_target_pairs={{0,24},{8,0},{16,8},{24,16},{1,25},{9,1},{17,9},{25,17},{2,26},{10... | collective-permute-start | bytes 196616 | tf_op jit(solution)/shard_map/ppermute | solution.py:215
  9.6 2.2 %copy-start.4 = (f32[4096]{0:T(1024)S(1)}, f32[4096]{0:T(1024)}, u32[]{:S(2)}) copy-start(f32[4096]{0:T(1024)} %param.12) | copy-start | bytes 49156
  9.6 2.2 %copy-start.5 = (f32[4096]{0:T(1024)S(1)}, f32[4096]{0:T(1024)}, u32[]{:S(2)}) copy-start(f32[4096]{0:T(1024)} %param.11) | copy-start | bytes 49156
  9.7 3.6 %collective-permute-start = (f32[64]{0:T(128)S(1)}, f32[64]{0:T(128)S(1)}, u32[]{:S(2)}, u32[]{:S(2)}) collective-permute-start(f32[64]{0:T(128)S(1)} %broadcast_select_fusion.1), channel_id=1, source_target_pairs={{0,4},{4,0},{1,5},{5,1},{2,6},{6,2},{3,7},{7,3},{8,12},{12,8},{9,1... | collective-permute-start | bytes 776 | tf_op jit(solution)/shard_map/ppermute | solution.py:19
  14.0 0.6 %copy-start.1 = (f32[4,16,256]{2,1,0:T(8,128)}, f32[4,16,256]{2,1,0:T(8,128)S(1)}, u32[]{:S(2)}) copy-start(f32[4,16,256]{2,1,0:T(8,128)S(1)} %collective-permute-done.1.refs_6_) | copy-start | bytes 196612
  14.0 0.6 %copy-start.2 = (f32[4,16,256]{2,1,0:T(8,128)}, f32[4,16,256]{2,1,0:T(8,128)S(1)}, u32[]{:S(2)}) copy-start(f32[4,16,256]{2,1,0:T(8,128)S(1)} %collective-permute-done.2.refs_7_) | copy-start | bytes 196612
  14.0 0.6 %copy-start.3 = (f32[4,16,256]{2,1,0:T(8,128)}, f32[4,16,256]{2,1,0:T(8,128)S(1)}, u32[]{:S(2)}) copy-start(f32[4,16,256]{2,1,0:T(8,128)S(1)} %collective-permute-done.3.refs_8_) | copy-start | bytes 196612

commit v8 on v7

--- a/solution.py
+++ b/solution.py
@@ -29,9 +29,10 @@
 
 def chain_kernel(*refs, aligned):
     place_ref, hyper_ref, window_ref, nodes_hbm, offsets_hbm = refs[:5]
-    blocks = len(refs) - 13
+    blocks = (len(refs) - 13) // 2
     pieces = refs[5 : 5 + blocks]
-    out_ref, piv_ref, slv_ref, data_ref, nodes_ref, offsets_ref, sems, piece_sems = refs[5 + blocks :]
+    outs = refs[5 + blocks : 5 + 2 * blocks]
+    out_ref, piv_ref, slv_ref, data_ref, nodes_ref, offsets_ref, sems, piece_sems = refs[5 + 2 * blocks :]
     _, _, rows, width = data_ref.shape
     first = pl.multiple_of(place_ref[1], 128) if aligned else 0
     node_copy = pltpu.make_async_copy(nodes_hbm.at[:, pl.ds(first, width)], nodes_ref, sems.at[0])
@@ -151,6 +152,8 @@
     )
     for block in range(blocks):
         out_ref[block, rows : rows + 8, :] = stats
+    for shift in range(blocks):
+        outs[shift][...] = out_ref[lax.rem(place + shift, blocks)]
 
 
 def run_chain(place, hyper, window, nodes, offsets, pieces):
@@ -161,10 +164,11 @@
     hbm = pl.BlockSpec(memory_space=pl.ANY)
     return pl.pallas_call(
         functools.partial(chain_kernel, aligned=nodes.shape[1] != width),
-        out_shape=jax.ShapeDtypeStruct((blocks, rows + 8, width), jnp.float32),
+        out_shape=[jax.ShapeDtypeStruct((rows + 8, width), jnp.float32)] * blocks,
         in_specs=[smem, smem, vmem, hbm, hbm] + [hbm] * blocks,
-        out_specs=vmem,
+        out_specs=[vmem] * blocks,
         scratch_shapes=[
+            pltpu.VMEM((blocks, rows + 8, width), jnp.float32),
             pltpu.VMEM((blocks, rows, width), jnp.float32),
             pltpu.VMEM((blocks, rows, width), jnp.float32),
             pltpu.VMEM((blocks, 4, rows, width), jnp.float32),
@@ -175,6 +179,53 @@
         ],
         interpret=INTERPRET,
     )(place, hyper, window, nodes, offsets, *pieces)
+
+
+def place_kernel(place_ref, *refs):
+    blocks = len(refs) - 3
+    pieces = refs[:blocks]
+    sol_ref, stat_ref, sems = refs[blocks:]
+    rows = sol_ref.shape[0]
+    width = pieces[0].shape[1]
+    place = place_ref[0]
+    copies = []
+    for shift in range(blocks):
+        column = pl.multiple_of(lax.rem(place - shift + blocks, blocks) * width, 128)
+        copies.append(
+            pltpu.make_async_copy(
+                pieces[shift].at[0:rows, :], sol_ref.at[:, pl.ds(column, width)], sems.at[0, shift]
+            )
+        )
+        copies.append(
+            pltpu.make_async_copy(
+                pieces[shift].at[rows : rows + 8, :],
+                stat_ref.at[:, pl.ds(column, width)],
+                sems.at[1, shift],
+            )
+        )
+    for copy in copies:
+        copy.start()
+    for copy in copies:
+        copy.wait()
+
+
+def run_place(place, pieces):
+    blocks = len(pieces)
+    rows = pieces[0].shape[0] - 8
+    width = pieces[0].shape[1]
+    hbm = pl.BlockSpec(memory_space=pl.ANY)
+    smem = pl.BlockSpec(memory_space=pltpu.SMEM)
+    return pl.pallas_call(
+        place_kernel,
+        out_shape=(
+            jax.ShapeDtypeStruct((rows, blocks * width), jnp.float32),
+            jax.ShapeDtypeStruct((8, blocks * width), jnp.float32),
+        ),
+        in_specs=[smem] + [hbm] * blocks,
+        out_specs=(hbm, hbm),
+        scratch_shapes=[pltpu.SemaphoreType.DMA((2, blocks))],
+        interpret=INTERPRET,
+    )(place, *pieces)
 
 
 def per_device_body(
@@ -227,9 +278,25 @@
         nodes = lax.dynamic_slice_in_dim(nodes, first, chunk, axis=1)
         near_off = lax.dynamic_slice_in_dim(offsets, first, chunk, axis=1)
     payload = run_chain(place, hyper_params, window, nodes, near_off, arrived)
-    received = lax.all_to_all(payload, "tm", 0, 0, tiled=True)
-    solution_out = received[:, :row_count].transpose(1, 0, 2).reshape(row_count, quarter)
-    stats_quarter = received[:, row_count : row_count + 5].transpose(1, 0, 2).reshape(5, quarter)
+    returned = [payload[0]] + [
+        lax.ppermute(
+            payload[shift],
+            "tm",
+            [(i, (i + shift) % time_count) for i in range(time_count)],
+        )
+        for shift in range(1, time_count)
+    ]
+    if chunk % 128 == 0:
+        solution_out, stats_out = run_place(place, returned)
+        stats_quarter = stats_out[:5]
+    else:
+        ordered = jnp.take(
+            jnp.stack(returned),
+            lax.rem(time_place - jnp.arange(time_count) + time_count, time_count),
+            axis=0,
+        )
+        solution_out = ordered[:, :row_count].transpose(1, 0, 2).reshape(row_count, quarter)
+        stats_quarter = ordered[:, row_count : row_count + 5].transpose(1, 0, 2).reshape(5, quarter)
     stats_full = lax.all_gather(stats_quarter, "hyp", axis=1, tiled=True)
     return (solution_out, stats_full[0], stats_full[1:5])
 

time: 35.1 us -> 37.5 us (1.068)
  blocking collectives: 14.5 us -> 5.63 us
  Pallas kernels: 3.63 us -> 8.44 us
  starting transfers between devices: 8.52 us -> 12.4 us
  waiting for transfers between devices: 0.74 us -> 3.45 us
    all_to_all x1 -> x0, blocking collectives: 9.12 us -> none  [per_device_body(): received = lax.all_to_all(payload, 'tm', 0, 0, tiled=True)]
    pallas_call x0 -> x1, Pallas kernels: none -> 4.82 us  [run_place(): pl.pallas_call(place_kernel, out_shape=(jax.ShapeDtypeStruct((rows, block...]
    ppermute x0 -> x3, starting transfers between devices: none -> 3.88 us  [per_device_body(): lax.ppermute(payload[shift], 'tm', [(i, (i + shift) % time_count) for i i...]
    ppermute x0 -> x3, waiting for transfers between devices: none -> 2.69 us  [per_device_body(): lax.ppermute(payload[shift], 'tm', [(i, (i + shift) % time_count) for i i...]
    reshape x1 -> x0, local copies, waits for them, and re-layouts: 0.64 us -> none  [per_device_body(): received[:, :row_count].transpose(1, 0, 2).reshape(row_count, quarter)]
    unnamed x15 -> x20, local copies, waits for them, and re-layouts: 0.66 us -> 1.29 us
  transfers between devices with their start and end apart: 4 -> 7, of which waited for: 1 -> 3; matrix products, arithmetic and copies ran while one was open for 6% -> 6% of each run, Pallas kernels for 0% -> 0%
where the time goes in v8:
time: 37.5 us; the launch traced here: 37.2 us
  starting transfers between devices  12.4 us (33%)
  Pallas kernels  8.44 us (23%)
  blocking collectives  5.63 us (15%)
  local copies, waits for them, and re-layouts  3.94 us (11%)
  waiting for transfers between devices  3.45 us (9%)
  other arithmetic  2.63 us (7%)
  between operations  0.76 us (2%)
    ppermute x3, starting transfers between devices, per_device_body(): lax.ppermute(pieces[shift], 'tm', [(i, (i + shift) % time_count) for i in...  6.99 us
    all_gather x1, blocking collectives, per_device_body(): stats_full = lax.all_gather(stats_quarter, 'hyp', axis=1, tiled=True)  5.63 us
    pallas_call x1, Pallas kernels, run_place(): pl.pallas_call(place_kernel, out_shape=(jax.ShapeDtypeStruct((rows, block...  4.82 us
    ppermute x3, starting transfers between devices, per_device_body(): lax.ppermute(payload[shift], 'tm', [(i, (i + shift) % time_count) for i i...  3.88 us
    pallas_call x1, Pallas kernels, run_chain(): pl.pallas_call(functools.partial(chain_kernel, aligned=nodes.shape[1] !=...  3.62 us
    ppermute x3, waiting for transfers between devices, per_device_body(): lax.ppermute(payload[shift], 'tm', [(i, (i + shift) % time_count) for i i...  2.69 us
    ppermute x1, starting transfers between devices, with_halo(): got = lax.ppermute(send, axis, [(0, 1), (1, 0)])  1.53 us
    unnamed x20, local copies, waits for them, and re-layouts  1.29 us
  transfers between devices with their start and end apart: 7, of which 3 were waited for; matrix products, arithmetic and copies ran while one was open for 6% of the time, Pallas kernels for 0%

profile of v8, /device:TPU:0, one launch (start us, length us, event | category | flops | bytes accessed | tf_op | source)
XLA Modules:
  0.0 37.2 jit_solution(14284288036896312800)
XLA Ops:
  0.7 1.3 %pad_maximum_fusion = f32[4,16,4096]{2,1,0:T(8,128)S(1)} fusion(f32[1,16,4096]{2,1,0:T(8,128)} %bitcast.10, f32[1,16,4096]{2,1,0:T(8,128)} %bitcast.11, f32[1,16,4096]{2,1,0:T(8,128)} %bitcast.12, f32[1,16,4096]{2,1,0:T(8,128)} %bitcast.13), kind=kLoop, calls=%fused_computation | loop fusion | flops 786432 | bytes 2097152 | tf_op jit(solution)/shard_map/stack | solution.py:255
  1.9 0.0 copy-start.9
  1.9 0.0 copy-start
  2.0 0.7 %constant_dynamic-slice_fusion = (f32[4,16,256]{2,1,0:T(8,128)S(1)}, f32[4,16,256]{2,1,0:T(8,128)S(1)}, f32[4,16,256]{2,1,0:T(8,128)S(1)}, f32[4,16,256]{2,1,0:T(8,128)}) fusion(f32[4,16,4096]{2,1,0:T(8,128)S(1)} %pad_maximum_fusion, s32[]{:T(128)S(6)} %select_n.42, s32[]{:T(128)S(6)} %select_n.41, s32[]{:T(128)S(6)} %select_n.40, s32[]{:T(128)S(6)} %select_n.39), kind=kLoop, calls=%fused_computation.3 | loop fusion | bytes 524304 | tf_op jit(solution)/shard_map/dynamic_slice | solution.py:257
  2.6 3.1 %collective-permute-start.1 = (f32[4,16,256]{2,1,0:T(8,128)S(1)}, f32[4,16,256]{2,1,0:T(8,128)S(1)}, u32[]{:S(2)}, u32[]{:S(2)}) collective-permute-start(f32[4,16,256]{2,1,0:T(8,128)S(1)} %get-tuple-element.17), channel_id=1, source_target_pairs={{0,8},{8,16},{16,24},{24,0},{1,9},{9,17},{17,25},{25,1},{2,10},{10... | collective-permute-start | bytes 196616 | tf_op jit(solution)/shard_map/ppermute | solution.py:266
  5.7 2.6 %collective-permute-start.2 = (f32[4,16,256]{2,1,0:T(8,128)S(1)}, f32[4,16,256]{2,1,0:T(8,128)S(1)}, u32[]{:S(2)}, u32[]{:S(2)}) collective-permute-start(f32[4,16,256]{2,1,0:T(8,128)S(1)} %get-tuple-element.16), channel_id=1, source_target_pairs={{0,16},{8,24},{16,0},{24,8},{1,17},{9,25},{17,1},{25,9},{2,18},{10... | collective-permute-start | bytes 196616 | tf_op jit(solution)/shard_map/ppermute | solution.py:266
  8.3 1.3 %collective-permute-start.3 = (f32[4,16,256]{2,1,0:T(8,128)S(1)}, f32[4,16,256]{2,1,0:T(8,128)S(1)}, u32[]{:S(2)}, u32[]{:S(2)}) collective-permute-start(f32[4,16,256]{2,1,0:T(8,128)S(1)} %get-tuple-element.15), channel_id=1, source_target_pairs={{0,24},{8,0},{16,8},{24,16},{1,25},{9,1},{17,9},{25,17},{2,26},{10... | collective-permute-start | bytes 196616 | tf_op jit(solution)/shard_map/ppermute | solution.py:266
  9.6 0.1 broadcast_select_fusion.1
  9.7 1.5 %collective-permute-start = (f32[64]{0:T(128)S(1)}, f32[64]{0:T(128)S(1)}, u32[]{:S(2)}, u32[]{:S(2)}) collective-permute-start(f32[64]{0:T(128)S(1)} %broadcast_select_fusion.1), channel_id=1, source_target_pairs={{0,4},{4,0},{1,5},{5,1},{2,6},{6,2},{3,7},{7,3},{8,12},{12,8},{9,1... | collective-permute-start | bytes 776 | tf_op jit(solution)/shard_map/ppermute | solution.py:19
  11.2 0.6 %pad_add_fusion.refs_0_.place_ref = s32[2]{0:T(128)} fusion(s32[1]{0:T(128)} %bitcast.1, s32[1]{0:T(128)} %bitcast), kind=kLoop, calls=%fused_computation.10 | loop fusion | flops 2 | bytes 16 | tf_op jit(solution)/shard_map/stack | solution.py:273
  11.8 0.7 %pad_maximum_fusion.1.refs_3_ = f32[6,4096]{1,0:T(8,128)} fusion(f32[4,4096]{1,0:T(4,128)S(1)} %copy-done, f32[1,4096]{1,0:T(1,128)S(1)} %bitcast.15, f32[1,4096]{1,0:T(1,128)S(1)} %bitcast.16), kind=kLoop, calls=%fused_computation.1 | loop fusion | flops 49152 | bytes 196608 | tf_op jit(solution)/shard_map/concatenate | solution.py:275
  12.5 0.8 %collective-permute-done = f32[64]{0:T(128)S(1)} collective-permute-done((f32[64]{0:T(128)S(1)}, f32[64]{0:T(128)S(1)}, u32[]{:S(2)}, u32[]{:S(2)}) %collective-permute-start) | collective-permute-done | bytes 288 | tf_op jit(solution)/shard_map/ppermute | solution.py:19
  13.3 0.1 concatenate.6
  13.4 0.1 dynamic_slice.15
  13.4 0.6 %broadcast_in_dim.9.refs_2_ = f32[1,384]{1,0:T(1,128)} reshape(f32[384]{0:T(512)S(1)} %dynamic_slice.15) | data formatting | bytes 3072 | tf_op jit(solution)/shard_map/broadcast_in_dim | solution.py:274
  14.0 0.0 collective-permute-done.1.refs_6_
  14.0 0.0 collective-permute-done.2.refs_7_
  14.1 0.6 %copy-done.1 = f32[4,16,256]{2,1,0:T(8,128)} copy-done((f32[4,16,256]{2,1,0:T(8,128)}, f32[4,16,256]{2,1,0:T(8,128)S(1)}, u32[]{:S(2)}) %copy-start.1) | copy-done | bytes 65560
  14.6 0.0 copy-done.2
  14.7 0.0 copy-done.3
  14.7 3.6 %shard_map.121 = (f32[24,256]{1,0:T(8,128)}, f32[24,256]{1,0:T(8,128)}, f32[24,256]{1,0:T(8,128)}, f32[24,256]{1,0:T(8,128)}) custom-call(s32[2]{0:T(128)} %pad_add_fusion.refs_0_.place_ref, f32[4]{0:T(128)} %refs_1_.1, f32[1,384]{1,0:T(1,128)} %broadcast_in_dim.9.refs_2_, f32[6,4096]{1,0:T(8,128)} %pad_maximum_fusion.1.refs_3_, s32[4,4096]{1,0:T(4,128)} %refs_4_.1, ...), custom_call_target="tpu_custom_call" | custom-call | tf_op jit(solution)/shard_map/pallas_call | solution.py:165
  18.3 0.7 %collective-permute-start.4 = (f32[24,256]{1,0:T(8,128)}, f32[24,256]{1,0:T(8,128)S(1)}, u32[]{:S(2)}, u32[]{:S(2)}) collective-permute-start(f32[24,256]{1,0:T(8,128)} %get-tuple-element.10), channel_id=1, source_target_pairs={{0,8},{8,16},{16,24},{24,0},{1,9},{9,17},{17,25},{25,1},{2,10},{10... | collective-permute-start | bytes 73736 | tf_op jit(solution)/shard_map/ppermute | solution.py:282
  19.0 1.8 %collective-permute-start.5 = (f32[24,256]{1,0:T(8,128)}, f32[24,256]{1,0:T(8,128)S(1)}, u32[]{:S(2)}, u32[]{:S(2)}) collective-permute-start(f32[24,256]{1,0:T(8,128)} %get-tuple-element.11), channel_id=1, source_target_pairs={{0,16},{8,24},{16,0},{24,8},{1,17},{9,25},{17,1},{25,9},{2,18},{10... | collective-permute-start | bytes 73736 | tf_op jit(solution)/shard_map/ppermute | solution.py:282
  20.9 1.3 %collective-permute-start.6 = (f32[24,256]{1,0:T(8,128)}, f32[24,256]{1,0:T(8,128)S(1)}, u32[]{:S(2)}, u32[]{:S(2)}) collective-permute-start(f32[24,256]{1,0:T(8,128)} %get-tuple-element.12), channel_id=1, source_target_pairs={{0,24},{8,0},{16,8},{24,16},{1,25},{9,1},{17,9},{25,17},{2,26},{10... | collective-permute-start | bytes 73736 | tf_op jit(solution)/shard_map/ppermute | solution.py:282
  22.2 2.0 %collective-permute-done.4.refs_1_ = f32[24,256]{1,0:T(8,128)S(1)} collective-permute-done((f32[24,256]{1,0:T(8,128)}, f32[24,256]{1,0:T(8,128)S(1)}, u32[]{:S(2)}, u32[]{:S(2)}) %collective-permute-start.4) | collective-permute-done | bytes 24608 | tf_op jit(solution)/shard_map/ppermute | solution.py:282
  24.3 0.0 collective-permute-done.5.refs_2_
  24.3 0.6 %collective-permute-done.6.refs_3_ = f32[24,256]{1,0:T(8,128)S(1)} collective-permute-done((f32[24,256]{1,0:T(8,128)}, f32[24,256]{1,0:T(8,128)S(1)}, u32[]{:S(2)}, u32[]{:S(2)}) %collective-permute-start.6) | collective-permute-done | bytes 24608 | tf_op jit(solution)/shard_map/ppermute | solution.py:282
  24.9 0.6 %copy-done.6 = f32[24,256]{1,0:T(8,128)} copy-done((f32[24,256]{1,0:T(8,128)}, f32[24,256]{1,0:T(8,128)S(1)}, u32[]{:S(2)}) %copy-start.6) | copy-done | bytes 24600
  25.5 4.8 %shard_map.122 = (f32[16,1024]{1,0:T(8,128)}, f32[8,1024]{1,0:T(8,128)}) custom-call(s32[2]{0:T(128)} %pad_add_fusion.refs_0_.place_ref, f32[24,256]{1,0:T(8,128)} %get-tuple-element.9.refs_0_, f32[24,256]{1,0:T(8,128)} %copy-done.4, f32[24,256]{1,0:T(8,128)} %copy-done.5, f32[24,256]{1,0:T(8,128)} %copy-done.6), custom_call_target="tpu_custom_call" | custom-call | tf_op jit(solution)/shard_map/pallas_call | solution.py:218
  30.3 5.6 %all_gather.3 = f32[5,4096]{1,0:T(8,128)S(1)} all-gather(f32[5,1024]{1,0:T(8,128)} %bitcast.14), channel_id=1, replica_groups=mesh['tm'=4,'space'=2,'hyp'=4] {'hyp'}, dimensions={1}, use_global_device_ids=true | all-gather | bytes 102400 | tf_op jit(solution)/shard_map/all_gather | solution.py:300
  36.0 0.6 %slice.23 = f32[4,4096]{1,0:T(4,128)} slice(f32[5,4096]{1,0:T(8,128)S(1)} %all_gather.3), slice={[1:5], [0:4096]} | slice | bytes 131072 | tf_op jit(solution)/shard_map/slice | solution.py:301
  36.6 0.6 %slice.22 = f32[1,4096]{1,0:T(1,128)} slice(f32[5,4096]{1,0:T(8,128)S(1)} %all_gather.3), slice={[0:1], [0:4096]} | slice | bytes 32768 | tf_op jit(solution)/shard_map/slice | solution.py:301
  (17 shorter events, 0.0 us)
Async XLA Ops:
  1.9 7.7 %copy-start.9 = (f32[4096]{0:T(1024)S(1)}, f32[4096]{0:T(1024)}, u32[]{:S(2)}) copy-start(f32[4096]{0:T(1024)} %param.10) | copy-start | bytes 49156
  1.9 9.9 %copy-start = (f32[4,4096]{1,0:T(4,128)S(1)}, f32[4,4096]{1,0:T(4,128)}, u32[]{:S(2)}) copy-start(f32[4,4096]{1,0:T(4,128)} %param.13) | copy-start | bytes 196612
  2.6 11.4 %collective-permute-start.1 = (f32[4,16,256]{2,1,0:T(8,128)S(1)}, f32[4,16,256]{2,1,0:T(8,128)S(1)}, u32[]{:S(2)}, u32[]{:S(2)}) collective-permute-start(f32[4,16,256]{2,1,0:T(8,128)S(1)} %get-tuple-element.17), channel_id=1, source_target_pairs={{0,8},{8,16},{16,24},{24,0},{1,9},{9,17},{17,25},{25,1},{2,10},{10... | collective-permute-start | bytes 196616 | tf_op jit(solution)/shard_map/ppermute | solution.py:266
  5.7 8.3 %collective-permute-start.2 = (f32[4,16,256]{2,1,0:T(8,128)S(1)}, f32[4,16,256]{2,1,0:T(8,128)S(1)}, u32[]{:S(2)}, u32[]{:S(2)}) collective-permute-start(f32[4,16,256]{2,1,0:T(8,128)S(1)} %get-tuple-element.16), channel_id=1, source_target_pairs={{0,16},{8,24},{16,0},{24,8},{1,17},{9,25},{17,1},{25,9},{2,18},{10... | collective-permute-start | bytes 196616 | tf_op jit(solution)/shard_map/ppermute | solution.py:266
  8.3 5.8 %collective-permute-start.3 = (f32[4,16,256]{2,1,0:T(8,128)S(1)}, f32[4,16,256]{2,1,0:T(8,128)S(1)}, u32[]{:S(2)}, u32[]{:S(2)}) collective-permute-start(f32[4,16,256]{2,1,0:T(8,128)S(1)} %get-tuple-element.15), channel_id=1, source_target_pairs={{0,24},{8,0},{16,8},{24,16},{1,25},{9,1},{17,9},{25,17},{2,26},{10... | collective-permute-start | bytes 196616 | tf_op jit(solution)/shard_map/ppermute | solution.py:266
  9.6 2.2 %copy-start.7 = (f32[4096]{0:T(1024)S(1)}, f32[4096]{0:T(1024)}, u32[]{:S(2)}) copy-start(f32[4096]{0:T(1024)} %param.12) | copy-start | bytes 49156
  9.6 2.2 %copy-start.8 = (f32[4096]{0:T(1024)S(1)}, f32[4096]{0:T(1024)}, u32[]{:S(2)}) copy-start(f32[4096]{0:T(1024)} %param.11) | copy-start | bytes 49156
  9.7 3.6 %collective-permute-start = (f32[64]{0:T(128)S(1)}, f32[64]{0:T(128)S(1)}, u32[]{:S(2)}, u32[]{:S(2)}) collective-permute-start(f32[64]{0:T(128)S(1)} %broadcast_select_fusion.1), channel_id=1, source_target_pairs={{0,4},{4,0},{1,5},{5,1},{2,6},{6,2},{3,7},{7,3},{8,12},{12,8},{9,1... | collective-permute-start | bytes 776 | tf_op jit(solution)/shard_map/ppermute | solution.py:19
  14.0 0.6 %copy-start.1 = (f32[4,16,256]{2,1,0:T(8,128)}, f32[4,16,256]{2,1,0:T(8,128)S(1)}, u32[]{:S(2)}) copy-start(f32[4,16,256]{2,1,0:T(8,128)S(1)} %collective-permute-done.1.refs_6_) | copy-start | bytes 196612
  14.0 0.6 %copy-start.2 = (f32[4,16,256]{2,1,0:T(8,128)}, f32[4,16,256]{2,1,0:T(8,128)S(1)}, u32[]{:S(2)}) copy-start(f32[4,16,256]{2,1,0:T(8,128)S(1)} %collective-permute-done.2.refs_7_) | copy-start | bytes 196612
  14.0 0.7 %copy-start.3 = (f32[4,16,256]{2,1,0:T(8,128)}, f32[4,16,256]{2,1,0:T(8,128)S(1)}, u32[]{:S(2)}) copy-start(f32[4,16,256]{2,1,0:T(8,128)S(1)} %collective-permute-done.3.refs_8_) | copy-start | bytes 196612
  18.3 5.9 %collective-permute-start.4 = (f32[24,256]{1,0:T(8,128)}, f32[24,256]{1,0:T(8,128)S(1)}, u32[]{:S(2)}, u32[]{:S(2)}) collective-permute-start(f32[24,256]{1,0:T(8,128)} %get-tuple-element.10), channel_id=1, source_target_pairs={{0,8},{8,16},{16,24},{24,0},{1,9},{9,17},{17,25},{25,1},{2,10},{10... | collective-permute-start | bytes 73736 | tf_op jit(solution)/shard_map/ppermute | solution.py:282
  19.0 5.2 %collective-permute-start.5 = (f32[24,256]{1,0:T(8,128)}, f32[24,256]{1,0:T(8,128)S(1)}, u32[]{:S(2)}, u32[]{:S(2)}) collective-permute-start(f32[24,256]{1,0:T(8,128)} %get-tuple-element.11), channel_id=1, source_target_pairs={{0,16},{8,24},{16,0},{24,8},{1,17},{9,25},{17,1},{25,9},{2,18},{10... | collective-permute-start | bytes 73736 | tf_op jit(solution)/shard_map/ppermute | solution.py:282
  20.9 4.0 %collective-permute-start.6 = (f32[24,256]{1,0:T(8,128)}, f32[24,256]{1,0:T(8,128)S(1)}, u32[]{:S(2)}, u32[]{:S(2)}) collective-permute-start(f32[24,256]{1,0:T(8,128)} %get-tuple-element.12), channel_id=1, source_target_pairs={{0,24},{8,0},{16,8},{24,16},{1,25},{9,1},{17,9},{25,17},{2,26},{10... | collective-permute-start | bytes 73736 | tf_op jit(solution)/shard_map/ppermute | solution.py:282
  24.2 0.6 %copy-start.4 = (f32[24,256]{1,0:T(8,128)}, f32[24,256]{1,0:T(8,128)S(1)}, u32[]{:S(2)}) copy-start(f32[24,256]{1,0:T(8,128)S(1)} %collective-permute-done.4.refs_1_) | copy-start | bytes 73732
  24.3 0.6 %copy-start.5 = (f32[24,256]{1,0:T(8,128)}, f32[24,256]{1,0:T(8,128)S(1)}, u32[]{:S(2)}) copy-start(f32[24,256]{1,0:T(8,128)S(1)} %collective-permute-done.5.refs_2_) | copy-start | bytes 73732
  24.9 0.6 %copy-start.6 = (f32[24,256]{1,0:T(8,128)}, f32[24,256]{1,0:T(8,128)S(1)}, u32[]{:S(2)}) copy-start(f32[24,256]{1,0:T(8,128)S(1)} %collective-permute-done.6.refs_3_) | copy-start | bytes 73732

commit v9 on v8

--- a/solution.py
+++ b/solution.py
@@ -161,7 +161,7 @@
     _, rows, width = pieces[0].shape
     vmem = pl.BlockSpec(memory_space=pltpu.VMEM)
     smem = pl.BlockSpec(memory_space=pltpu.SMEM)
-    hbm = pl.BlockSpec(memory_space=pl.ANY)
+    hbm = pl.BlockSpec(memory_space=pltpu.HBM)
     return pl.pallas_call(
         functools.partial(chain_kernel, aligned=nodes.shape[1] != width),
         out_shape=[jax.ShapeDtypeStruct((rows + 8, width), jnp.float32)] * blocks,
@@ -182,48 +182,48 @@
 
 
 def place_kernel(place_ref, *refs):
-    blocks = len(refs) - 3
+    blocks = len(refs) - 4
     pieces = refs[:blocks]
-    sol_ref, stat_ref, sems = refs[blocks:]
+    sol_ref, stat_ref, arrived_ref, sems = refs[blocks:]
     rows = sol_ref.shape[0]
     width = pieces[0].shape[1]
     place = place_ref[0]
-    copies = []
+    copies = [
+        pltpu.make_async_copy(pieces[shift], arrived_ref.at[shift - 1], sems.at[shift - 1])
+        for shift in range(1, blocks)
+    ]
+    for copy in copies:
+        copy.start()
     for shift in range(blocks):
         column = pl.multiple_of(lax.rem(place - shift + blocks, blocks) * width, 128)
-        copies.append(
-            pltpu.make_async_copy(
-                pieces[shift].at[0:rows, :], sol_ref.at[:, pl.ds(column, width)], sems.at[0, shift]
-            )
-        )
-        copies.append(
-            pltpu.make_async_copy(
-                pieces[shift].at[rows : rows + 8, :],
-                stat_ref.at[:, pl.ds(column, width)],
-                sems.at[1, shift],
-            )
-        )
-    for copy in copies:
-        copy.start()
-    for copy in copies:
-        copy.wait()
+        if shift == 0:
+            piece = pieces[0][...]
+        else:
+            copies[shift - 1].wait()
+            piece = arrived_ref[shift - 1]
+        sol_ref[:, pl.ds(column, width)] = piece[0:rows, :]
+        stat_ref[:, pl.ds(column, width)] = piece[rows : rows + 8, :]
 
 
 def run_place(place, pieces):
     blocks = len(pieces)
     rows = pieces[0].shape[0] - 8
     width = pieces[0].shape[1]
-    hbm = pl.BlockSpec(memory_space=pl.ANY)
+    vmem = pl.BlockSpec(memory_space=pltpu.VMEM)
     smem = pl.BlockSpec(memory_space=pltpu.SMEM)
+    hbm = pl.BlockSpec(memory_space=pltpu.HBM)
     return pl.pallas_call(
         place_kernel,
         out_shape=(
             jax.ShapeDtypeStruct((rows, blocks * width), jnp.float32),
             jax.ShapeDtypeStruct((8, blocks * width), jnp.float32),
         ),
-        in_specs=[smem] + [hbm] * blocks,
-        out_specs=(hbm, hbm),
-        scratch_shapes=[pltpu.SemaphoreType.DMA((2, blocks))],
+        in_specs=[smem, vmem] + [hbm] * (blocks - 1),
+        out_specs=(vmem, vmem),
+        scratch_shapes=[
+            pltpu.VMEM((blocks - 1, rows + 8, width), jnp.float32),
+            pltpu.SemaphoreType.DMA((blocks - 1,)),
+        ],
         interpret=INTERPRET,
     )(place, *pieces)
 
@@ -252,16 +252,17 @@
     kappa_sq = jnp.exp(2.0 * log_kappa)
     padded = with_halo(kappa_sq, "space", BAND)
 
-    stacked = jnp.stack([roughness, coupling, obs_weight, observed])
-    pieces = [
-        lax.dynamic_slice_in_dim(
-            stacked,
-            hyp_place * quarter + lax.rem(time_place + shift, time_count) * chunk,
-            chunk,
-            axis=2,
+    pieces = []
+    for shift in range(time_count):
+        start = hyp_place * quarter + lax.rem(time_place + shift, time_count) * chunk
+        pieces.append(
+            jnp.stack(
+                [
+                    lax.dynamic_slice_in_dim(rows, start, chunk, axis=1)
+                    for rows in (roughness, coupling, obs_weight, observed)
+                ]
+            )
         )
-        for shift in range(time_count)
-    ]
     arrived = [pieces[0]] + [
         lax.ppermute(
             pieces[shift],

time: 37.5 us -> 37.9 us (1.011)
  Pallas kernels: 8.44 us -> 5.8 us
  local copies, waits for them, and re-layouts: 3.94 us -> 5.58 us
  starting transfers between devices: 12.4 us -> 13.9 us
    pallas_call x1, Pallas kernels: 4.82 us -> 2.18 us  [run_place(): pl.pallas_call(place_kernel, out_shape=(jax.ShapeDtypeStruct((rows, block...]
    another operation x0 -> x2, local copies, waits for them, and re-layouts: none -> 1.71 us  [per_device_body(): jnp.stack([lax.dynamic_slice_in_dim(rows, start, chunk, axis=1) for rows...]
    ppermute x1, starting transfers between devices: 1.53 us -> 3 us  [with_halo(): got = lax.ppermute(send, axis, [(0, 1), (1, 0)])]
    ppermute x1, waiting for transfers between devices: 0.75 us -> 0.01 us  [with_halo(): got = lax.ppermute(send, axis, [(0, 1), (1, 0)])]
    exp x1, other arithmetic: 0.01 us -> 0.73 us  [per_device_body(): kappa_sq = jnp.exp(2.0 * log_kappa)]
    dynamic_slice x1 -> x0, local copies, waits for them, and re-layouts: 0.66 us -> none  [per_device_body(): lax.dynamic_slice_in_dim(stacked, hyp_place * quarter + lax.rem(time_plac...]
    another operation x1 -> x4, other arithmetic: 1.26 us -> 0.65 us  [per_device_body(): jnp.stack([lax.dynamic_slice_in_dim(rows, start, chunk, axis=1) for rows...]
    unnamed x20 -> x18, local copies, waits for them, and re-layouts: 1.29 us -> 1.88 us
  transfers between devices with their start and end apart: 7 -> 7, of which waited for: 3 -> 2; matrix products, arithmetic and copies ran while one was open for 6% -> 12% of each run, Pallas kernels for 0% -> 0%
where the time goes in v9:
time: 37.9 us; the launch traced here: 37.4 us
  starting transfers between devices  13.9 us (37%)
  Pallas kernels  5.8 us (15%)
  blocking collectives  5.63 us (15%)
  local copies, waits for them, and re-layouts  5.58 us (15%)
  waiting for transfers between devices  3.09 us (8%)
  other arithmetic  2.74 us (7%)
  between operations  0.71 us (2%)
    ppermute x3, starting transfers between devices, per_device_body(): lax.ppermute(pieces[shift], 'tm', [(i, (i + shift) % time_count) for i in...  6.53 us
    all_gather x1, blocking collectives, per_device_body(): stats_full = lax.all_gather(stats_quarter, 'hyp', axis=1, tiled=True)  5.63 us
    ppermute x3, starting transfers between devices, per_device_body(): lax.ppermute(payload[shift], 'tm', [(i, (i + shift) % time_count) for i i...  4.34 us
    pallas_call x1, Pallas kernels, run_chain(): pl.pallas_call(functools.partial(chain_kernel, aligned=nodes.shape[1] !=...  3.62 us
    ppermute x3, waiting for transfers between devices, per_device_body(): lax.ppermute(payload[shift], 'tm', [(i, (i + shift) % time_count) for i i...  3.05 us
    ppermute x1, starting transfers between devices, with_halo(): got = lax.ppermute(send, axis, [(0, 1), (1, 0)])  3 us
    pallas_call x1, Pallas kernels, run_place(): pl.pallas_call(place_kernel, out_shape=(jax.ShapeDtypeStruct((rows, block...  2.18 us
    unnamed x18, local copies, waits for them, and re-layouts  1.88 us
  transfers between devices with their start and end apart: 7, of which 2 were waited for; matrix products, arithmetic and copies ran while one was open for 12% of the time, Pallas kernels for 0%

profile of v9, /device:TPU:0, one launch (start us, length us, event | category | flops | bytes accessed | tf_op | source)
XLA Modules:
  0.0 37.4 jit_solution(3582727990718406454)
XLA Ops:
  0.6 0.7 %multiply_exponential_fusion = f32[4096]{0:T(1024)S(1)} fusion(f32[4096]{0:T(1024)} %param.10), kind=kLoop, calls=%fused_computation.21 | loop fusion | flops 4096 | bytes 32768 | tf_op jit(solution)/shard_map/exp | solution.py:252
  1.4 0.1 broadcast_select_fusion.1
  1.4 3.0 %collective-permute-start = (f32[64]{0:T(128)S(1)}, f32[64]{0:T(128)S(1)}, u32[]{:S(2)}, u32[]{:S(2)}) collective-permute-start(f32[64]{0:T(128)S(1)} %broadcast_select_fusion.1), channel_id=1, source_target_pairs={{0,4},{4,0},{1,5},{5,1},{2,6},{6,2},{3,7},{7,3},{8,12},{12,8},{9,1... | collective-permute-start | bytes 776 | tf_op jit(solution)/shard_map/ppermute | solution.py:19
  4.4 0.8 %dynamic-slice_bitcast_fusion.2 = (f32[1,16,256]{2,1,0:T(8,128)S(1)}, f32[1,16,256]{2,1,0:T(8,128)S(1)}, f32[1,16,256]{2,1,0:T(8,128)S(1)}, f32[1,16,256]{2,1,0:...) fusion(f32[16,4096]{1,0:T(8,128)} %param.16, ...), kind=kLoop, calls=%fused_computation.7 | loop fusion | bytes 262160 | tf_op jit(solution)/shard_map/stack | solution.py:259
  5.3 0.9 %dynamic-slice_bitcast_fusion = (f32[1,16,256]{2,1,0:T(8,128)S(1)}, f32[1,16,256]{2,1,0:T(8,128)S(1)}, f32[1,16,256]{2,1,0:T(8,128)S(1)}, f32[1,16,256]{2,1,0:T(...) fusion(f32[16,4096]{1,0:T(8,128)} %param.18, ...), kind=kLoop, calls=%fused_computation.5 | loop fusion | bytes 262160 | tf_op jit(solution)/shard_map/stack | solution.py:259
  6.2 2.7 %collective-permute-start.2 = (f32[4,16,256]{2,1,0:T(8,128)S(1)}, f32[4,16,256]{2,1,0:T(8,128)S(1)}, u32[]{:S(2)}, u32[]{:S(2)}) collective-permute-start(f32[4,16,256]{2,1,0:T(8,128)S(1)} %pad_maximum_fusion.3), channel_id=1, source_target_pairs={{0,16},{8,24},{16,0},{24,8},{1,17},{9,25},{17,1},{25,9},{2,18},{10... | collective-permute-start | bytes 196616 | tf_op jit(solution)/shard_map/ppermute | solution.py:267
  8.8 1.6 %collective-permute-start.1 = (f32[4,16,256]{2,1,0:T(8,128)S(1)}, f32[4,16,256]{2,1,0:T(8,128)S(1)}, u32[]{:S(2)}, u32[]{:S(2)}) collective-permute-start(f32[4,16,256]{2,1,0:T(8,128)S(1)} %pad_maximum_fusion.2), channel_id=1, source_target_pairs={{0,8},{8,16},{16,24},{24,0},{1,9},{9,17},{17,25},{25,1},{2,10},{10... | collective-permute-start | bytes 196616 | tf_op jit(solution)/shard_map/ppermute | solution.py:267
  10.4 2.3 %collective-permute-start.3 = (f32[4,16,256]{2,1,0:T(8,128)S(1)}, f32[4,16,256]{2,1,0:T(8,128)S(1)}, u32[]{:S(2)}, u32[]{:S(2)}) collective-permute-start(f32[4,16,256]{2,1,0:T(8,128)S(1)} %pad_maximum_fusion.4), channel_id=1, source_target_pairs={{0,24},{8,0},{16,8},{24,16},{1,25},{9,1},{17,9},{25,17},{2,26},{10... | collective-permute-start | bytes 196616 | tf_op jit(solution)/shard_map/ppermute | solution.py:267
  12.7 0.6 %pad_add_fusion.refs_0_.place_ref = s32[2]{0:T(128)} fusion(s32[1]{0:T(128)} %bitcast.1, s32[1]{0:T(128)} %bitcast), kind=kLoop, calls=%fused_computation.25 | loop fusion | flops 2 | bytes 16 | tf_op jit(solution)/shard_map/stack | solution.py:274
  13.3 0.7 %pad_maximum_fusion.refs_3_ = f32[6,4096]{1,0:T(8,128)} fusion(f32[4,4096]{1,0:T(4,128)S(1)} %copy-done, f32[1,4096]{1,0:T(1,128)S(1)} %bitcast.39, f32[1,4096]{1,0:T(1,128)S(1)} %bitcast.40), kind=kLoop, calls=%fused_computation | loop fusion | flops 49152 | bytes 196608 | tf_op jit(solution)/shard_map/concatenate | solution.py:276
  14.0 0.6 %pad_maximum_fusion.1.refs_5_ = f32[4,16,256]{2,1,0:T(8,128)} fusion(f32[1,16,256]{2,1,0:T(8,128)S(1)} %get-tuple-element.29, f32[1,16,256]{2,1,0:T(8,128)S(1)} %get-tuple-element.34, f32[1,16,256]{2,1,0:T(8,128)S(1)} %get-tuple-element.21, f32[1,16,256]{2,1,0:T(8,128)S(1)} %get-tuple-element.38), kind=kLoop, calls=%fused_computation.1 | loop fusion | flops 49152 | bytes 131072 | tf_op jit(solution)/shard_map/stack | solution.py:259
  14.7 0.1 concatenate.6
  14.7 0.1 dynamic_slice.51
  14.8 0.6 %broadcast_in_dim.9.refs_2_ = f32[1,384]{1,0:T(1,128)} reshape(f32[384]{0:T(512)S(1)} %dynamic_slice.51) | data formatting | bytes 3072 | tf_op jit(solution)/shard_map/broadcast_in_dim | solution.py:275
  15.4 0.0 collective-permute-done.2.refs_7_
  15.4 0.0 collective-permute-done.1.refs_6_
  15.4 0.0 copy-start.2
  15.4 0.0 collective-permute-done.3.refs_8_
  15.4 0.6 %copy-done.1 = f32[4,16,256]{2,1,0:T(8,128)} copy-done((f32[4,16,256]{2,1,0:T(8,128)}, f32[4,16,256]{2,1,0:T(8,128)S(1)}, u32[]{:S(2)}) %copy-start.1) | copy-done | bytes 65560
  16.0 0.0 copy-done.2
  16.0 0.6 %copy-done.3 = f32[4,16,256]{2,1,0:T(8,128)} copy-done((f32[4,16,256]{2,1,0:T(8,128)}, f32[4,16,256]{2,1,0:T(8,128)S(1)}, u32[]{:S(2)}) %copy-start.3) | copy-done | bytes 65560
  16.7 3.6 %shard_map.121 = (f32[24,256]{1,0:T(8,128)}, f32[24,256]{1,0:T(8,128)}, f32[24,256]{1,0:T(8,128)}, f32[24,256]{1,0:T(8,128)}) custom-call(s32[2]{0:T(128)} %pad_add_fusion.refs_0_.place_ref, f32[4]{0:T(128)} %refs_1_.1, f32[1,384]{1,0:T(1,128)} %broadcast_in_dim.9.refs_2_, f32[6,4096]{1,0:T(8,128)} %pad_maximum_fusion.refs_3_, s32[4,4096]{1,0:T(4,128)} %refs_4_.1, ...), custom_call_target="tpu_custom_call" | custom-call | tf_op jit(solution)/shard_map/pallas_call | solution.py:165
  20.3 0.1 collective-permute-start.4
  20.4 3.3 %collective-permute-start.5 = (f32[24,256]{1,0:T(8,128)}, f32[24,256]{1,0:T(8,128)S(1)}, u32[]{:S(2)}, u32[]{:S(2)}) collective-permute-start(f32[24,256]{1,0:T(8,128)} %get-tuple-element.11), channel_id=1, source_target_pairs={{0,16},{8,24},{16,0},{24,8},{1,17},{9,25},{17,1},{25,9},{2,18},{10... | collective-permute-start | bytes 73736 | tf_op jit(solution)/shard_map/ppermute | solution.py:283
  23.7 1.0 %collective-permute-start.6 = (f32[24,256]{1,0:T(8,128)}, f32[24,256]{1,0:T(8,128)S(1)}, u32[]{:S(2)}, u32[]{:S(2)}) collective-permute-start(f32[24,256]{1,0:T(8,128)} %get-tuple-element.12), channel_id=1, source_target_pairs={{0,24},{8,0},{16,8},{24,16},{1,25},{9,1},{17,9},{25,17},{2,26},{10... | collective-permute-start | bytes 73736 | tf_op jit(solution)/shard_map/ppermute | solution.py:283
  24.7 1.5 %collective-permute-done.4.refs_1_ = f32[24,256]{1,0:T(8,128)S(1)} collective-permute-done((f32[24,256]{1,0:T(8,128)}, f32[24,256]{1,0:T(8,128)S(1)}, u32[]{:S(2)}, u32[]{:S(2)}) %collective-permute-start.4) | collective-permute-done | bytes 24608 | tf_op jit(solution)/shard_map/ppermute | solution.py:283
  26.2 1.5 %collective-permute-done.6.refs_3_ = f32[24,256]{1,0:T(8,128)S(1)} collective-permute-done((f32[24,256]{1,0:T(8,128)}, f32[24,256]{1,0:T(8,128)S(1)}, u32[]{:S(2)}, u32[]{:S(2)}) %collective-permute-start.6) | collective-permute-done | bytes 24608 | tf_op jit(solution)/shard_map/ppermute | solution.py:283
  27.7 0.6 %copy-done.6 = f32[24,256]{1,0:T(8,128)} copy-done((f32[24,256]{1,0:T(8,128)}, f32[24,256]{1,0:T(8,128)S(1)}, u32[]{:S(2)}) %copy-start.6) | copy-done | bytes 24600
  28.3 2.2 %shard_map.122 = (f32[16,1024]{1,0:T(8,128)}, f32[8,1024]{1,0:T(8,128)}) custom-call(s32[2]{0:T(128)} %pad_add_fusion.refs_0_.place_ref, f32[24,256]{1,0:T(8,128)} %get-tuple-element.9.refs_0_, f32[24,256]{1,0:T(8,128)} %copy-done.4, f32[24,256]{1,0:T(8,128)} %copy-done.5, f32[24,256]{1,0:T(8,128)} %copy-done.6), custom_call_target="tpu_custom_call" | custom-call | tf_op jit(solution)/shard_map/pallas_call | solution.py:215
  30.5 5.6 %all_gather.3 = f32[5,4096]{1,0:T(8,128)S(1)} all-gather(f32[5,1024]{1,0:T(8,128)} %bitcast.38), channel_id=1, replica_groups=mesh['tm'=4,'space'=2,'hyp'=4] {'hyp'}, dimensions={1}, use_global_device_ids=true | all-gather | bytes 102400 | tf_op jit(solution)/shard_map/all_gather | solution.py:301
  36.2 0.6 %slice.22 = f32[1,4096]{1,0:T(1,128)} slice(f32[5,4096]{1,0:T(8,128)S(1)} %all_gather.3), slice={[0:1], [0:4096]} | slice | bytes 32768 | tf_op jit(solution)/shard_map/slice | solution.py:302
  36.8 0.6 %slice.23 = f32[4,4096]{1,0:T(4,128)} slice(f32[5,4096]{1,0:T(8,128)S(1)} %all_gather.3), slice={[1:5], [0:4096]} | slice | bytes 131072 | tf_op jit(solution)/shard_map/slice | solution.py:302
  (19 shorter events, 0.1 us)
Async XLA Ops:
  1.4 13.2 %collective-permute-start = (f32[64]{0:T(128)S(1)}, f32[64]{0:T(128)S(1)}, u32[]{:S(2)}, u32[]{:S(2)}) collective-permute-start(f32[64]{0:T(128)S(1)} %broadcast_select_fusion.1), channel_id=1, source_target_pairs={{0,4},{4,0},{1,5},{5,1},{2,6},{6,2},{3,7},{7,3},{8,12},{12,8},{9,1... | collective-permute-start | bytes 776 | tf_op jit(solution)/shard_map/ppermute | solution.py:19
  6.2 9.2 %collective-permute-start.2 = (f32[4,16,256]{2,1,0:T(8,128)S(1)}, f32[4,16,256]{2,1,0:T(8,128)S(1)}, u32[]{:S(2)}, u32[]{:S(2)}) collective-permute-start(f32[4,16,256]{2,1,0:T(8,128)S(1)} %pad_maximum_fusion.3), channel_id=1, source_target_pairs={{0,16},{8,24},{16,0},{24,8},{1,17},{9,25},{17,1},{25,9},{2,18},{10... | collective-permute-start | bytes 196616 | tf_op jit(solution)/shard_map/ppermute | solution.py:267
  8.8 6.6 %collective-permute-start.1 = (f32[4,16,256]{2,1,0:T(8,128)S(1)}, f32[4,16,256]{2,1,0:T(8,128)S(1)}, u32[]{:S(2)}, u32[]{:S(2)}) collective-permute-start(f32[4,16,256]{2,1,0:T(8,128)S(1)} %pad_maximum_fusion.2), channel_id=1, source_target_pairs={{0,8},{8,16},{16,24},{24,0},{1,9},{9,17},{17,25},{25,1},{2,10},{10... | collective-permute-start | bytes 196616 | tf_op jit(solution)/shard_map/ppermute | solution.py:267
  10.4 2.9 %copy-start = (f32[4,4096]{1,0:T(4,128)S(1)}, f32[4,4096]{1,0:T(4,128)}, u32[]{:S(2)}) copy-start(f32[4,4096]{1,0:T(4,128)} %param.13) | copy-start | bytes 196612
  10.4 2.9 %copy-start.7 = (f32[4096]{0:T(1024)S(1)}, f32[4096]{0:T(1024)}, u32[]{:S(2)}) copy-start(f32[4096]{0:T(1024)} %param.12) | copy-start | bytes 49156
  10.4 2.9 %copy-start.8 = (f32[4096]{0:T(1024)S(1)}, f32[4096]{0:T(1024)}, u32[]{:S(2)}) copy-start(f32[4096]{0:T(1024)} %param.11) | copy-start | bytes 49156
  10.4 5.0 %collective-permute-start.3 = (f32[4,16,256]{2,1,0:T(8,128)S(1)}, f32[4,16,256]{2,1,0:T(8,128)S(1)}, u32[]{:S(2)}, u32[]{:S(2)}) collective-permute-start(f32[4,16,256]{2,1,0:T(8,128)S(1)} %pad_maximum_fusion.4), channel_id=1, source_target_pairs={{0,24},{8,0},{16,8},{24,16},{1,25},{9,1},{17,9},{25,17},{2,26},{10... | collective-permute-start | bytes 196616 | tf_op jit(solution)/shard_map/ppermute | solution.py:267
  15.4 0.6 %copy-start.1 = (f32[4,16,256]{2,1,0:T(8,128)}, f32[4,16,256]{2,1,0:T(8,128)S(1)}, u32[]{:S(2)}) copy-start(f32[4,16,256]{2,1,0:T(8,128)S(1)} %collective-permute-done.2.refs_7_) | copy-start | bytes 196612
  15.4 0.6 %copy-start.2 = (f32[4,16,256]{2,1,0:T(8,128)}, f32[4,16,256]{2,1,0:T(8,128)S(1)}, u32[]{:S(2)}) copy-start(f32[4,16,256]{2,1,0:T(8,128)S(1)} %collective-permute-done.1.refs_6_) | copy-start | bytes 196612
  16.0 0.6 %copy-start.3 = (f32[4,16,256]{2,1,0:T(8,128)}, f32[4,16,256]{2,1,0:T(8,128)S(1)}, u32[]{:S(2)}) copy-start(f32[4,16,256]{2,1,0:T(8,128)S(1)} %collective-permute-done.3.refs_8_) | copy-start | bytes 196612
  20.3 5.9 %collective-permute-start.4 = (f32[24,256]{1,0:T(8,128)}, f32[24,256]{1,0:T(8,128)S(1)}, u32[]{:S(2)}, u32[]{:S(2)}) collective-permute-start(f32[24,256]{1,0:T(8,128)} %get-tuple-element.10), channel_id=1, source_target_pairs={{0,8},{8,16},{16,24},{24,0},{1,9},{9,17},{17,25},{25,1},{2,10},{10... | collective-permute-start | bytes 73736 | tf_op jit(solution)/shard_map/ppermute | solution.py:283
  20.4 5.8 %collective-permute-start.5 = (f32[24,256]{1,0:T(8,128)}, f32[24,256]{1,0:T(8,128)S(1)}, u32[]{:S(2)}, u32[]{:S(2)}) collective-permute-start(f32[24,256]{1,0:T(8,128)} %get-tuple-element.11), channel_id=1, source_target_pairs={{0,16},{8,24},{16,0},{24,8},{1,17},{9,25},{17,1},{25,9},{2,18},{10... | collective-permute-start | bytes 73736 | tf_op jit(solution)/shard_map/ppermute | solution.py:283
  23.7 4.0 %collective-permute-start.6 = (f32[24,256]{1,0:T(8,128)}, f32[24,256]{1,0:T(8,128)S(1)}, u32[]{:S(2)}, u32[]{:S(2)}) collective-permute-start(f32[24,256]{1,0:T(8,128)} %get-tuple-element.12), channel_id=1, source_target_pairs={{0,24},{8,0},{16,8},{24,16},{1,25},{9,1},{17,9},{25,17},{2,26},{10... | collective-permute-start | bytes 73736 | tf_op jit(solution)/shard_map/ppermute | solution.py:283
  26.2 1.5 %copy-start.4 = (f32[24,256]{1,0:T(8,128)}, f32[24,256]{1,0:T(8,128)S(1)}, u32[]{:S(2)}) copy-start(f32[24,256]{1,0:T(8,128)S(1)} %collective-permute-done.4.refs_1_) | copy-start | bytes 73732
  26.2 1.5 %copy-start.5 = (f32[24,256]{1,0:T(8,128)}, f32[24,256]{1,0:T(8,128)S(1)}, u32[]{:S(2)}) copy-start(f32[24,256]{1,0:T(8,128)S(1)} %collective-permute-done.5.refs_2_) | copy-start | bytes 73732
  27.7 0.6 %copy-start.6 = (f32[24,256]{1,0:T(8,128)}, f32[24,256]{1,0:T(8,128)S(1)}, u32[]{:S(2)}) copy-start(f32[24,256]{1,0:T(8,128)S(1)} %collective-permute-done.6.refs_3_) | copy-start | bytes 73732

commit v10 on v8

--- a/solution.py
+++ b/solution.py
@@ -113,7 +113,7 @@
             slv_ref[block, pl.ds(t, 1), :] = solved
             return (inv, t0, t1, t2, t3, solved, c0, c1, c2, c3, logs)
 
-        carry = lax.fori_loop(0, rows, forward, carry, unroll=8)
+        carry = lax.fori_loop(0, rows, forward, carry, unroll=True)
     c0, c1, c2, c3, logs = carry[6:]
     closing = (zeros,) * 5
     for block in reversed(range(blocks)):
@@ -136,7 +136,7 @@
             out_ref[block, pl.ds(t, 1), :] = values
             return (offdiag * values, q0, q1, q2, q3)
 
-        closing = lax.fori_loop(0, rows, backward, closing, unroll=8)
+        closing = lax.fori_loop(0, rows, backward, closing, unroll=True)
     q0, q1, q2, q3 = closing[1:]
     scale = 1.0 / (rows * blocks)
     stats = jnp.concatenate(
@@ -182,38 +182,23 @@
 
 
 def place_kernel(place_ref, *refs):
-    blocks = len(refs) - 3
+    blocks = len(refs) - 2
     pieces = refs[:blocks]
-    sol_ref, stat_ref, sems = refs[blocks:]
+    sol_ref, stat_ref = refs[blocks:]
     rows = sol_ref.shape[0]
     width = pieces[0].shape[1]
     place = place_ref[0]
-    copies = []
     for shift in range(blocks):
         column = pl.multiple_of(lax.rem(place - shift + blocks, blocks) * width, 128)
-        copies.append(
-            pltpu.make_async_copy(
-                pieces[shift].at[0:rows, :], sol_ref.at[:, pl.ds(column, width)], sems.at[0, shift]
-            )
-        )
-        copies.append(
-            pltpu.make_async_copy(
-                pieces[shift].at[rows : rows + 8, :],
-                stat_ref.at[:, pl.ds(column, width)],
-                sems.at[1, shift],
-            )
-        )
-    for copy in copies:
-        copy.start()
-    for copy in copies:
-        copy.wait()
+        sol_ref[:, pl.ds(column, width)] = pieces[shift][0:rows, :]
+        stat_ref[:, pl.ds(column, width)] = pieces[shift][rows : rows + 8, :]
 
 
 def run_place(place, pieces):
     blocks = len(pieces)
     rows = pieces[0].shape[0] - 8
     width = pieces[0].shape[1]
-    hbm = pl.BlockSpec(memory_space=pl.ANY)
+    vmem = pl.BlockSpec(memory_space=pltpu.VMEM)
     smem = pl.BlockSpec(memory_space=pltpu.SMEM)
     return pl.pallas_call(
         place_kernel,
@@ -221,9 +206,8 @@
             jax.ShapeDtypeStruct((rows, blocks * width), jnp.float32),
             jax.ShapeDtypeStruct((8, blocks * width), jnp.float32),
         ),
-        in_specs=[smem] + [hbm] * blocks,
-        out_specs=(hbm, hbm),
-        scratch_shapes=[pltpu.SemaphoreType.DMA((2, blocks))],
+        in_specs=[smem] + [vmem] * blocks,
+        out_specs=(vmem, vmem),
         interpret=INTERPRET,
     )(place, *pieces)
 

time: 37.5 us -> 34 us (0.907)
  Pallas kernels: 8.44 us -> 4.99 us
    pallas_call x1, Pallas kernels: 4.82 us -> 1.46 us  [run_place(): pl.pallas_call(place_kernel, out_shape=(jax.ShapeDtypeStruct((rows, block...]
where the time goes in v10:
time: 34 us; the launch traced here: 33.8 us
  starting transfers between devices  12.4 us (36%)
  blocking collectives  5.61 us (16%)
  Pallas kernels  4.99 us (15%)
  local copies, waits for them, and re-layouts  3.94 us (12%)
  waiting for transfers between devices  3.45 us (10%)
  other arithmetic  2.63 us (8%)
  between operations  0.75 us (2%)
    ppermute x3, starting transfers between devices, per_device_body(): lax.ppermute(pieces[shift], 'tm', [(i, (i + shift) % time_count) for i in...  6.99 us
    all_gather x1, blocking collectives, per_device_body(): stats_full = lax.all_gather(stats_quarter, 'hyp', axis=1, tiled=True)  5.61 us
    ppermute x3, starting transfers between devices, per_device_body(): lax.ppermute(payload[shift], 'tm', [(i, (i + shift) % time_count) for i i...  3.88 us
    pallas_call x1, Pallas kernels, run_chain(): pl.pallas_call(functools.partial(chain_kernel, aligned=nodes.shape[1] !=...  3.53 us
    ppermute x3, waiting for transfers between devices, per_device_body(): lax.ppermute(payload[shift], 'tm', [(i, (i + shift) % time_count) for i i...  2.69 us
    ppermute x1, starting transfers between devices, with_halo(): got = lax.ppermute(send, axis, [(0, 1), (1, 0)])  1.53 us
    pallas_call x1, Pallas kernels, run_place(): pl.pallas_call(place_kernel, out_shape=(jax.ShapeDtypeStruct((rows, block...  1.46 us
    unnamed x20, local copies, waits for them, and re-layouts  1.29 us
  transfers between devices with their start and end apart: 7, of which 3 were waited for; matrix products, arithmetic and copies ran while one was open for 6% of the time, Pallas kernels for 0%

profile of v10, /device:TPU:0, one launch (start us, length us, event | category | flops | bytes accessed | tf_op | source)
XLA Modules:
  0.0 33.8 jit_solution(2472730631387476584)
XLA Ops:
  0.7 1.3 %pad_maximum_fusion = f32[4,16,4096]{2,1,0:T(8,128)S(1)} fusion(f32[1,16,4096]{2,1,0:T(8,128)} %bitcast.10, f32[1,16,4096]{2,1,0:T(8,128)} %bitcast.11, f32[1,16,4096]{2,1,0:T(8,128)} %bitcast.12, f32[1,16,4096]{2,1,0:T(8,128)} %bitcast.13), kind=kLoop, calls=%fused_computation | loop fusion | flops 786432 | bytes 2097152 | tf_op jit(solution)/shard_map/stack | solution.py:239
  1.9 0.0 copy-start.9
  1.9 0.0 copy-start
  2.0 0.7 %constant_dynamic-slice_fusion = (f32[4,16,256]{2,1,0:T(8,128)S(1)}, f32[4,16,256]{2,1,0:T(8,128)S(1)}, f32[4,16,256]{2,1,0:T(8,128)S(1)}, f32[4,16,256]{2,1,0:T(8,128)}) fusion(f32[4,16,4096]{2,1,0:T(8,128)S(1)} %pad_maximum_fusion, s32[]{:T(128)S(6)} %select_n.42, s32[]{:T(128)S(6)} %select_n.41, s32[]{:T(128)S(6)} %select_n.40, s32[]{:T(128)S(6)} %select_n.39), kind=kLoop, calls=%fused_computation.3 | loop fusion | bytes 524304 | tf_op jit(solution)/shard_map/dynamic_slice | solution.py:241
  2.6 3.1 %collective-permute-start.1 = (f32[4,16,256]{2,1,0:T(8,128)S(1)}, f32[4,16,256]{2,1,0:T(8,128)S(1)}, u32[]{:S(2)}, u32[]{:S(2)}) collective-permute-start(f32[4,16,256]{2,1,0:T(8,128)S(1)} %get-tuple-element.17), channel_id=1, source_target_pairs={{0,8},{8,16},{16,24},{24,0},{1,9},{9,17},{17,25},{25,1},{2,10},{10... | collective-permute-start | bytes 196616 | tf_op jit(solution)/shard_map/ppermute | solution.py:250
  5.7 2.6 %collective-permute-start.2 = (f32[4,16,256]{2,1,0:T(8,128)S(1)}, f32[4,16,256]{2,1,0:T(8,128)S(1)}, u32[]{:S(2)}, u32[]{:S(2)}) collective-permute-start(f32[4,16,256]{2,1,0:T(8,128)S(1)} %get-tuple-element.16), channel_id=1, source_target_pairs={{0,16},{8,24},{16,0},{24,8},{1,17},{9,25},{17,1},{25,9},{2,18},{10... | collective-permute-start | bytes 196616 | tf_op jit(solution)/shard_map/ppermute | solution.py:250
  8.3 1.3 %collective-permute-start.3 = (f32[4,16,256]{2,1,0:T(8,128)S(1)}, f32[4,16,256]{2,1,0:T(8,128)S(1)}, u32[]{:S(2)}, u32[]{:S(2)}) collective-permute-start(f32[4,16,256]{2,1,0:T(8,128)S(1)} %get-tuple-element.15), channel_id=1, source_target_pairs={{0,24},{8,0},{16,8},{24,16},{1,25},{9,1},{17,9},{25,17},{2,26},{10... | collective-permute-start | bytes 196616 | tf_op jit(solution)/shard_map/ppermute | solution.py:250
  9.6 0.1 broadcast_select_fusion.1
  9.7 1.5 %collective-permute-start = (f32[64]{0:T(128)S(1)}, f32[64]{0:T(128)S(1)}, u32[]{:S(2)}, u32[]{:S(2)}) collective-permute-start(f32[64]{0:T(128)S(1)} %broadcast_select_fusion.1), channel_id=1, source_target_pairs={{0,4},{4,0},{1,5},{5,1},{2,6},{6,2},{3,7},{7,3},{8,12},{12,8},{9,1... | collective-permute-start | bytes 776 | tf_op jit(solution)/shard_map/ppermute | solution.py:19
  11.2 0.6 %pad_add_fusion.refs_0_.place_ref = s32[2]{0:T(128)} fusion(s32[1]{0:T(128)} %bitcast.1, s32[1]{0:T(128)} %bitcast), kind=kLoop, calls=%fused_computation.10 | loop fusion | flops 2 | bytes 16 | tf_op jit(solution)/shard_map/stack | solution.py:257
  11.8 0.7 %pad_maximum_fusion.1.refs_3_ = f32[6,4096]{1,0:T(8,128)} fusion(f32[4,4096]{1,0:T(4,128)S(1)} %copy-done, f32[1,4096]{1,0:T(1,128)S(1)} %bitcast.15, f32[1,4096]{1,0:T(1,128)S(1)} %bitcast.16), kind=kLoop, calls=%fused_computation.1 | loop fusion | flops 49152 | bytes 196608 | tf_op jit(solution)/shard_map/concatenate | solution.py:259
  12.5 0.8 %collective-permute-done = f32[64]{0:T(128)S(1)} collective-permute-done((f32[64]{0:T(128)S(1)}, f32[64]{0:T(128)S(1)}, u32[]{:S(2)}, u32[]{:S(2)}) %collective-permute-start) | collective-permute-done | bytes 288 | tf_op jit(solution)/shard_map/ppermute | solution.py:19
  13.3 0.1 concatenate.6
  13.4 0.1 dynamic_slice.15
  13.4 0.6 %broadcast_in_dim.9.refs_2_ = f32[1,384]{1,0:T(1,128)} reshape(f32[384]{0:T(512)S(1)} %dynamic_slice.15) | data formatting | bytes 3072 | tf_op jit(solution)/shard_map/broadcast_in_dim | solution.py:258
  14.0 0.0 collective-permute-done.1.refs_6_
  14.0 0.0 collective-permute-done.2.refs_7_
  14.1 0.6 %copy-done.1 = f32[4,16,256]{2,1,0:T(8,128)} copy-done((f32[4,16,256]{2,1,0:T(8,128)}, f32[4,16,256]{2,1,0:T(8,128)S(1)}, u32[]{:S(2)}) %copy-start.1) | copy-done | bytes 65560
  14.6 0.0 copy-done.2
  14.7 0.0 copy-done.3
  14.7 3.5 %shard_map.121 = (f32[24,256]{1,0:T(8,128)}, f32[24,256]{1,0:T(8,128)}, f32[24,256]{1,0:T(8,128)}, f32[24,256]{1,0:T(8,128)}) custom-call(s32[2]{0:T(128)} %pad_add_fusion.refs_0_.place_ref, f32[4]{0:T(128)} %refs_1_.1, f32[1,384]{1,0:T(1,128)} %broadcast_in_dim.9.refs_2_, f32[6,4096]{1,0:T(8,128)} %pad_maximum_fusion.1.refs_3_, s32[4,4096]{1,0:T(4,128)} %refs_4_.1, ...), custom_call_target="tpu_custom_call" | custom-call | tf_op jit(solution)/shard_map/pallas_call | solution.py:165
  18.2 0.7 %collective-permute-start.4 = (f32[24,256]{1,0:T(8,128)}, f32[24,256]{1,0:T(8,128)S(1)}, u32[]{:S(2)}, u32[]{:S(2)}) collective-permute-start(f32[24,256]{1,0:T(8,128)} %get-tuple-element.10), channel_id=1, source_target_pairs={{0,8},{8,16},{16,24},{24,0},{1,9},{9,17},{17,25},{25,1},{2,10},{10... | collective-permute-start | bytes 73736 | tf_op jit(solution)/shard_map/ppermute | solution.py:266
  19.0 1.8 %collective-permute-start.5 = (f32[24,256]{1,0:T(8,128)}, f32[24,256]{1,0:T(8,128)S(1)}, u32[]{:S(2)}, u32[]{:S(2)}) collective-permute-start(f32[24,256]{1,0:T(8,128)} %get-tuple-element.11), channel_id=1, source_target_pairs={{0,16},{8,24},{16,0},{24,8},{1,17},{9,25},{17,1},{25,9},{2,18},{10... | collective-permute-start | bytes 73736 | tf_op jit(solution)/shard_map/ppermute | solution.py:266
  20.8 1.3 %collective-permute-start.6 = (f32[24,256]{1,0:T(8,128)}, f32[24,256]{1,0:T(8,128)S(1)}, u32[]{:S(2)}, u32[]{:S(2)}) collective-permute-start(f32[24,256]{1,0:T(8,128)} %get-tuple-element.12), channel_id=1, source_target_pairs={{0,24},{8,0},{16,8},{24,16},{1,25},{9,1},{17,9},{25,17},{2,26},{10... | collective-permute-start | bytes 73736 | tf_op jit(solution)/shard_map/ppermute | solution.py:266
  22.1 2.0 %collective-permute-done.4.refs_1_ = f32[24,256]{1,0:T(8,128)S(1)} collective-permute-done((f32[24,256]{1,0:T(8,128)}, f32[24,256]{1,0:T(8,128)S(1)}, u32[]{:S(2)}, u32[]{:S(2)}) %collective-permute-start.4) | collective-permute-done | bytes 24608 | tf_op jit(solution)/shard_map/ppermute | solution.py:266
  24.2 0.0 collective-permute-done.5.refs_2_
  24.2 0.6 %collective-permute-done.6.refs_3_ = f32[24,256]{1,0:T(8,128)S(1)} collective-permute-done((f32[24,256]{1,0:T(8,128)}, f32[24,256]{1,0:T(8,128)S(1)}, u32[]{:S(2)}, u32[]{:S(2)}) %collective-permute-start.6) | collective-permute-done | bytes 24608 | tf_op jit(solution)/shard_map/ppermute | solution.py:266
  24.8 0.6 %copy-done.6 = f32[24,256]{1,0:T(8,128)} copy-done((f32[24,256]{1,0:T(8,128)}, f32[24,256]{1,0:T(8,128)S(1)}, u32[]{:S(2)}) %copy-start.6) | copy-done | bytes 24600
  25.4 1.5 %shard_map.122 = (f32[16,1024]{1,0:T(8,128)}, f32[8,1024]{1,0:T(8,128)}) custom-call(s32[2]{0:T(128)} %pad_add_fusion.refs_0_.place_ref, f32[24,256]{1,0:T(8,128)} %get-tuple-element.9.refs_0_, f32[24,256]{1,0:T(8,128)} %copy-done.4, f32[24,256]{1,0:T(8,128)} %copy-done.5, f32[24,256]{1,0:T(8,128)} %copy-done.6), custom_call_target="tpu_custom_call" | custom-call | tf_op jit(solution)/shard_map/pallas_call | solution.py:203
  26.9 5.6 %all_gather.3 = f32[5,4096]{1,0:T(8,128)S(1)} all-gather(f32[5,1024]{1,0:T(8,128)} %bitcast.14), channel_id=1, replica_groups=mesh['tm'=4,'space'=2,'hyp'=4] {'hyp'}, dimensions={1}, use_global_device_ids=true | all-gather | bytes 102400 | tf_op jit(solution)/shard_map/all_gather | solution.py:284
  32.5 0.6 %slice.23 = f32[4,4096]{1,0:T(4,128)} slice(f32[5,4096]{1,0:T(8,128)S(1)} %all_gather.3), slice={[1:5], [0:4096]} | slice | bytes 131072 | tf_op jit(solution)/shard_map/slice | solution.py:285
  33.2 0.6 %slice.22 = f32[1,4096]{1,0:T(1,128)} slice(f32[5,4096]{1,0:T(8,128)S(1)} %all_gather.3), slice={[0:1], [0:4096]} | slice | bytes 32768 | tf_op jit(solution)/shard_map/slice | solution.py:285
  (17 shorter events, 0.0 us)
Async XLA Ops:
  1.9 7.7 %copy-start.9 = (f32[4096]{0:T(1024)S(1)}, f32[4096]{0:T(1024)}, u32[]{:S(2)}) copy-start(f32[4096]{0:T(1024)} %param.10) | copy-start | bytes 49156
  1.9 9.9 %copy-start = (f32[4,4096]{1,0:T(4,128)S(1)}, f32[4,4096]{1,0:T(4,128)}, u32[]{:S(2)}) copy-start(f32[4,4096]{1,0:T(4,128)} %param.13) | copy-start | bytes 196612
  2.6 11.4 %collective-permute-start.1 = (f32[4,16,256]{2,1,0:T(8,128)S(1)}, f32[4,16,256]{2,1,0:T(8,128)S(1)}, u32[]{:S(2)}, u32[]{:S(2)}) collective-permute-start(f32[4,16,256]{2,1,0:T(8,128)S(1)} %get-tuple-element.17), channel_id=1, source_target_pairs={{0,8},{8,16},{16,24},{24,0},{1,9},{9,17},{17,25},{25,1},{2,10},{10... | collective-permute-start | bytes 196616 | tf_op jit(solution)/shard_map/ppermute | solution.py:250
  5.7 8.3 %collective-permute-start.2 = (f32[4,16,256]{2,1,0:T(8,128)S(1)}, f32[4,16,256]{2,1,0:T(8,128)S(1)}, u32[]{:S(2)}, u32[]{:S(2)}) collective-permute-start(f32[4,16,256]{2,1,0:T(8,128)S(1)} %get-tuple-element.16), channel_id=1, source_target_pairs={{0,16},{8,24},{16,0},{24,8},{1,17},{9,25},{17,1},{25,9},{2,18},{10... | collective-permute-start | bytes 196616 | tf_op jit(solution)/shard_map/ppermute | solution.py:250
  8.3 5.8 %collective-permute-start.3 = (f32[4,16,256]{2,1,0:T(8,128)S(1)}, f32[4,16,256]{2,1,0:T(8,128)S(1)}, u32[]{:S(2)}, u32[]{:S(2)}) collective-permute-start(f32[4,16,256]{2,1,0:T(8,128)S(1)} %get-tuple-element.15), channel_id=1, source_target_pairs={{0,24},{8,0},{16,8},{24,16},{1,25},{9,1},{17,9},{25,17},{2,26},{10... | collective-permute-start | bytes 196616 | tf_op jit(solution)/shard_map/ppermute | solution.py:250
  9.6 2.2 %copy-start.7 = (f32[4096]{0:T(1024)S(1)}, f32[4096]{0:T(1024)}, u32[]{:S(2)}) copy-start(f32[4096]{0:T(1024)} %param.12) | copy-start | bytes 49156
  9.6 2.2 %copy-start.8 = (f32[4096]{0:T(1024)S(1)}, f32[4096]{0:T(1024)}, u32[]{:S(2)}) copy-start(f32[4096]{0:T(1024)} %param.11) | copy-start | bytes 49156
  9.7 3.6 %collective-permute-start = (f32[64]{0:T(128)S(1)}, f32[64]{0:T(128)S(1)}, u32[]{:S(2)}, u32[]{:S(2)}) collective-permute-start(f32[64]{0:T(128)S(1)} %broadcast_select_fusion.1), channel_id=1, source_target_pairs={{0,4},{4,0},{1,5},{5,1},{2,6},{6,2},{3,7},{7,3},{8,12},{12,8},{9,1... | collective-permute-start | bytes 776 | tf_op jit(solution)/shard_map/ppermute | solution.py:19
  14.0 0.6 %copy-start.1 = (f32[4,16,256]{2,1,0:T(8,128)}, f32[4,16,256]{2,1,0:T(8,128)S(1)}, u32[]{:S(2)}) copy-start(f32[4,16,256]{2,1,0:T(8,128)S(1)} %collective-permute-done.1.refs_6_) | copy-start | bytes 196612
  14.0 0.6 %copy-start.2 = (f32[4,16,256]{2,1,0:T(8,128)}, f32[4,16,256]{2,1,0:T(8,128)S(1)}, u32[]{:S(2)}) copy-start(f32[4,16,256]{2,1,0:T(8,128)S(1)} %collective-permute-done.2.refs_7_) | copy-start | bytes 196612
  14.0 0.7 %copy-start.3 = (f32[4,16,256]{2,1,0:T(8,128)}, f32[4,16,256]{2,1,0:T(8,128)S(1)}, u32[]{:S(2)}) copy-start(f32[4,16,256]{2,1,0:T(8,128)S(1)} %collective-permute-done.3.refs_8_) | copy-start | bytes 196612
  18.2 5.9 %collective-permute-start.4 = (f32[24,256]{1,0:T(8,128)}, f32[24,256]{1,0:T(8,128)S(1)}, u32[]{:S(2)}, u32[]{:S(2)}) collective-permute-start(f32[24,256]{1,0:T(8,128)} %get-tuple-element.10), channel_id=1, source_target_pairs={{0,8},{8,16},{16,24},{24,0},{1,9},{9,17},{17,25},{25,1},{2,10},{10... | collective-permute-start | bytes 73736 | tf_op jit(solution)/shard_map/ppermute | solution.py:266
  19.0 5.2 %collective-permute-start.5 = (f32[24,256]{1,0:T(8,128)}, f32[24,256]{1,0:T(8,128)S(1)}, u32[]{:S(2)}, u32[]{:S(2)}) collective-permute-start(f32[24,256]{1,0:T(8,128)} %get-tuple-element.11), channel_id=1, source_target_pairs={{0,16},{8,24},{16,0},{24,8},{1,17},{9,25},{17,1},{25,9},{2,18},{10... | collective-permute-start | bytes 73736 | tf_op jit(solution)/shard_map/ppermute | solution.py:266
  20.8 4.0 %collective-permute-start.6 = (f32[24,256]{1,0:T(8,128)}, f32[24,256]{1,0:T(8,128)S(1)}, u32[]{:S(2)}, u32[]{:S(2)}) collective-permute-start(f32[24,256]{1,0:T(8,128)} %get-tuple-element.12), channel_id=1, source_target_pairs={{0,24},{8,0},{16,8},{24,16},{1,25},{9,1},{17,9},{25,17},{2,26},{10... | collective-permute-start | bytes 73736 | tf_op jit(solution)/shard_map/ppermute | solution.py:266
  24.2 0.6 %copy-start.4 = (f32[24,256]{1,0:T(8,128)}, f32[24,256]{1,0:T(8,128)S(1)}, u32[]{:S(2)}) copy-start(f32[24,256]{1,0:T(8,128)S(1)} %collective-permute-done.4.refs_1_) | copy-start | bytes 73732
  24.2 0.6 %copy-start.5 = (f32[24,256]{1,0:T(8,128)}, f32[24,256]{1,0:T(8,128)S(1)}, u32[]{:S(2)}) copy-start(f32[24,256]{1,0:T(8,128)S(1)} %collective-permute-done.5.refs_2_) | copy-start | bytes 73732
  24.8 0.6 %copy-start.6 = (f32[24,256]{1,0:T(8,128)}, f32[24,256]{1,0:T(8,128)S(1)}, u32[]{:S(2)}) copy-start(f32[24,256]{1,0:T(8,128)S(1)} %collective-permute-done.6.refs_3_) | copy-start | bytes 73732

commit v11 on v10

--- a/solution.py
+++ b/solution.py
@@ -27,30 +27,17 @@
     return jnp.concatenate([low, block, high])
 
 
-def chain_kernel(*refs, aligned):
-    place_ref, hyper_ref, window_ref, nodes_hbm, offsets_hbm = refs[:5]
-    blocks = (len(refs) - 13) // 2
-    pieces = refs[5 : 5 + blocks]
-    outs = refs[5 + blocks : 5 + 2 * blocks]
-    out_ref, piv_ref, slv_ref, data_ref, nodes_ref, offsets_ref, sems, piece_sems = refs[5 + 2 * blocks :]
-    _, _, rows, width = data_ref.shape
+def param_kernel(place_ref, hyper_ref, window_ref, nodes_hbm, offsets_hbm, par_ref, nodes_ref, offsets_ref, sems, *, aligned):
+    width = par_ref.shape[1]
     first = pl.multiple_of(place_ref[1], 128) if aligned else 0
     node_copy = pltpu.make_async_copy(nodes_hbm.at[:, pl.ds(first, width)], nodes_ref, sems.at[0])
     offsets_copy = pltpu.make_async_copy(
         offsets_hbm.at[:, pl.ds(first, width)], offsets_ref, sems.at[1]
     )
-    piece_copies = [
-        pltpu.make_async_copy(pieces[shift], data_ref.at[shift], piece_sems.at[shift])
-        for shift in range(blocks)
-    ]
     node_copy.start()
     offsets_copy.start()
-    for copy in piece_copies:
-        copy.start()
     node_copy.wait()
     offsets_copy.wait()
-
-    place = place_ref[0]
     window = window_ref[...]
     span = window.shape[1]
     near_off = offsets_ref[...]
@@ -78,6 +65,51 @@
     mps = -persist * scaled
     qs = 2.0 * persist * (1.0 - persist * persist) * scaled
     two_ls2 = 2.0 * ls2
+    par_ref[0:1, :] = sp
+    par_ref[1:2, :] = mps
+    par_ref[2:3, :] = qs
+    par_ref[3:4, :] = ns
+    par_ref[4:5, :] = two_ls2
+    par_ref[5:8, :] = jnp.zeros((3, width), jnp.float32)
+
+
+def run_params(place, hyper, window, nodes, offsets, width):
+    vmem = pl.BlockSpec(memory_space=pltpu.VMEM)
+    smem = pl.BlockSpec(memory_space=pltpu.SMEM)
+    hbm = pl.BlockSpec(memory_space=pl.ANY)
+    return pl.pallas_call(
+        functools.partial(param_kernel, aligned=nodes.shape[1] != width),
+        out_shape=jax.ShapeDtypeStruct((8, width), jnp.float32),
+        in_specs=[smem, smem, vmem, hbm, hbm],
+        out_specs=vmem,
+        scratch_shapes=[
+            pltpu.VMEM((6, width), jnp.float32),
+            pltpu.VMEM((4, width), jnp.int32),
+            pltpu.SemaphoreType.DMA((2,)),
+        ],
+        interpret=INTERPRET,
+    )(place, hyper, window, nodes, offsets)
+
+
+def chain_kernel(*refs):
+    place_ref, par_ref = refs[:2]
+    blocks = (len(refs) - 7) // 2
+    pieces = refs[2 : 2 + blocks]
+    outs = refs[2 + blocks : 2 + 2 * blocks]
+    out_ref, piv_ref, slv_ref, data_ref, piece_sems = refs[2 + 2 * blocks :]
+    _, _, rows, width = data_ref.shape
+    place = place_ref[0]
+    piece_copies = [
+        pltpu.make_async_copy(pieces[shift], data_ref.at[shift], piece_sems.at[shift])
+        for shift in range(blocks)
+    ]
+    for copy in piece_copies:
+        copy.start()
+    sp = par_ref[0:1, :]
+    mps = par_ref[1:2, :]
+    qs = par_ref[2:3, :]
+    ns = par_ref[3:4, :]
+    two_ls2 = par_ref[4:5, :]
     zeros = jnp.zeros_like(sp)
     carry = (zeros,) * 11
     for copy in piece_copies:
@@ -156,29 +188,26 @@
         outs[shift][...] = out_ref[lax.rem(place + shift, blocks)]
 
 
-def run_chain(place, hyper, window, nodes, offsets, pieces):
+def run_chain(place, params, pieces):
     blocks = len(pieces)
     _, rows, width = pieces[0].shape
     vmem = pl.BlockSpec(memory_space=pltpu.VMEM)
     smem = pl.BlockSpec(memory_space=pltpu.SMEM)
     hbm = pl.BlockSpec(memory_space=pl.ANY)
     return pl.pallas_call(
-        functools.partial(chain_kernel, aligned=nodes.shape[1] != width),
+        chain_kernel,
         out_shape=[jax.ShapeDtypeStruct((rows + 8, width), jnp.float32)] * blocks,
-        in_specs=[smem, smem, vmem, hbm, hbm] + [hbm] * blocks,
+        in_specs=[smem, vmem] + [hbm] * blocks,
         out_specs=[vmem] * blocks,
         scratch_shapes=[
             pltpu.VMEM((blocks, rows + 8, width), jnp.float32),
             pltpu.VMEM((blocks, rows, width), jnp.float32),
             pltpu.VMEM((blocks, rows, width), jnp.float32),
             pltpu.VMEM((blocks, 4, rows, width), jnp.float32),
-            pltpu.VMEM((6, width), jnp.float32),
-            pltpu.VMEM((4, width), jnp.int32),
-            pltpu.SemaphoreType.DMA((2,)),
             pltpu.SemaphoreType.DMA((blocks,)),
         ],
         interpret=INTERPRET,
-    )(place, hyper, window, nodes, offsets, *pieces)
+    )(place, params, *pieces)
 
 
 def place_kernel(place_ref, *refs):
@@ -261,7 +290,8 @@
     if chunk % 128:
         nodes = lax.dynamic_slice_in_dim(nodes, first, chunk, axis=1)
         near_off = lax.dynamic_slice_in_dim(offsets, first, chunk, axis=1)
-    payload = run_chain(place, hyper_params, window, nodes, near_off, arrived)
+    params = run_params(place, hyper_params, window, nodes, near_off, chunk)
+    payload = run_chain(place, params, arrived)
     returned = [payload[0]] + [
         lax.ppermute(
             payload[shift],

time: 34 us -> 36.2 us (1.065)
  Pallas kernels: 4.99 us -> 7.17 us
    pallas_call x1 -> x2, Pallas kernels: 3.53 us -> 5.71 us  [the longest x1 3.19 us: run_chain(): pl.pallas_call(chain_kernel, out_shape=[jax.ShapeDtypeStruct((rows + 8, w...]
  transfers between devices with their start and end apart: 7 -> 7, of which waited for: 3 -> 3; matrix products, arithmetic and copies ran while one was open for 6% -> 6% of each run, Pallas kernels for 0% -> 7%
where the time goes in v11:
time: 36.2 us; the launch traced here: 35.8 us
  starting transfers between devices  12.4 us (34%)
  Pallas kernels  7.17 us (20%)
  blocking collectives  5.61 us (15%)
  local copies, waits for them, and re-layouts  3.92 us (11%)
  waiting for transfers between devices  3.27 us (9%)
  other arithmetic  2.69 us (7%)
  between operations  0.78 us (2%)
    ppermute x3, starting transfers between devices, per_device_body(): lax.ppermute(pieces[shift], 'tm', [(i, (i + shift) % time_count) for i in...  6.99 us
    all_gather x1, blocking collectives, per_device_body(): stats_full = lax.all_gather(stats_quarter, 'hyp', axis=1, tiled=True)  5.61 us
    ppermute x3, starting transfers between devices, per_device_body(): lax.ppermute(payload[shift], 'tm', [(i, (i + shift) % time_count) for i i...  3.88 us
    pallas_call x1, Pallas kernels, run_chain(): pl.pallas_call(chain_kernel, out_shape=[jax.ShapeDtypeStruct((rows + 8, w...  3.19 us
    ppermute x3, waiting for transfers between devices, per_device_body(): lax.ppermute(payload[shift], 'tm', [(i, (i + shift) % time_count) for i i...  2.57 us
    pallas_call x1, Pallas kernels, run_params(): pl.pallas_call(functools.partial(param_kernel, aligned=nodes.shape[1] !=...  2.52 us
    ppermute x1, starting transfers between devices, with_halo(): got = lax.ppermute(send, axis, [(0, 1), (1, 0)])  1.53 us
    pallas_call x1, Pallas kernels, run_place(): pl.pallas_call(place_kernel, out_shape=(jax.ShapeDtypeStruct((rows, block...  1.46 us
  transfers between devices with their start and end apart: 7, of which 3 were waited for; matrix products, arithmetic and copies ran while one was open for 6% of the time, Pallas kernels for 7%

profile of v11, /device:TPU:0, one launch (start us, length us, event | category | flops | bytes accessed | tf_op | source)
XLA Modules:
  0.0 35.8 jit_solution(1654115679706228178)
XLA Ops:
  0.7 1.3 %pad_maximum_fusion = f32[4,16,4096]{2,1,0:T(8,128)S(1)} fusion(f32[1,16,4096]{2,1,0:T(8,128)} %bitcast.10, f32[1,16,4096]{2,1,0:T(8,128)} %bitcast.11, f32[1,16,4096]{2,1,0:T(8,128)} %bitcast.12, f32[1,16,4096]{2,1,0:T(8,128)} %bitcast.13), kind=kLoop, calls=%fused_computation | loop fusion | flops 786432 | bytes 2097152 | tf_op jit(solution)/shard_map/stack | solution.py:268
  1.9 0.0 copy-start.9
  1.9 0.0 copy-start
  2.0 0.7 %constant_dynamic-slice_fusion = (f32[4,16,256]{2,1,0:T(8,128)S(1)}, f32[4,16,256]{2,1,0:T(8,128)S(1)}, f32[4,16,256]{2,1,0:T(8,128)S(1)}, f32[4,16,256]{2,1,0:T(8,128)}) fusion(f32[4,16,4096]{2,1,0:T(8,128)S(1)} %pad_maximum_fusion, s32[]{:T(128)S(6)} %select_n.42, s32[]{:T(128)S(6)} %select_n.41, s32[]{:T(128)S(6)} %select_n.40, s32[]{:T(128)S(6)} %select_n.39), kind=kLoop, calls=%fused_computation.3 | loop fusion | bytes 524304 | tf_op jit(solution)/shard_map/dynamic_slice | solution.py:270
  2.6 3.1 %collective-permute-start.1 = (f32[4,16,256]{2,1,0:T(8,128)S(1)}, f32[4,16,256]{2,1,0:T(8,128)S(1)}, u32[]{:S(2)}, u32[]{:S(2)}) collective-permute-start(f32[4,16,256]{2,1,0:T(8,128)S(1)} %get-tuple-element.17), channel_id=1, source_target_pairs={{0,8},{8,16},{16,24},{24,0},{1,9},{9,17},{17,25},{25,1},{2,10},{10... | collective-permute-start | bytes 196616 | tf_op jit(solution)/shard_map/ppermute | solution.py:279
  5.7 2.6 %collective-permute-start.2 = (f32[4,16,256]{2,1,0:T(8,128)S(1)}, f32[4,16,256]{2,1,0:T(8,128)S(1)}, u32[]{:S(2)}, u32[]{:S(2)}) collective-permute-start(f32[4,16,256]{2,1,0:T(8,128)S(1)} %get-tuple-element.16), channel_id=1, source_target_pairs={{0,16},{8,24},{16,0},{24,8},{1,17},{9,25},{17,1},{25,9},{2,18},{10... | collective-permute-start | bytes 196616 | tf_op jit(solution)/shard_map/ppermute | solution.py:279
  8.3 1.3 %collective-permute-start.3 = (f32[4,16,256]{2,1,0:T(8,128)S(1)}, f32[4,16,256]{2,1,0:T(8,128)S(1)}, u32[]{:S(2)}, u32[]{:S(2)}) collective-permute-start(f32[4,16,256]{2,1,0:T(8,128)S(1)} %get-tuple-element.15), channel_id=1, source_target_pairs={{0,24},{8,0},{16,8},{24,16},{1,25},{9,1},{17,9},{25,17},{2,26},{10... | collective-permute-start | bytes 196616 | tf_op jit(solution)/shard_map/ppermute | solution.py:279
  9.6 0.1 broadcast_select_fusion.1
  9.7 1.5 %collective-permute-start = (f32[64]{0:T(128)S(1)}, f32[64]{0:T(128)S(1)}, u32[]{:S(2)}, u32[]{:S(2)}) collective-permute-start(f32[64]{0:T(128)S(1)} %broadcast_select_fusion.1), channel_id=1, source_target_pairs={{0,4},{4,0},{1,5},{5,1},{2,6},{6,2},{3,7},{7,3},{8,12},{12,8},{9,1... | collective-permute-start | bytes 776 | tf_op jit(solution)/shard_map/ppermute | solution.py:19
  11.2 0.6 %pad_add_fusion.place_ref.refs_0_ = s32[2]{0:T(128)} fusion(s32[1]{0:T(128)} %bitcast.1, s32[1]{0:T(128)} %bitcast), kind=kLoop, calls=%fused_computation.10 | loop fusion | flops 2 | bytes 16 | tf_op jit(solution)/shard_map/stack | solution.py:286
  11.9 0.7 %pad_maximum_fusion.1.nodes_hbm = f32[6,4096]{1,0:T(8,128)} fusion(f32[4,4096]{1,0:T(4,128)S(1)} %copy-done, f32[1,4096]{1,0:T(1,128)S(1)} %bitcast.15, f32[1,4096]{1,0:T(1,128)S(1)} %bitcast.16), kind=kLoop, calls=%fused_computation.1 | loop fusion | flops 49152 | bytes 196608 | tf_op jit(solution)/shard_map/concatenate | solution.py:288
  12.6 0.7 %collective-permute-done = f32[64]{0:T(128)S(1)} collective-permute-done((f32[64]{0:T(128)S(1)}, f32[64]{0:T(128)S(1)}, u32[]{:S(2)}, u32[]{:S(2)}) %collective-permute-start) | collective-permute-done | bytes 288 | tf_op jit(solution)/shard_map/ppermute | solution.py:19
  13.3 0.1 concatenate.6
  13.4 0.1 dynamic_slice.15
  13.4 0.6 %broadcast_in_dim.9.window_ref = f32[1,384]{1,0:T(1,128)} reshape(f32[384]{0:T(512)S(1)} %dynamic_slice.15) | data formatting | bytes 3072 | tf_op jit(solution)/shard_map/broadcast_in_dim | solution.py:287
  14.0 2.5 %shard_map.121.refs_1_ = f32[8,256]{1,0:T(8,128)} custom-call(s32[2]{0:T(128)} %pad_add_fusion.place_ref.refs_0_, f32[4]{0:T(128)} %hyper_ref.1, f32[1,384]{1,0:T(1,128)} %broadcast_in_dim.9.window_ref, f32[6,4096]{1,0:T(8,128)} %pad_maximum_fusion.1.nodes_hbm, s32[4,4096]{1,0:T(4,128)} %offsets_hbm.1), custom_call_target="tpu_custom_call" | custom-call | tf_op jit(solution)/shard_map/pallas_call | solution.py:80
  16.5 0.0 copy-start.1
  16.6 0.6 %copy-done.1 = f32[4,16,256]{2,1,0:T(8,128)} copy-done((f32[4,16,256]{2,1,0:T(8,128)}, f32[4,16,256]{2,1,0:T(8,128)S(1)}, u32[]{:S(2)}) %copy-start.1) | copy-done | bytes 65560
  17.2 0.0 copy-done.2
  17.2 0.0 copy-done.3
  17.2 3.2 %shard_map.122 = (f32[24,256]{1,0:T(8,128)}, f32[24,256]{1,0:T(8,128)}, f32[24,256]{1,0:T(8,128)}, f32[24,256]{1,0:T(8,128)}) custom-call(s32[2]{0:T(128)} %pad_add_fusion.place_ref.refs_0_, f32[8,256]{1,0:T(8,128)} %shard_map.121.refs_1_, f32[4,16,256]{2,1,0:T(8,128)} %get-tuple-element.18.refs_2_, f32[4,16,256]{2,1,0:T(8,128)} %copy-done.1, ...), custom_call_target="tpu_custom_call" | custom-call | tf_op jit(solution)/shard_map/pallas_call | solution.py:197
  20.4 0.7 %collective-permute-start.4 = (f32[24,256]{1,0:T(8,128)}, f32[24,256]{1,0:T(8,128)S(1)}, u32[]{:S(2)}, u32[]{:S(2)}) collective-permute-start(f32[24,256]{1,0:T(8,128)} %get-tuple-element.10), channel_id=1, source_target_pairs={{0,8},{8,16},{16,24},{24,0},{1,9},{9,17},{17,25},{25,1},{2,10},{10... | collective-permute-start | bytes 73736 | tf_op jit(solution)/shard_map/ppermute | solution.py:296
  21.1 0.3 collective-permute-start.5
  21.5 2.8 %collective-permute-start.6 = (f32[24,256]{1,0:T(8,128)}, f32[24,256]{1,0:T(8,128)S(1)}, u32[]{:S(2)}, u32[]{:S(2)}) collective-permute-start(f32[24,256]{1,0:T(8,128)} %get-tuple-element.12), channel_id=1, source_target_pairs={{0,24},{8,0},{16,8},{24,16},{1,25},{9,1},{17,9},{25,17},{2,26},{10... | collective-permute-start | bytes 73736 | tf_op jit(solution)/shard_map/ppermute | solution.py:296
  24.3 2.0 %collective-permute-done.4.refs_1_ = f32[24,256]{1,0:T(8,128)S(1)} collective-permute-done((f32[24,256]{1,0:T(8,128)}, f32[24,256]{1,0:T(8,128)S(1)}, u32[]{:S(2)}, u32[]{:S(2)}) %collective-permute-start.4) | collective-permute-done | bytes 24608 | tf_op jit(solution)/shard_map/ppermute | solution.py:296
  26.3 0.5 %collective-permute-done.6.refs_3_ = f32[24,256]{1,0:T(8,128)S(1)} collective-permute-done((f32[24,256]{1,0:T(8,128)}, f32[24,256]{1,0:T(8,128)S(1)}, u32[]{:S(2)}, u32[]{:S(2)}) %collective-permute-start.6) | collective-permute-done | bytes 24608 | tf_op jit(solution)/shard_map/ppermute | solution.py:296
  26.9 0.1 copy-done.4
  27.0 0.5 %copy-done.6 = f32[24,256]{1,0:T(8,128)} copy-done((f32[24,256]{1,0:T(8,128)}, f32[24,256]{1,0:T(8,128)S(1)}, u32[]{:S(2)}) %copy-start.6) | copy-done | bytes 24600
  27.5 1.5 %shard_map.123 = (f32[16,1024]{1,0:T(8,128)}, f32[8,1024]{1,0:T(8,128)}) custom-call(s32[2]{0:T(128)} %pad_add_fusion.place_ref.refs_0_, f32[24,256]{1,0:T(8,128)} %get-tuple-element.9.refs_0_, f32[24,256]{1,0:T(8,128)} %copy-done.4, f32[24,256]{1,0:T(8,128)} %copy-done.5, f32[24,256]{1,0:T(8,128)} %copy-done.6), custom_call_target="tpu_custom_call" | custom-call | tf_op jit(solution)/shard_map/pallas_call | solution.py:232
  28.9 5.6 %all_gather.3 = f32[5,4096]{1,0:T(8,128)S(1)} all-gather(f32[5,1024]{1,0:T(8,128)} %bitcast.14), channel_id=1, replica_groups=mesh['tm'=4,'space'=2,'hyp'=4] {'hyp'}, dimensions={1}, use_global_device_ids=true | all-gather | bytes 102400 | tf_op jit(solution)/shard_map/all_gather | solution.py:314
  34.6 0.6 %slice.23 = f32[4,4096]{1,0:T(4,128)} slice(f32[5,4096]{1,0:T(8,128)S(1)} %all_gather.3), slice={[1:5], [0:4096]} | slice | bytes 131072 | tf_op jit(solution)/shard_map/slice | solution.py:315
  35.2 0.6 %slice.22 = f32[1,4096]{1,0:T(1,128)} slice(f32[5,4096]{1,0:T(8,128)S(1)} %all_gather.3), slice={[0:1], [0:4096]} | slice | bytes 32768 | tf_op jit(solution)/shard_map/slice | solution.py:315
  (18 shorter events, 0.0 us)
Async XLA Ops:
  1.9 7.7 %copy-start.9 = (f32[4096]{0:T(1024)S(1)}, f32[4096]{0:T(1024)}, u32[]{:S(2)}) copy-start(f32[4096]{0:T(1024)} %param.10) | copy-start | bytes 49156
  1.9 9.9 %copy-start = (f32[4,4096]{1,0:T(4,128)S(1)}, f32[4,4096]{1,0:T(4,128)}, u32[]{:S(2)}) copy-start(f32[4,4096]{1,0:T(4,128)} %param.13) | copy-start | bytes 196612
  2.6 13.9 %collective-permute-start.1 = (f32[4,16,256]{2,1,0:T(8,128)S(1)}, f32[4,16,256]{2,1,0:T(8,128)S(1)}, u32[]{:S(2)}, u32[]{:S(2)}) collective-permute-start(f32[4,16,256]{2,1,0:T(8,128)S(1)} %get-tuple-element.17), channel_id=1, source_target_pairs={{0,8},{8,16},{16,24},{24,0},{1,9},{9,17},{17,25},{25,1},{2,10},{10... | collective-permute-start | bytes 196616 | tf_op jit(solution)/shard_map/ppermute | solution.py:279
  5.7 10.9 %collective-permute-start.2 = (f32[4,16,256]{2,1,0:T(8,128)S(1)}, f32[4,16,256]{2,1,0:T(8,128)S(1)}, u32[]{:S(2)}, u32[]{:S(2)}) collective-permute-start(f32[4,16,256]{2,1,0:T(8,128)S(1)} %get-tuple-element.16), channel_id=1, source_target_pairs={{0,16},{8,24},{16,0},{24,8},{1,17},{9,25},{17,1},{25,9},{2,18},{10... | collective-permute-start | bytes 196616 | tf_op jit(solution)/shard_map/ppermute | solution.py:279
  8.3 8.3 %collective-permute-start.3 = (f32[4,16,256]{2,1,0:T(8,128)S(1)}, f32[4,16,256]{2,1,0:T(8,128)S(1)}, u32[]{:S(2)}, u32[]{:S(2)}) collective-permute-start(f32[4,16,256]{2,1,0:T(8,128)S(1)} %get-tuple-element.15), channel_id=1, source_target_pairs={{0,24},{8,0},{16,8},{24,16},{1,25},{9,1},{17,9},{25,17},{2,26},{10... | collective-permute-start | bytes 196616 | tf_op jit(solution)/shard_map/ppermute | solution.py:279
  9.6 2.3 %copy-start.7 = (f32[4096]{0:T(1024)S(1)}, f32[4096]{0:T(1024)}, u32[]{:S(2)}) copy-start(f32[4096]{0:T(1024)} %param.12) | copy-start | bytes 49156
  9.6 2.3 %copy-start.8 = (f32[4096]{0:T(1024)S(1)}, f32[4096]{0:T(1024)}, u32[]{:S(2)}) copy-start(f32[4096]{0:T(1024)} %param.11) | copy-start | bytes 49156
  9.7 3.6 %collective-permute-start = (f32[64]{0:T(128)S(1)}, f32[64]{0:T(128)S(1)}, u32[]{:S(2)}, u32[]{:S(2)}) collective-permute-start(f32[64]{0:T(128)S(1)} %broadcast_select_fusion.1), channel_id=1, source_target_pairs={{0,4},{4,0},{1,5},{5,1},{2,6},{6,2},{3,7},{7,3},{8,12},{12,8},{9,1... | collective-permute-start | bytes 776 | tf_op jit(solution)/shard_map/ppermute | solution.py:19
  16.5 0.6 %copy-start.1 = (f32[4,16,256]{2,1,0:T(8,128)}, f32[4,16,256]{2,1,0:T(8,128)S(1)}, u32[]{:S(2)}) copy-start(f32[4,16,256]{2,1,0:T(8,128)S(1)} %collective-permute-done.1.refs_3_) | copy-start | bytes 196612
  16.6 0.6 %copy-start.2 = (f32[4,16,256]{2,1,0:T(8,128)}, f32[4,16,256]{2,1,0:T(8,128)S(1)}, u32[]{:S(2)}) copy-start(f32[4,16,256]{2,1,0:T(8,128)S(1)} %collective-permute-done.2.refs_4_) | copy-start | bytes 196612
  16.6 0.6 %copy-start.3 = (f32[4,16,256]{2,1,0:T(8,128)}, f32[4,16,256]{2,1,0:T(8,128)S(1)}, u32[]{:S(2)}) copy-start(f32[4,16,256]{2,1,0:T(8,128)S(1)} %collective-permute-done.3.refs_5_) | copy-start | bytes 196612
  20.4 5.9 %collective-permute-start.4 = (f32[24,256]{1,0:T(8,128)}, f32[24,256]{1,0:T(8,128)S(1)}, u32[]{:S(2)}, u32[]{:S(2)}) collective-permute-start(f32[24,256]{1,0:T(8,128)} %get-tuple-element.10), channel_id=1, source_target_pairs={{0,8},{8,16},{16,24},{24,0},{1,9},{9,17},{17,25},{25,1},{2,10},{10... | collective-permute-start | bytes 73736 | tf_op jit(solution)/shard_map/ppermute | solution.py:296
  21.1 5.2 %collective-permute-start.5 = (f32[24,256]{1,0:T(8,128)}, f32[24,256]{1,0:T(8,128)S(1)}, u32[]{:S(2)}, u32[]{:S(2)}) collective-permute-start(f32[24,256]{1,0:T(8,128)} %get-tuple-element.11), channel_id=1, source_target_pairs={{0,16},{8,24},{16,0},{24,8},{1,17},{9,25},{17,1},{25,9},{2,18},{10... | collective-permute-start | bytes 73736 | tf_op jit(solution)/shard_map/ppermute | solution.py:296
  21.5 5.4 %collective-permute-start.6 = (f32[24,256]{1,0:T(8,128)}, f32[24,256]{1,0:T(8,128)S(1)}, u32[]{:S(2)}, u32[]{:S(2)}) collective-permute-start(f32[24,256]{1,0:T(8,128)} %get-tuple-element.12), channel_id=1, source_target_pairs={{0,24},{8,0},{16,8},{24,16},{1,25},{9,1},{17,9},{25,17},{2,26},{10... | collective-permute-start | bytes 73736 | tf_op jit(solution)/shard_map/ppermute | solution.py:296
  26.3 0.6 %copy-start.4 = (f32[24,256]{1,0:T(8,128)}, f32[24,256]{1,0:T(8,128)S(1)}, u32[]{:S(2)}) copy-start(f32[24,256]{1,0:T(8,128)S(1)} %collective-permute-done.4.refs_1_) | copy-start | bytes 73732
  26.3 0.6 %copy-start.5 = (f32[24,256]{1,0:T(8,128)}, f32[24,256]{1,0:T(8,128)S(1)}, u32[]{:S(2)}) copy-start(f32[24,256]{1,0:T(8,128)S(1)} %collective-permute-done.5.refs_2_) | copy-start | bytes 73732
  26.9 0.6 %copy-start.6 = (f32[24,256]{1,0:T(8,128)}, f32[24,256]{1,0:T(8,128)S(1)}, u32[]{:S(2)}) copy-start(f32[24,256]{1,0:T(8,128)S(1)} %collective-permute-done.6.refs_3_) | copy-start | bytes 73732

commit v12 on v11

--- a/solution.py
+++ b/solution.py
@@ -42,13 +42,23 @@
     span = window.shape[1]
     near_off = offsets_ref[...]
     ones = jnp.ones((1, width), jnp.float32)
-    nearby = jnp.zeros(near_off.shape, jnp.float32)
-    own_kappa = None
-    for shift in range(-BAND, BAND + 1):
-        moved = pltpu.roll(window, (span - BAND - shift) % span, 1)[:, :width]
-        if shift == 0:
-            own_kappa = moved
-        nearby = jnp.where(near_off == shift, moved, nearby)
+    own_kappa = pltpu.roll(window, span - BAND, 1)[:, :width]
+    lanes = lax.broadcasted_iota(jnp.int32, (1, width), 1)
+    targets = jnp.concatenate(
+        [BAND + lanes + near_off[k : k + 1, :] for k in range(near_off.shape[0])], axis=1
+    )
+    picks = (lax.broadcasted_iota(jnp.int32, (span, targets.shape[1]), 0) == targets).astype(
+        jnp.float32
+    )
+    gathered = jnp.dot(
+        jnp.broadcast_to(window, (8, span)),
+        picks,
+        precision=lax.Precision.HIGHEST,
+        preferred_element_type=jnp.float32,
+    )[0:1, :]
+    nearby = jnp.concatenate(
+        [gathered[:, k * width : (k + 1) * width] for k in range(near_off.shape[0])], axis=0
+    )
     weights = nodes_ref[2:6, :]
     edge_sum = (
         weights[0:1] * nearby[0:1]

time: 36.2 us -> 36.7 us (1.014)
  Pallas kernels: 7.17 us -> 7.63 us
    pallas_call x1, Pallas kernels: 2.52 us -> 2.98 us  [run_params(): pl.pallas_call(functools.partial(param_kernel, aligned=nodes.shape[1] !=...]
  transfers between devices with their start and end apart: 7 -> 7, of which waited for: 3 -> 3; matrix products, arithmetic and copies ran while one was open for 6% -> 6% of each run, Pallas kernels for 7% -> 8%
where the time goes in v12:
time: 36.7 us; the launch traced here: 36.3 us
  starting transfers between devices  12.4 us (34%)
  Pallas kernels  7.63 us (21%)
  blocking collectives  5.61 us (15%)
  local copies, waits for them, and re-layouts  3.92 us (11%)
  waiting for transfers between devices  3.27 us (9%)
  other arithmetic  2.69 us (7%)
  between operations  0.78 us (2%)
    ppermute x3, starting transfers between devices, per_device_body(): lax.ppermute(pieces[shift], 'tm', [(i, (i + shift) % time_count) for i in...  6.99 us
    all_gather x1, blocking collectives, per_device_body(): stats_full = lax.all_gather(stats_quarter, 'hyp', axis=1, tiled=True)  5.61 us
    ppermute x3, starting transfers between devices, per_device_body(): lax.ppermute(payload[shift], 'tm', [(i, (i + shift) % time_count) for i i...  3.88 us
    pallas_call x1, Pallas kernels, run_chain(): pl.pallas_call(chain_kernel, out_shape=[jax.ShapeDtypeStruct((rows + 8, w...  3.19 us
    pallas_call x1, Pallas kernels, run_params(): pl.pallas_call(functools.partial(param_kernel, aligned=nodes.shape[1] !=...  2.98 us
    ppermute x3, waiting for transfers between devices, per_device_body(): lax.ppermute(payload[shift], 'tm', [(i, (i + shift) % time_count) for i i...  2.57 us
    ppermute x1, starting transfers between devices, with_halo(): got = lax.ppermute(send, axis, [(0, 1), (1, 0)])  1.53 us
    pallas_call x1, Pallas kernels, run_place(): pl.pallas_call(place_kernel, out_shape=(jax.ShapeDtypeStruct((rows, block...  1.46 us
  transfers between devices with their start and end apart: 7, of which 3 were waited for; matrix products, arithmetic and copies ran while one was open for 6% of the time, Pallas kernels for 8%

profile of v12, /device:TPU:0, one launch (start us, length us, event | category | flops | bytes accessed | tf_op | source)
XLA Modules:
  0.0 36.3 jit_solution(1041976500244402897)
XLA Ops:
  0.7 1.3 %pad_maximum_fusion = f32[4,16,4096]{2,1,0:T(8,128)S(1)} fusion(f32[1,16,4096]{2,1,0:T(8,128)} %bitcast.10, f32[1,16,4096]{2,1,0:T(8,128)} %bitcast.11, f32[1,16,4096]{2,1,0:T(8,128)} %bitcast.12, f32[1,16,4096]{2,1,0:T(8,128)} %bitcast.13), kind=kLoop, calls=%fused_computation | loop fusion | flops 786432 | bytes 2097152 | tf_op jit(solution)/shard_map/stack | solution.py:278
  1.9 0.0 copy-start.9
  1.9 0.0 copy-start
  2.0 0.7 %constant_dynamic-slice_fusion = (f32[4,16,256]{2,1,0:T(8,128)S(1)}, f32[4,16,256]{2,1,0:T(8,128)S(1)}, f32[4,16,256]{2,1,0:T(8,128)S(1)}, f32[4,16,256]{2,1,0:T(8,128)}) fusion(f32[4,16,4096]{2,1,0:T(8,128)S(1)} %pad_maximum_fusion, s32[]{:T(128)S(6)} %select_n.42, s32[]{:T(128)S(6)} %select_n.41, s32[]{:T(128)S(6)} %select_n.40, s32[]{:T(128)S(6)} %select_n.39), kind=kLoop, calls=%fused_computation.3 | loop fusion | bytes 524304 | tf_op jit(solution)/shard_map/dynamic_slice | solution.py:280
  2.6 3.1 %collective-permute-start.1 = (f32[4,16,256]{2,1,0:T(8,128)S(1)}, f32[4,16,256]{2,1,0:T(8,128)S(1)}, u32[]{:S(2)}, u32[]{:S(2)}) collective-permute-start(f32[4,16,256]{2,1,0:T(8,128)S(1)} %get-tuple-element.17), channel_id=1, source_target_pairs={{0,8},{8,16},{16,24},{24,0},{1,9},{9,17},{17,25},{25,1},{2,10},{10... | collective-permute-start | bytes 196616 | tf_op jit(solution)/shard_map/ppermute | solution.py:289
  5.7 2.6 %collective-permute-start.2 = (f32[4,16,256]{2,1,0:T(8,128)S(1)}, f32[4,16,256]{2,1,0:T(8,128)S(1)}, u32[]{:S(2)}, u32[]{:S(2)}) collective-permute-start(f32[4,16,256]{2,1,0:T(8,128)S(1)} %get-tuple-element.16), channel_id=1, source_target_pairs={{0,16},{8,24},{16,0},{24,8},{1,17},{9,25},{17,1},{25,9},{2,18},{10... | collective-permute-start | bytes 196616 | tf_op jit(solution)/shard_map/ppermute | solution.py:289
  8.3 1.3 %collective-permute-start.3 = (f32[4,16,256]{2,1,0:T(8,128)S(1)}, f32[4,16,256]{2,1,0:T(8,128)S(1)}, u32[]{:S(2)}, u32[]{:S(2)}) collective-permute-start(f32[4,16,256]{2,1,0:T(8,128)S(1)} %get-tuple-element.15), channel_id=1, source_target_pairs={{0,24},{8,0},{16,8},{24,16},{1,25},{9,1},{17,9},{25,17},{2,26},{10... | collective-permute-start | bytes 196616 | tf_op jit(solution)/shard_map/ppermute | solution.py:289
  9.6 0.1 broadcast_select_fusion.1
  9.7 1.5 %collective-permute-start = (f32[64]{0:T(128)S(1)}, f32[64]{0:T(128)S(1)}, u32[]{:S(2)}, u32[]{:S(2)}) collective-permute-start(f32[64]{0:T(128)S(1)} %broadcast_select_fusion.1), channel_id=1, source_target_pairs={{0,4},{4,0},{1,5},{5,1},{2,6},{6,2},{3,7},{7,3},{8,12},{12,8},{9,1... | collective-permute-start | bytes 776 | tf_op jit(solution)/shard_map/ppermute | solution.py:19
  11.2 0.6 %pad_add_fusion.place_ref.refs_0_ = s32[2]{0:T(128)} fusion(s32[1]{0:T(128)} %bitcast.1, s32[1]{0:T(128)} %bitcast), kind=kLoop, calls=%fused_computation.10 | loop fusion | flops 2 | bytes 16 | tf_op jit(solution)/shard_map/stack | solution.py:296
  11.9 0.7 %pad_maximum_fusion.1.nodes_hbm = f32[6,4096]{1,0:T(8,128)} fusion(f32[4,4096]{1,0:T(4,128)S(1)} %copy-done, f32[1,4096]{1,0:T(1,128)S(1)} %bitcast.15, f32[1,4096]{1,0:T(1,128)S(1)} %bitcast.16), kind=kLoop, calls=%fused_computation.1 | loop fusion | flops 49152 | bytes 196608 | tf_op jit(solution)/shard_map/concatenate | solution.py:298
  12.6 0.7 %collective-permute-done = f32[64]{0:T(128)S(1)} collective-permute-done((f32[64]{0:T(128)S(1)}, f32[64]{0:T(128)S(1)}, u32[]{:S(2)}, u32[]{:S(2)}) %collective-permute-start) | collective-permute-done | bytes 288 | tf_op jit(solution)/shard_map/ppermute | solution.py:19
  13.3 0.1 concatenate.6
  13.4 0.1 dynamic_slice.15
  13.4 0.6 %broadcast_in_dim.9.window_ref = f32[1,384]{1,0:T(1,128)} reshape(f32[384]{0:T(512)S(1)} %dynamic_slice.15) | data formatting | bytes 3072 | tf_op jit(solution)/shard_map/broadcast_in_dim | solution.py:297
  14.0 3.0 %shard_map.121.refs_1_ = f32[8,256]{1,0:T(8,128)} custom-call(s32[2]{0:T(128)} %pad_add_fusion.place_ref.refs_0_, f32[4]{0:T(128)} %hyper_ref.1, f32[1,384]{1,0:T(1,128)} %broadcast_in_dim.9.window_ref, f32[6,4096]{1,0:T(8,128)} %pad_maximum_fusion.1.nodes_hbm, s32[4,4096]{1,0:T(4,128)} %offsets_hbm.1), custom_call_target="tpu_custom_call" | custom-call | tf_op jit(solution)/shard_map/pallas_call | solution.py:90
  17.0 0.0 copy-start.1
  17.1 0.6 %copy-done.1 = f32[4,16,256]{2,1,0:T(8,128)} copy-done((f32[4,16,256]{2,1,0:T(8,128)}, f32[4,16,256]{2,1,0:T(8,128)S(1)}, u32[]{:S(2)}) %copy-start.1) | copy-done | bytes 65560
  17.6 0.0 copy-done.3
  17.7 3.2 %shard_map.122 = (f32[24,256]{1,0:T(8,128)}, f32[24,256]{1,0:T(8,128)}, f32[24,256]{1,0:T(8,128)}, f32[24,256]{1,0:T(8,128)}) custom-call(s32[2]{0:T(128)} %pad_add_fusion.place_ref.refs_0_, f32[8,256]{1,0:T(8,128)} %shard_map.121.refs_1_, f32[4,16,256]{2,1,0:T(8,128)} %get-tuple-element.18.refs_2_, f32[4,16,256]{2,1,0:T(8,128)} %copy-done.1, ...), custom_call_target="tpu_custom_call" | custom-call | tf_op jit(solution)/shard_map/pallas_call | solution.py:207
  20.9 0.7 %collective-permute-start.4 = (f32[24,256]{1,0:T(8,128)}, f32[24,256]{1,0:T(8,128)S(1)}, u32[]{:S(2)}, u32[]{:S(2)}) collective-permute-start(f32[24,256]{1,0:T(8,128)} %get-tuple-element.10), channel_id=1, source_target_pairs={{0,8},{8,16},{16,24},{24,0},{1,9},{9,17},{17,25},{25,1},{2,10},{10... | collective-permute-start | bytes 73736 | tf_op jit(solution)/shard_map/ppermute | solution.py:306
  21.6 0.3 collective-permute-start.5
  21.9 2.8 %collective-permute-start.6 = (f32[24,256]{1,0:T(8,128)}, f32[24,256]{1,0:T(8,128)S(1)}, u32[]{:S(2)}, u32[]{:S(2)}) collective-permute-start(f32[24,256]{1,0:T(8,128)} %get-tuple-element.12), channel_id=1, source_target_pairs={{0,24},{8,0},{16,8},{24,16},{1,25},{9,1},{17,9},{25,17},{2,26},{10... | collective-permute-start | bytes 73736 | tf_op jit(solution)/shard_map/ppermute | solution.py:306
  24.8 2.0 %collective-permute-done.4.refs_1_ = f32[24,256]{1,0:T(8,128)S(1)} collective-permute-done((f32[24,256]{1,0:T(8,128)}, f32[24,256]{1,0:T(8,128)S(1)}, u32[]{:S(2)}, u32[]{:S(2)}) %collective-permute-start.4) | collective-permute-done | bytes 24608 | tf_op jit(solution)/shard_map/ppermute | solution.py:306
  26.8 0.5 %collective-permute-done.6.refs_3_ = f32[24,256]{1,0:T(8,128)S(1)} collective-permute-done((f32[24,256]{1,0:T(8,128)}, f32[24,256]{1,0:T(8,128)S(1)}, u32[]{:S(2)}, u32[]{:S(2)}) %collective-permute-start.6) | collective-permute-done | bytes 24608 | tf_op jit(solution)/shard_map/ppermute | solution.py:306
  27.3 0.1 copy-done.4
  27.4 0.0 copy-done.5
  27.4 0.5 %copy-done.6 = f32[24,256]{1,0:T(8,128)} copy-done((f32[24,256]{1,0:T(8,128)}, f32[24,256]{1,0:T(8,128)S(1)}, u32[]{:S(2)}) %copy-start.6) | copy-done | bytes 24600
  28.0 1.5 %shard_map.123 = (f32[16,1024]{1,0:T(8,128)}, f32[8,1024]{1,0:T(8,128)}) custom-call(s32[2]{0:T(128)} %pad_add_fusion.place_ref.refs_0_, f32[24,256]{1,0:T(8,128)} %get-tuple-element.9.refs_0_, f32[24,256]{1,0:T(8,128)} %copy-done.4, f32[24,256]{1,0:T(8,128)} %copy-done.5, f32[24,256]{1,0:T(8,128)} %copy-done.6), custom_call_target="tpu_custom_call" | custom-call | tf_op jit(solution)/shard_map/pallas_call | solution.py:242
  29.4 5.6 %all_gather.3 = f32[5,4096]{1,0:T(8,128)S(1)} all-gather(f32[5,1024]{1,0:T(8,128)} %bitcast.14), channel_id=1, replica_groups=mesh['tm'=4,'space'=2,'hyp'=4] {'hyp'}, dimensions={1}, use_global_device_ids=true | all-gather | bytes 102400 | tf_op jit(solution)/shard_map/all_gather | solution.py:324
  35.0 0.6 %slice.23 = f32[4,4096]{1,0:T(4,128)} slice(f32[5,4096]{1,0:T(8,128)S(1)} %all_gather.3), slice={[1:5], [0:4096]} | slice | bytes 131072 | tf_op jit(solution)/shard_map/slice | solution.py:325
  35.7 0.6 %slice.22 = f32[1,4096]{1,0:T(1,128)} slice(f32[5,4096]{1,0:T(8,128)S(1)} %all_gather.3), slice={[0:1], [0:4096]} | slice | bytes 32768 | tf_op jit(solution)/shard_map/slice | solution.py:325
  (18 shorter events, 0.0 us)
Async XLA Ops:
  1.9 7.7 %copy-start.9 = (f32[4096]{0:T(1024)S(1)}, f32[4096]{0:T(1024)}, u32[]{:S(2)}) copy-start(f32[4096]{0:T(1024)} %param.10) | copy-start | bytes 49156
  1.9 9.9 %copy-start = (f32[4,4096]{1,0:T(4,128)S(1)}, f32[4,4096]{1,0:T(4,128)}, u32[]{:S(2)}) copy-start(f32[4,4096]{1,0:T(4,128)} %param.13) | copy-start | bytes 196612
  2.6 14.4 %collective-permute-start.1 = (f32[4,16,256]{2,1,0:T(8,128)S(1)}, f32[4,16,256]{2,1,0:T(8,128)S(1)}, u32[]{:S(2)}, u32[]{:S(2)}) collective-permute-start(f32[4,16,256]{2,1,0:T(8,128)S(1)} %get-tuple-element.17), channel_id=1, source_target_pairs={{0,8},{8,16},{16,24},{24,0},{1,9},{9,17},{17,25},{25,1},{2,10},{10... | collective-permute-start | bytes 196616 | tf_op jit(solution)/shard_map/ppermute | solution.py:289
  5.7 11.4 %collective-permute-start.2 = (f32[4,16,256]{2,1,0:T(8,128)S(1)}, f32[4,16,256]{2,1,0:T(8,128)S(1)}, u32[]{:S(2)}, u32[]{:S(2)}) collective-permute-start(f32[4,16,256]{2,1,0:T(8,128)S(1)} %get-tuple-element.16), channel_id=1, source_target_pairs={{0,16},{8,24},{16,0},{24,8},{1,17},{9,25},{17,1},{25,9},{2,18},{10... | collective-permute-start | bytes 196616 | tf_op jit(solution)/shard_map/ppermute | solution.py:289
  8.3 8.8 %collective-permute-start.3 = (f32[4,16,256]{2,1,0:T(8,128)S(1)}, f32[4,16,256]{2,1,0:T(8,128)S(1)}, u32[]{:S(2)}, u32[]{:S(2)}) collective-permute-start(f32[4,16,256]{2,1,0:T(8,128)S(1)} %get-tuple-element.15), channel_id=1, source_target_pairs={{0,24},{8,0},{16,8},{24,16},{1,25},{9,1},{17,9},{25,17},{2,26},{10... | collective-permute-start | bytes 196616 | tf_op jit(solution)/shard_map/ppermute | solution.py:289
  9.6 2.3 %copy-start.7 = (f32[4096]{0:T(1024)S(1)}, f32[4096]{0:T(1024)}, u32[]{:S(2)}) copy-start(f32[4096]{0:T(1024)} %param.12) | copy-start | bytes 49156
  9.6 2.3 %copy-start.8 = (f32[4096]{0:T(1024)S(1)}, f32[4096]{0:T(1024)}, u32[]{:S(2)}) copy-start(f32[4096]{0:T(1024)} %param.11) | copy-start | bytes 49156
  9.7 3.6 %collective-permute-start = (f32[64]{0:T(128)S(1)}, f32[64]{0:T(128)S(1)}, u32[]{:S(2)}, u32[]{:S(2)}) collective-permute-start(f32[64]{0:T(128)S(1)} %broadcast_select_fusion.1), channel_id=1, source_target_pairs={{0,4},{4,0},{1,5},{5,1},{2,6},{6,2},{3,7},{7,3},{8,12},{12,8},{9,1... | collective-permute-start | bytes 776 | tf_op jit(solution)/shard_map/ppermute | solution.py:19
  17.0 0.6 %copy-start.1 = (f32[4,16,256]{2,1,0:T(8,128)}, f32[4,16,256]{2,1,0:T(8,128)S(1)}, u32[]{:S(2)}) copy-start(f32[4,16,256]{2,1,0:T(8,128)S(1)} %collective-permute-done.1.refs_3_) | copy-start | bytes 196612
  17.0 0.6 %copy-start.2 = (f32[4,16,256]{2,1,0:T(8,128)}, f32[4,16,256]{2,1,0:T(8,128)S(1)}, u32[]{:S(2)}) copy-start(f32[4,16,256]{2,1,0:T(8,128)S(1)} %collective-permute-done.2.refs_4_) | copy-start | bytes 196612
  17.0 0.6 %copy-start.3 = (f32[4,16,256]{2,1,0:T(8,128)}, f32[4,16,256]{2,1,0:T(8,128)S(1)}, u32[]{:S(2)}) copy-start(f32[4,16,256]{2,1,0:T(8,128)S(1)} %collective-permute-done.3.refs_5_) | copy-start | bytes 196612
  20.9 5.9 %collective-permute-start.4 = (f32[24,256]{1,0:T(8,128)}, f32[24,256]{1,0:T(8,128)S(1)}, u32[]{:S(2)}, u32[]{:S(2)}) collective-permute-start(f32[24,256]{1,0:T(8,128)} %get-tuple-element.10), channel_id=1, source_target_pairs={{0,8},{8,16},{16,24},{24,0},{1,9},{9,17},{17,25},{25,1},{2,10},{10... | collective-permute-start | bytes 73736 | tf_op jit(solution)/shard_map/ppermute | solution.py:306
  21.6 5.2 %collective-permute-start.5 = (f32[24,256]{1,0:T(8,128)}, f32[24,256]{1,0:T(8,128)S(1)}, u32[]{:S(2)}, u32[]{:S(2)}) collective-permute-start(f32[24,256]{1,0:T(8,128)} %get-tuple-element.11), channel_id=1, source_target_pairs={{0,16},{8,24},{16,0},{24,8},{1,17},{9,25},{17,1},{25,9},{2,18},{10... | collective-permute-start | bytes 73736 | tf_op jit(solution)/shard_map/ppermute | solution.py:306
  21.9 5.4 %collective-permute-start.6 = (f32[24,256]{1,0:T(8,128)}, f32[24,256]{1,0:T(8,128)S(1)}, u32[]{:S(2)}, u32[]{:S(2)}) collective-permute-start(f32[24,256]{1,0:T(8,128)} %get-tuple-element.12), channel_id=1, source_target_pairs={{0,24},{8,0},{16,8},{24,16},{1,25},{9,1},{17,9},{25,17},{2,26},{10... | collective-permute-start | bytes 73736 | tf_op jit(solution)/shard_map/ppermute | solution.py:306
  26.8 0.6 %copy-start.4 = (f32[24,256]{1,0:T(8,128)}, f32[24,256]{1,0:T(8,128)S(1)}, u32[]{:S(2)}) copy-start(f32[24,256]{1,0:T(8,128)S(1)} %collective-permute-done.4.refs_1_) | copy-start | bytes 73732
  26.8 0.6 %copy-start.5 = (f32[24,256]{1,0:T(8,128)}, f32[24,256]{1,0:T(8,128)S(1)}, u32[]{:S(2)}) copy-start(f32[24,256]{1,0:T(8,128)S(1)} %collective-permute-done.5.refs_2_) | copy-start | bytes 73732
  27.3 0.6 %copy-start.6 = (f32[24,256]{1,0:T(8,128)}, f32[24,256]{1,0:T(8,128)S(1)}, u32[]{:S(2)}) copy-start(f32[24,256]{1,0:T(8,128)S(1)} %collective-permute-done.6.refs_3_) | copy-start | bytes 73732

commit v13 on v10

--- a/solution.py
+++ b/solution.py
@@ -11,20 +11,22 @@
 INTERPRET = False
 
 
-def with_halo(block, axis, width):
+def with_halo(log_block, axis, width):
     count = lax.axis_size(axis)
+    low_edge = jnp.exp(2.0 * log_block[:width])
+    high_edge = jnp.exp(2.0 * log_block[-width:])
     if count == 2:
         place = lax.axis_index(axis)
-        send = jnp.where(place == 0, block[-width:], block[:width])
+        send = jnp.where(place == 0, high_edge, low_edge)
         got = lax.ppermute(send, axis, [(0, 1), (1, 0)])
         low = jnp.where(place == 1, got, jnp.zeros_like(got))
         high = jnp.where(place == 0, got, jnp.zeros_like(got))
     else:
         forward = [(i, i + 1) for i in range(count - 1)]
         backward = [(target, source) for source, target in forward]
-        low = lax.ppermute(block[-width:], axis, forward)
-        high = lax.ppermute(block[:width], axis, backward)
-    return jnp.concatenate([low, block, high])
+        low = lax.ppermute(high_edge, axis, forward)
+        high = lax.ppermute(low_edge, axis, backward)
+    return jnp.concatenate([low, jnp.exp(2.0 * log_block), high])
 
 
 def chain_kernel(*refs, aligned):
@@ -233,8 +235,7 @@
     chunk = quarter // time_count
     first = hyp_place * quarter + time_place * chunk
 
-    kappa_sq = jnp.exp(2.0 * log_kappa)
-    padded = with_halo(kappa_sq, "space", BAND)
+    padded = with_halo(log_kappa, "space", BAND)
 
     stacked = jnp.stack([roughness, coupling, obs_weight, observed])
     pieces = [

time: 34 us -> 34.1 us (level)
  no operation moved by 1% of the time
where the time goes in v13:
time: 34.1 us; the launch traced here: 33.8 us
  starting transfers between devices  12.4 us (36%)
  blocking collectives  5.61 us (16%)
  Pallas kernels  4.99 us (15%)
  local copies, waits for them, and re-layouts  4.05 us (12%)
  waiting for transfers between devices  3.33 us (10%)
  other arithmetic  2.63 us (8%)
  between operations  0.75 us (2%)
    ppermute x3, starting transfers between devices, per_device_body(): lax.ppermute(pieces[shift], 'tm', [(i, (i + shift) % time_count) for i in...  6.99 us
    all_gather x1, blocking collectives, per_device_body(): stats_full = lax.all_gather(stats_quarter, 'hyp', axis=1, tiled=True)  5.61 us
    ppermute x3, starting transfers between devices, per_device_body(): lax.ppermute(payload[shift], 'tm', [(i, (i + shift) % time_count) for i i...  3.88 us
    pallas_call x1, Pallas kernels, run_chain(): pl.pallas_call(functools.partial(chain_kernel, aligned=nodes.shape[1] !=...  3.53 us
    ppermute x3, waiting for transfers between devices, per_device_body(): lax.ppermute(payload[shift], 'tm', [(i, (i + shift) % time_count) for i i...  2.7 us
    ppermute x1, starting transfers between devices, with_halo(): got = lax.ppermute(send, axis, [(0, 1), (1, 0)])  1.53 us
    pallas_call x1, Pallas kernels, run_place(): pl.pallas_call(place_kernel, out_shape=(jax.ShapeDtypeStruct((rows, block...  1.46 us
    unnamed x20, local copies, waits for them, and re-layouts  1.4 us
  transfers between devices with their start and end apart: 7, of which 3 were waited for; matrix products, arithmetic and copies ran while one was open for 6% of the time, Pallas kernels for 0%

profile of v13, /device:TPU:0, one launch (start us, length us, event | category | flops | bytes accessed | tf_op | source)
XLA Modules:
  0.0 33.8 jit_solution(8280876283473764132)
XLA Ops:
  0.7 1.3 %pad_maximum_fusion = f32[4,16,4096]{2,1,0:T(8,128)S(1)} fusion(f32[1,16,4096]{2,1,0:T(8,128)} %bitcast.10, f32[1,16,4096]{2,1,0:T(8,128)} %bitcast.11, f32[1,16,4096]{2,1,0:T(8,128)} %bitcast.12, f32[1,16,4096]{2,1,0:T(8,128)} %bitcast.13), kind=kLoop, calls=%fused_computation | loop fusion | flops 786432 | bytes 2097152 | tf_op jit(solution)/shard_map/stack | solution.py:240
  1.9 0.0 copy-start.7
  1.9 0.0 copy-start
  2.0 0.7 %constant_dynamic-slice_fusion = (f32[4,16,256]{2,1,0:T(8,128)S(1)}, f32[4,16,256]{2,1,0:T(8,128)S(1)}, f32[4,16,256]{2,1,0:T(8,128)S(1)}, f32[4,16,256]{2,1,0:T(8,128)}) fusion(f32[4,16,4096]{2,1,0:T(8,128)S(1)} %pad_maximum_fusion, s32[]{:T(128)S(6)} %select_n.42, s32[]{:T(128)S(6)} %select_n.41, s32[]{:T(128)S(6)} %select_n.40, s32[]{:T(128)S(6)} %select_n.39), kind=kLoop, calls=%fused_computation.3 | loop fusion | bytes 524304 | tf_op jit(solution)/shard_map/dynamic_slice | solution.py:242
  2.6 3.1 %collective-permute-start.1 = (f32[4,16,256]{2,1,0:T(8,128)S(1)}, f32[4,16,256]{2,1,0:T(8,128)S(1)}, u32[]{:S(2)}, u32[]{:S(2)}) collective-permute-start(f32[4,16,256]{2,1,0:T(8,128)S(1)} %get-tuple-element.17), channel_id=1, source_target_pairs={{0,8},{8,16},{16,24},{24,0},{1,9},{9,17},{17,25},{25,1},{2,10},{10... | collective-permute-start | bytes 196616 | tf_op jit(solution)/shard_map/ppermute | solution.py:251
  5.7 2.6 %collective-permute-start.2 = (f32[4,16,256]{2,1,0:T(8,128)S(1)}, f32[4,16,256]{2,1,0:T(8,128)S(1)}, u32[]{:S(2)}, u32[]{:S(2)}) collective-permute-start(f32[4,16,256]{2,1,0:T(8,128)S(1)} %get-tuple-element.16), channel_id=1, source_target_pairs={{0,16},{8,24},{16,0},{24,8},{1,17},{9,25},{17,1},{25,9},{2,18},{10... | collective-permute-start | bytes 196616 | tf_op jit(solution)/shard_map/ppermute | solution.py:251
  8.3 1.3 %collective-permute-start.3 = (f32[4,16,256]{2,1,0:T(8,128)S(1)}, f32[4,16,256]{2,1,0:T(8,128)S(1)}, u32[]{:S(2)}, u32[]{:S(2)}) collective-permute-start(f32[4,16,256]{2,1,0:T(8,128)S(1)} %get-tuple-element.15), channel_id=1, source_target_pairs={{0,24},{8,0},{16,8},{24,16},{1,25},{9,1},{17,9},{25,17},{2,26},{10... | collective-permute-start | bytes 196616 | tf_op jit(solution)/shard_map/ppermute | solution.py:251
  9.6 0.1 broadcast_select_fusion.1
  9.7 1.5 %collective-permute-start = (f32[64]{0:T(128)S(1)}, f32[64]{0:T(128)S(1)}, u32[]{:S(2)}, u32[]{:S(2)}) collective-permute-start(f32[64]{0:T(128)S(1)} %broadcast_select_fusion.1), channel_id=1, source_target_pairs={{0,4},{4,0},{1,5},{5,1},{2,6},{6,2},{3,7},{7,3},{8,12},{12,8},{9,1... | collective-permute-start | bytes 776 | tf_op jit(solution)/shard_map/ppermute | solution.py:21
  11.2 0.6 %pad_add_fusion.refs_0_.place_ref = s32[2]{0:T(128)} fusion(s32[1]{0:T(128)} %bitcast.1, s32[1]{0:T(128)} %bitcast), kind=kLoop, calls=%fused_computation.10 | loop fusion | flops 2 | bytes 16 | tf_op jit(solution)/shard_map/stack | solution.py:258
  11.8 0.1 copy-done.8
  11.9 0.0 copy-done.9
  11.9 0.7 %pad_maximum_fusion.1.refs_3_ = f32[6,4096]{1,0:T(8,128)} fusion(f32[4,4096]{1,0:T(4,128)S(1)} %copy-done, f32[1,4096]{1,0:T(1,128)S(1)} %bitcast.15, f32[1,4096]{1,0:T(1,128)S(1)} %bitcast.16), kind=kLoop, calls=%fused_computation.1 | loop fusion | flops 49152 | bytes 196608 | tf_op jit(solution)/shard_map/concatenate | solution.py:260
  12.6 0.6 %collective-permute-done = f32[64]{0:T(128)S(1)} collective-permute-done((f32[64]{0:T(128)S(1)}, f32[64]{0:T(128)S(1)}, u32[]{:S(2)}, u32[]{:S(2)}) %collective-permute-start) | collective-permute-done | bytes 288 | tf_op jit(solution)/shard_map/ppermute | solution.py:21
  13.3 0.1 concatenate.6
  13.3 0.1 dynamic_slice.15
  13.4 0.6 %broadcast_in_dim.9.refs_2_ = f32[1,384]{1,0:T(1,128)} reshape(f32[384]{0:T(512)S(1)} %dynamic_slice.15) | data formatting | bytes 3072 | tf_op jit(solution)/shard_map/broadcast_in_dim | solution.py:259
  14.0 0.0 collective-permute-done.1.refs_6_
  14.0 0.6 %copy-done.1 = f32[4,16,256]{2,1,0:T(8,128)} copy-done((f32[4,16,256]{2,1,0:T(8,128)}, f32[4,16,256]{2,1,0:T(8,128)S(1)}, u32[]{:S(2)}) %copy-start.1) | copy-done | bytes 65560
  14.6 0.0 copy-done.2
  14.6 0.0 copy-done.3
  14.7 3.5 %shard_map.121 = (f32[24,256]{1,0:T(8,128)}, f32[24,256]{1,0:T(8,128)}, f32[24,256]{1,0:T(8,128)}, f32[24,256]{1,0:T(8,128)}) custom-call(s32[2]{0:T(128)} %pad_add_fusion.refs_0_.place_ref, f32[4]{0:T(128)} %refs_1_.1, f32[1,384]{1,0:T(1,128)} %broadcast_in_dim.9.refs_2_, f32[6,4096]{1,0:T(8,128)} %pad_maximum_fusion.1.refs_3_, s32[4,4096]{1,0:T(4,128)} %refs_4_.1, ...), custom_call_target="tpu_custom_call" | custom-call | tf_op jit(solution)/shard_map/pallas_call | solution.py:167
  18.2 0.7 %collective-permute-start.4 = (f32[24,256]{1,0:T(8,128)}, f32[24,256]{1,0:T(8,128)S(1)}, u32[]{:S(2)}, u32[]{:S(2)}) collective-permute-start(f32[24,256]{1,0:T(8,128)} %get-tuple-element.10), channel_id=1, source_target_pairs={{0,8},{8,16},{16,24},{24,0},{1,9},{9,17},{17,25},{25,1},{2,10},{10... | collective-permute-start | bytes 73736 | tf_op jit(solution)/shard_map/ppermute | solution.py:267
  18.9 1.8 %collective-permute-start.5 = (f32[24,256]{1,0:T(8,128)}, f32[24,256]{1,0:T(8,128)S(1)}, u32[]{:S(2)}, u32[]{:S(2)}) collective-permute-start(f32[24,256]{1,0:T(8,128)} %get-tuple-element.11), channel_id=1, source_target_pairs={{0,16},{8,24},{16,0},{24,8},{1,17},{9,25},{17,1},{25,9},{2,18},{10... | collective-permute-start | bytes 73736 | tf_op jit(solution)/shard_map/ppermute | solution.py:267
  20.8 1.3 %collective-permute-start.6 = (f32[24,256]{1,0:T(8,128)}, f32[24,256]{1,0:T(8,128)S(1)}, u32[]{:S(2)}, u32[]{:S(2)}) collective-permute-start(f32[24,256]{1,0:T(8,128)} %get-tuple-element.12), channel_id=1, source_target_pairs={{0,24},{8,0},{16,8},{24,16},{1,25},{9,1},{17,9},{25,17},{2,26},{10... | collective-permute-start | bytes 73736 | tf_op jit(solution)/shard_map/ppermute | solution.py:267
  22.1 2.0 %collective-permute-done.4.refs_1_ = f32[24,256]{1,0:T(8,128)S(1)} collective-permute-done((f32[24,256]{1,0:T(8,128)}, f32[24,256]{1,0:T(8,128)S(1)}, u32[]{:S(2)}, u32[]{:S(2)}) %collective-permute-start.4) | collective-permute-done | bytes 24608 | tf_op jit(solution)/shard_map/ppermute | solution.py:267
  24.2 0.6 %collective-permute-done.6.refs_3_ = f32[24,256]{1,0:T(8,128)S(1)} collective-permute-done((f32[24,256]{1,0:T(8,128)}, f32[24,256]{1,0:T(8,128)S(1)}, u32[]{:S(2)}, u32[]{:S(2)}) %collective-permute-start.6) | collective-permute-done | bytes 24608 | tf_op jit(solution)/shard_map/ppermute | solution.py:267
  24.8 0.6 %copy-done.6 = f32[24,256]{1,0:T(8,128)} copy-done((f32[24,256]{1,0:T(8,128)}, f32[24,256]{1,0:T(8,128)S(1)}, u32[]{:S(2)}) %copy-start.6) | copy-done | bytes 24600
  25.4 1.5 %shard_map.122 = (f32[16,1024]{1,0:T(8,128)}, f32[8,1024]{1,0:T(8,128)}) custom-call(s32[2]{0:T(128)} %pad_add_fusion.refs_0_.place_ref, f32[24,256]{1,0:T(8,128)} %get-tuple-element.9.refs_0_, f32[24,256]{1,0:T(8,128)} %copy-done.4, f32[24,256]{1,0:T(8,128)} %copy-done.5, f32[24,256]{1,0:T(8,128)} %copy-done.6), custom_call_target="tpu_custom_call" | custom-call | tf_op jit(solution)/shard_map/pallas_call | solution.py:205
  26.9 5.6 %all_gather.3 = f32[5,4096]{1,0:T(8,128)S(1)} all-gather(f32[5,1024]{1,0:T(8,128)} %bitcast.14), channel_id=1, replica_groups=mesh['tm'=4,'space'=2,'hyp'=4] {'hyp'}, dimensions={1}, use_global_device_ids=true | all-gather | bytes 102400 | tf_op jit(solution)/shard_map/all_gather | solution.py:285
  32.5 0.6 %slice.21 = f32[4,4096]{1,0:T(4,128)} slice(f32[5,4096]{1,0:T(8,128)S(1)} %all_gather.3), slice={[1:5], [0:4096]} | slice | bytes 131072 | tf_op jit(solution)/shard_map/slice | solution.py:286
  33.2 0.6 %slice.20 = f32[1,4096]{1,0:T(1,128)} slice(f32[5,4096]{1,0:T(8,128)S(1)} %all_gather.3), slice={[0:1], [0:4096]} | slice | bytes 32768 | tf_op jit(solution)/shard_map/slice | solution.py:286
  (17 shorter events, 0.0 us)
Async XLA Ops:
  1.9 7.7 %copy-start.7 = (f32[4096]{0:T(1024)S(1)}, f32[4096]{0:T(1024)}, u32[]{:S(2)}) copy-start(f32[4096]{0:T(1024)} %param.10) | copy-start | bytes 49156
  1.9 9.9 %copy-start = (f32[4,4096]{1,0:T(4,128)S(1)}, f32[4,4096]{1,0:T(4,128)}, u32[]{:S(2)}) copy-start(f32[4,4096]{1,0:T(4,128)} %param.13) | copy-start | bytes 196612
  2.6 11.4 %collective-permute-start.1 = (f32[4,16,256]{2,1,0:T(8,128)S(1)}, f32[4,16,256]{2,1,0:T(8,128)S(1)}, u32[]{:S(2)}, u32[]{:S(2)}) collective-permute-start(f32[4,16,256]{2,1,0:T(8,128)S(1)} %get-tuple-element.17), channel_id=1, source_target_pairs={{0,8},{8,16},{16,24},{24,0},{1,9},{9,17},{17,25},{25,1},{2,10},{10... | collective-permute-start | bytes 196616 | tf_op jit(solution)/shard_map/ppermute | solution.py:251
  5.7 8.3 %collective-permute-start.2 = (f32[4,16,256]{2,1,0:T(8,128)S(1)}, f32[4,16,256]{2,1,0:T(8,128)S(1)}, u32[]{:S(2)}, u32[]{:S(2)}) collective-permute-start(f32[4,16,256]{2,1,0:T(8,128)S(1)} %get-tuple-element.16), channel_id=1, source_target_pairs={{0,16},{8,24},{16,0},{24,8},{1,17},{9,25},{17,1},{25,9},{2,18},{10... | collective-permute-start | bytes 196616 | tf_op jit(solution)/shard_map/ppermute | solution.py:251
  8.3 5.8 %collective-permute-start.3 = (f32[4,16,256]{2,1,0:T(8,128)S(1)}, f32[4,16,256]{2,1,0:T(8,128)S(1)}, u32[]{:S(2)}, u32[]{:S(2)}) collective-permute-start(f32[4,16,256]{2,1,0:T(8,128)S(1)} %get-tuple-element.15), channel_id=1, source_target_pairs={{0,24},{8,0},{16,8},{24,16},{1,25},{9,1},{17,9},{25,17},{2,26},{10... | collective-permute-start | bytes 196616 | tf_op jit(solution)/shard_map/ppermute | solution.py:251
  9.7 3.6 %collective-permute-start = (f32[64]{0:T(128)S(1)}, f32[64]{0:T(128)S(1)}, u32[]{:S(2)}, u32[]{:S(2)}) collective-permute-start(f32[64]{0:T(128)S(1)} %broadcast_select_fusion.1), channel_id=1, source_target_pairs={{0,4},{4,0},{1,5},{5,1},{2,6},{6,2},{3,7},{7,3},{8,12},{12,8},{9,1... | collective-permute-start | bytes 776 | tf_op jit(solution)/shard_map/ppermute | solution.py:21
  11.2 0.7 %copy-start.8 = (f32[4096]{0:T(1024)S(1)}, f32[4096]{0:T(1024)}, u32[]{:S(2)}) copy-start(f32[4096]{0:T(1024)} %param.12) | copy-start | bytes 49156
  11.2 0.7 %copy-start.9 = (f32[4096]{0:T(1024)S(1)}, f32[4096]{0:T(1024)}, u32[]{:S(2)}) copy-start(f32[4096]{0:T(1024)} %param.11) | copy-start | bytes 49156
  14.0 0.6 %copy-start.1 = (f32[4,16,256]{2,1,0:T(8,128)}, f32[4,16,256]{2,1,0:T(8,128)S(1)}, u32[]{:S(2)}) copy-start(f32[4,16,256]{2,1,0:T(8,128)S(1)} %collective-permute-done.1.refs_6_) | copy-start | bytes 196612
  14.0 0.6 %copy-start.2 = (f32[4,16,256]{2,1,0:T(8,128)}, f32[4,16,256]{2,1,0:T(8,128)S(1)}, u32[]{:S(2)}) copy-start(f32[4,16,256]{2,1,0:T(8,128)S(1)} %collective-permute-done.2.refs_7_) | copy-start | bytes 196612
  14.0 0.7 %copy-start.3 = (f32[4,16,256]{2,1,0:T(8,128)}, f32[4,16,256]{2,1,0:T(8,128)S(1)}, u32[]{:S(2)}) copy-start(f32[4,16,256]{2,1,0:T(8,128)S(1)} %collective-permute-done.3.refs_8_) | copy-start | bytes 196612
  18.2 5.9 %collective-permute-start.4 = (f32[24,256]{1,0:T(8,128)}, f32[24,256]{1,0:T(8,128)S(1)}, u32[]{:S(2)}, u32[]{:S(2)}) collective-permute-start(f32[24,256]{1,0:T(8,128)} %get-tuple-element.10), channel_id=1, source_target_pairs={{0,8},{8,16},{16,24},{24,0},{1,9},{9,17},{17,25},{25,1},{2,10},{10... | collective-permute-start | bytes 73736 | tf_op jit(solution)/shard_map/ppermute | solution.py:267
  18.9 5.2 %collective-permute-start.5 = (f32[24,256]{1,0:T(8,128)}, f32[24,256]{1,0:T(8,128)S(1)}, u32[]{:S(2)}, u32[]{:S(2)}) collective-permute-start(f32[24,256]{1,0:T(8,128)} %get-tuple-element.11), channel_id=1, source_target_pairs={{0,16},{8,24},{16,0},{24,8},{1,17},{9,25},{17,1},{25,9},{2,18},{10... | collective-permute-start | bytes 73736 | tf_op jit(solution)/shard_map/ppermute | solution.py:267
  20.8 4.0 %collective-permute-start.6 = (f32[24,256]{1,0:T(8,128)}, f32[24,256]{1,0:T(8,128)S(1)}, u32[]{:S(2)}, u32[]{:S(2)}) collective-permute-start(f32[24,256]{1,0:T(8,128)} %get-tuple-element.12), channel_id=1, source_target_pairs={{0,24},{8,0},{16,8},{24,16},{1,25},{9,1},{17,9},{25,17},{2,26},{10... | collective-permute-start | bytes 73736 | tf_op jit(solution)/shard_map/ppermute | solution.py:267
  24.1 0.7 %copy-start.4 = (f32[24,256]{1,0:T(8,128)}, f32[24,256]{1,0:T(8,128)S(1)}, u32[]{:S(2)}) copy-start(f32[24,256]{1,0:T(8,128)S(1)} %collective-permute-done.4.refs_1_) | copy-start | bytes 73732
  24.2 0.7 %copy-start.5 = (f32[24,256]{1,0:T(8,128)}, f32[24,256]{1,0:T(8,128)S(1)}, u32[]{:S(2)}) copy-start(f32[24,256]{1,0:T(8,128)S(1)} %collective-permute-done.5.refs_2_) | copy-start | bytes 73732
  24.8 0.6 %copy-start.6 = (f32[24,256]{1,0:T(8,128)}, f32[24,256]{1,0:T(8,128)S(1)}, u32[]{:S(2)}) copy-start(f32[24,256]{1,0:T(8,128)S(1)} %collective-permute-done.6.refs_3_) | copy-start | bytes 73732

commit v14 on v10

--- a/solution.py
+++ b/solution.py
@@ -55,13 +55,23 @@
     span = window.shape[1]
     near_off = offsets_ref[...]
     ones = jnp.ones((1, width), jnp.float32)
-    nearby = jnp.zeros(near_off.shape, jnp.float32)
+    neigh = near_off.shape[0]
+    paired = jnp.concatenate(
+        [
+            jnp.broadcast_to(window, (neigh, span)),
+            jnp.broadcast_to(pltpu.roll(window, span - 1, 1), (neigh, span)),
+        ],
+        axis=0,
+    )
+    paired_off = jnp.concatenate([near_off, near_off - 1], axis=0)
+    both = jnp.zeros(paired_off.shape, jnp.float32)
     own_kappa = None
-    for shift in range(-BAND, BAND + 1):
-        moved = pltpu.roll(window, (span - BAND - shift) % span, 1)[:, :width]
+    for shift in range(-BAND, BAND + 1, 2):
+        moved = pltpu.roll(paired, (span - BAND - shift) % span, 1)[:, :width]
         if shift == 0:
-            own_kappa = moved
-        nearby = jnp.where(near_off == shift, moved, nearby)
+            own_kappa = moved[0:1]
+        both = jnp.where(paired_off == shift, moved, both)
+    nearby = both[:neigh] + both[neigh:]
     weights = nodes_ref[2:6, :]
     edge_sum = (
         weights[0:1] * nearby[0:1]
@@ -98,16 +108,18 @@
             pivots = diagonal - offdiag * offdiag * inv
             ratios = offdiag * inv
             rr = ratios * ratios
-            t0 = rr * t0 + 2.0 * prior - 4.0 * offdiag * ratios
-            t1 = rr * t1 + prior - 2.0 * offdiag * ratios
+            od_r = offdiag * ratios
+            t0 = rr * t0 + 2.0 * prior - 4.0 * od_r
+            t1 = rr * t1 + prior - 2.0 * od_r
             t2 = rr * t2 + qs * rough - two_ls2 * offdiag * ratios
             t3 = rr * t3 + nugget
             solved = obs - ratios * solved
             inv = 1.0 / pivots
-            c0 = c0 + 0.5 * t0 * inv
-            c1 = c1 + 0.5 * t1 * inv
-            c2 = c2 + 0.5 * t2 * inv
-            c3 = c3 + 0.5 * t3 * inv
+            half_inv = 0.5 * inv
+            c0 = c0 + t0 * half_inv
+            c1 = c1 + t1 * half_inv
+            c2 = c2 + t2 * half_inv
+            c3 = c3 + t3 * half_inv
             logs = logs + jnp.log(pivots)
             piv_ref[block, pl.ds(t, 1), :] = inv
             slv_ref[block, pl.ds(t, 1), :] = solved
@@ -129,8 +141,10 @@
             nugget = ns * weight
             offdiag = mps * coup
             values = (slv_ref[block, pl.ds(t, 1), :] - following) * piv_ref[block, pl.ds(t, 1), :]
-            q0 = q0 + 2.0 * prior * values * values + 4.0 * values * following
-            q1 = q1 + prior * values * values + 2.0 * values * following
+            pvv = prior * values * values
+            vf = values * following
+            q0 = q0 + 2.0 * pvv + 4.0 * vf
+            q1 = q1 + pvv + 2.0 * vf
             q2 = q2 + qs * rough * values * values + two_ls2 * values * following
             q3 = q3 + nugget * values * values
             out_ref[block, pl.ds(t, 1), :] = values

time: 34 us -> 33.9 us (level)
  no operation moved by 1% of the time
where the time goes in v14:
time: 33.9 us; the launch traced here: 33.6 us
  starting transfers between devices  12.4 us (37%)
  blocking collectives  5.61 us (17%)
  Pallas kernels  4.86 us (14%)
  local copies, waits for them, and re-layouts  3.94 us (12%)
  waiting for transfers between devices  3.45 us (10%)
  other arithmetic  2.63 us (8%)
  between operations  0.75 us (2%)
    ppermute x3, starting transfers between devices, per_device_body(): lax.ppermute(pieces[shift], 'tm', [(i, (i + shift) % time_count) for i in...  6.99 us
    all_gather x1, blocking collectives, per_device_body(): stats_full = lax.all_gather(stats_quarter, 'hyp', axis=1, tiled=True)  5.61 us
    ppermute x3, starting transfers between devices, per_device_body(): lax.ppermute(payload[shift], 'tm', [(i, (i + shift) % time_count) for i i...  3.88 us
    pallas_call x1, Pallas kernels, run_chain(): pl.pallas_call(functools.partial(chain_kernel, aligned=nodes.shape[1] !=...  3.4 us
    ppermute x3, waiting for transfers between devices, per_device_body(): lax.ppermute(payload[shift], 'tm', [(i, (i + shift) % time_count) for i i...  2.69 us
    ppermute x1, starting transfers between devices, with_halo(): got = lax.ppermute(send, axis, [(0, 1), (1, 0)])  1.53 us
    pallas_call x1, Pallas kernels, run_place(): pl.pallas_call(place_kernel, out_shape=(jax.ShapeDtypeStruct((rows, block...  1.46 us
    unnamed x20, local copies, waits for them, and re-layouts  1.29 us
  transfers between devices with their start and end apart: 7, of which 3 were waited for; matrix products, arithmetic and copies ran while one was open for 6% of the time, Pallas kernels for 0%

profile of v14, /device:TPU:0, one launch (start us, length us, event | category | flops | bytes accessed | tf_op | source)
XLA Modules:
  0.0 33.6 jit_solution(10620903306967453870)
XLA Ops:
  0.7 1.3 %pad_maximum_fusion = f32[4,16,4096]{2,1,0:T(8,128)S(1)} fusion(f32[1,16,4096]{2,1,0:T(8,128)} %bitcast.10, f32[1,16,4096]{2,1,0:T(8,128)} %bitcast.11, f32[1,16,4096]{2,1,0:T(8,128)} %bitcast.12, f32[1,16,4096]{2,1,0:T(8,128)} %bitcast.13), kind=kLoop, calls=%fused_computation | loop fusion | flops 786432 | bytes 2097152 | tf_op jit(solution)/shard_map/stack | solution.py:253
  1.9 0.0 copy-start.9
  1.9 0.0 copy-start
  2.0 0.7 %constant_dynamic-slice_fusion = (f32[4,16,256]{2,1,0:T(8,128)S(1)}, f32[4,16,256]{2,1,0:T(8,128)S(1)}, f32[4,16,256]{2,1,0:T(8,128)S(1)}, f32[4,16,256]{2,1,0:T(8,128)}) fusion(f32[4,16,4096]{2,1,0:T(8,128)S(1)} %pad_maximum_fusion, s32[]{:T(128)S(6)} %select_n.42, s32[]{:T(128)S(6)} %select_n.41, s32[]{:T(128)S(6)} %select_n.40, s32[]{:T(128)S(6)} %select_n.39), kind=kLoop, calls=%fused_computation.3 | loop fusion | bytes 524304 | tf_op jit(solution)/shard_map/dynamic_slice | solution.py:255
  2.6 3.1 %collective-permute-start.1 = (f32[4,16,256]{2,1,0:T(8,128)S(1)}, f32[4,16,256]{2,1,0:T(8,128)S(1)}, u32[]{:S(2)}, u32[]{:S(2)}) collective-permute-start(f32[4,16,256]{2,1,0:T(8,128)S(1)} %get-tuple-element.17), channel_id=1, source_target_pairs={{0,8},{8,16},{16,24},{24,0},{1,9},{9,17},{17,25},{25,1},{2,10},{10... | collective-permute-start | bytes 196616 | tf_op jit(solution)/shard_map/ppermute | solution.py:264
  5.7 2.6 %collective-permute-start.2 = (f32[4,16,256]{2,1,0:T(8,128)S(1)}, f32[4,16,256]{2,1,0:T(8,128)S(1)}, u32[]{:S(2)}, u32[]{:S(2)}) collective-permute-start(f32[4,16,256]{2,1,0:T(8,128)S(1)} %get-tuple-element.16), channel_id=1, source_target_pairs={{0,16},{8,24},{16,0},{24,8},{1,17},{9,25},{17,1},{25,9},{2,18},{10... | collective-permute-start | bytes 196616 | tf_op jit(solution)/shard_map/ppermute | solution.py:264
  8.3 1.3 %collective-permute-start.3 = (f32[4,16,256]{2,1,0:T(8,128)S(1)}, f32[4,16,256]{2,1,0:T(8,128)S(1)}, u32[]{:S(2)}, u32[]{:S(2)}) collective-permute-start(f32[4,16,256]{2,1,0:T(8,128)S(1)} %get-tuple-element.15), channel_id=1, source_target_pairs={{0,24},{8,0},{16,8},{24,16},{1,25},{9,1},{17,9},{25,17},{2,26},{10... | collective-permute-start | bytes 196616 | tf_op jit(solution)/shard_map/ppermute | solution.py:264
  9.6 0.1 broadcast_select_fusion.1
  9.7 1.5 %collective-permute-start = (f32[64]{0:T(128)S(1)}, f32[64]{0:T(128)S(1)}, u32[]{:S(2)}, u32[]{:S(2)}) collective-permute-start(f32[64]{0:T(128)S(1)} %broadcast_select_fusion.1), channel_id=1, source_target_pairs={{0,4},{4,0},{1,5},{5,1},{2,6},{6,2},{3,7},{7,3},{8,12},{12,8},{9,1... | collective-permute-start | bytes 776 | tf_op jit(solution)/shard_map/ppermute | solution.py:19
  11.2 0.6 %pad_add_fusion.refs_0_.place_ref = s32[2]{0:T(128)} fusion(s32[1]{0:T(128)} %bitcast.1, s32[1]{0:T(128)} %bitcast), kind=kLoop, calls=%fused_computation.10 | loop fusion | flops 2 | bytes 16 | tf_op jit(solution)/shard_map/stack | solution.py:271
  11.8 0.7 %pad_maximum_fusion.1.refs_3_ = f32[6,4096]{1,0:T(8,128)} fusion(f32[4,4096]{1,0:T(4,128)S(1)} %copy-done, f32[1,4096]{1,0:T(1,128)S(1)} %bitcast.15, f32[1,4096]{1,0:T(1,128)S(1)} %bitcast.16), kind=kLoop, calls=%fused_computation.1 | loop fusion | flops 49152 | bytes 196608 | tf_op jit(solution)/shard_map/concatenate | solution.py:273
  12.5 0.8 %collective-permute-done = f32[64]{0:T(128)S(1)} collective-permute-done((f32[64]{0:T(128)S(1)}, f32[64]{0:T(128)S(1)}, u32[]{:S(2)}, u32[]{:S(2)}) %collective-permute-start) | collective-permute-done | bytes 288 | tf_op jit(solution)/shard_map/ppermute | solution.py:19
  13.3 0.1 concatenate.6
  13.4 0.1 dynamic_slice.15
  13.4 0.6 %broadcast_in_dim.9.refs_2_ = f32[1,384]{1,0:T(1,128)} reshape(f32[384]{0:T(512)S(1)} %dynamic_slice.15) | data formatting | bytes 3072 | tf_op jit(solution)/shard_map/broadcast_in_dim | solution.py:272
  14.0 0.0 collective-permute-done.1.refs_6_
  14.0 0.0 collective-permute-done.2.refs_7_
  14.1 0.6 %copy-done.1 = f32[4,16,256]{2,1,0:T(8,128)} copy-done((f32[4,16,256]{2,1,0:T(8,128)}, f32[4,16,256]{2,1,0:T(8,128)S(1)}, u32[]{:S(2)}) %copy-start.1) | copy-done | bytes 65560
  14.6 0.0 copy-done.2
  14.7 0.0 copy-done.3
  14.7 3.4 %shard_map.121 = (f32[24,256]{1,0:T(8,128)}, f32[24,256]{1,0:T(8,128)}, f32[24,256]{1,0:T(8,128)}, f32[24,256]{1,0:T(8,128)}) custom-call(s32[2]{0:T(128)} %pad_add_fusion.refs_0_.place_ref, f32[4]{0:T(128)} %refs_1_.1, f32[1,384]{1,0:T(1,128)} %broadcast_in_dim.9.refs_2_, f32[6,4096]{1,0:T(8,128)} %pad_maximum_fusion.1.refs_3_, s32[4,4096]{1,0:T(4,128)} %refs_4_.1, ...), custom_call_target="tpu_custom_call" | custom-call | tf_op jit(solution)/shard_map/pallas_call | solution.py:179
  18.1 0.7 %collective-permute-start.4 = (f32[24,256]{1,0:T(8,128)}, f32[24,256]{1,0:T(8,128)S(1)}, u32[]{:S(2)}, u32[]{:S(2)}) collective-permute-start(f32[24,256]{1,0:T(8,128)} %get-tuple-element.10), channel_id=1, source_target_pairs={{0,8},{8,16},{16,24},{24,0},{1,9},{9,17},{17,25},{25,1},{2,10},{10... | collective-permute-start | bytes 73736 | tf_op jit(solution)/shard_map/ppermute | solution.py:280
  18.8 1.8 %collective-permute-start.5 = (f32[24,256]{1,0:T(8,128)}, f32[24,256]{1,0:T(8,128)S(1)}, u32[]{:S(2)}, u32[]{:S(2)}) collective-permute-start(f32[24,256]{1,0:T(8,128)} %get-tuple-element.11), channel_id=1, source_target_pairs={{0,16},{8,24},{16,0},{24,8},{1,17},{9,25},{17,1},{25,9},{2,18},{10... | collective-permute-start | bytes 73736 | tf_op jit(solution)/shard_map/ppermute | solution.py:280
  20.6 1.3 %collective-permute-start.6 = (f32[24,256]{1,0:T(8,128)}, f32[24,256]{1,0:T(8,128)S(1)}, u32[]{:S(2)}, u32[]{:S(2)}) collective-permute-start(f32[24,256]{1,0:T(8,128)} %get-tuple-element.12), channel_id=1, source_target_pairs={{0,24},{8,0},{16,8},{24,16},{1,25},{9,1},{17,9},{25,17},{2,26},{10... | collective-permute-start | bytes 73736 | tf_op jit(solution)/shard_map/ppermute | solution.py:280
  22.0 2.0 %collective-permute-done.4.refs_1_ = f32[24,256]{1,0:T(8,128)S(1)} collective-permute-done((f32[24,256]{1,0:T(8,128)}, f32[24,256]{1,0:T(8,128)S(1)}, u32[]{:S(2)}, u32[]{:S(2)}) %collective-permute-start.4) | collective-permute-done | bytes 24608 | tf_op jit(solution)/shard_map/ppermute | solution.py:280
  24.0 0.0 collective-permute-done.5.refs_2_
  24.0 0.6 %collective-permute-done.6.refs_3_ = f32[24,256]{1,0:T(8,128)S(1)} collective-permute-done((f32[24,256]{1,0:T(8,128)}, f32[24,256]{1,0:T(8,128)S(1)}, u32[]{:S(2)}, u32[]{:S(2)}) %collective-permute-start.6) | collective-permute-done | bytes 24608 | tf_op jit(solution)/shard_map/ppermute | solution.py:280
  24.7 0.6 %copy-done.6 = f32[24,256]{1,0:T(8,128)} copy-done((f32[24,256]{1,0:T(8,128)}, f32[24,256]{1,0:T(8,128)S(1)}, u32[]{:S(2)}) %copy-start.6) | copy-done | bytes 24600
  25.3 1.5 %shard_map.122 = (f32[16,1024]{1,0:T(8,128)}, f32[8,1024]{1,0:T(8,128)}) custom-call(s32[2]{0:T(128)} %pad_add_fusion.refs_0_.place_ref, f32[24,256]{1,0:T(8,128)} %get-tuple-element.9.refs_0_, f32[24,256]{1,0:T(8,128)} %copy-done.4, f32[24,256]{1,0:T(8,128)} %copy-done.5, f32[24,256]{1,0:T(8,128)} %copy-done.6), custom_call_target="tpu_custom_call" | custom-call | tf_op jit(solution)/shard_map/pallas_call | solution.py:217
  26.8 5.6 %all_gather.3 = f32[5,4096]{1,0:T(8,128)S(1)} all-gather(f32[5,1024]{1,0:T(8,128)} %bitcast.14), channel_id=1, replica_groups=mesh['tm'=4,'space'=2,'hyp'=4] {'hyp'}, dimensions={1}, use_global_device_ids=true | all-gather | bytes 102400 | tf_op jit(solution)/shard_map/all_gather | solution.py:298
  32.4 0.6 %slice.23 = f32[4,4096]{1,0:T(4,128)} slice(f32[5,4096]{1,0:T(8,128)S(1)} %all_gather.3), slice={[1:5], [0:4096]} | slice | bytes 131072 | tf_op jit(solution)/shard_map/slice | solution.py:299
  33.0 0.6 %slice.22 = f32[1,4096]{1,0:T(1,128)} slice(f32[5,4096]{1,0:T(8,128)S(1)} %all_gather.3), slice={[0:1], [0:4096]} | slice | bytes 32768 | tf_op jit(solution)/shard_map/slice | solution.py:299
  (17 shorter events, 0.0 us)
Async XLA Ops:
  1.9 7.7 %copy-start.9 = (f32[4096]{0:T(1024)S(1)}, f32[4096]{0:T(1024)}, u32[]{:S(2)}) copy-start(f32[4096]{0:T(1024)} %param.10) | copy-start | bytes 49156
  1.9 9.9 %copy-start = (f32[4,4096]{1,0:T(4,128)S(1)}, f32[4,4096]{1,0:T(4,128)}, u32[]{:S(2)}) copy-start(f32[4,4096]{1,0:T(4,128)} %param.13) | copy-start | bytes 196612
  2.6 11.4 %collective-permute-start.1 = (f32[4,16,256]{2,1,0:T(8,128)S(1)}, f32[4,16,256]{2,1,0:T(8,128)S(1)}, u32[]{:S(2)}, u32[]{:S(2)}) collective-permute-start(f32[4,16,256]{2,1,0:T(8,128)S(1)} %get-tuple-element.17), channel_id=1, source_target_pairs={{0,8},{8,16},{16,24},{24,0},{1,9},{9,17},{17,25},{25,1},{2,10},{10... | collective-permute-start | bytes 196616 | tf_op jit(solution)/shard_map/ppermute | solution.py:264
  5.7 8.3 %collective-permute-start.2 = (f32[4,16,256]{2,1,0:T(8,128)S(1)}, f32[4,16,256]{2,1,0:T(8,128)S(1)}, u32[]{:S(2)}, u32[]{:S(2)}) collective-permute-start(f32[4,16,256]{2,1,0:T(8,128)S(1)} %get-tuple-element.16), channel_id=1, source_target_pairs={{0,16},{8,24},{16,0},{24,8},{1,17},{9,25},{17,1},{25,9},{2,18},{10... | collective-permute-start | bytes 196616 | tf_op jit(solution)/shard_map/ppermute | solution.py:264
  8.3 5.8 %collective-permute-start.3 = (f32[4,16,256]{2,1,0:T(8,128)S(1)}, f32[4,16,256]{2,1,0:T(8,128)S(1)}, u32[]{:S(2)}, u32[]{:S(2)}) collective-permute-start(f32[4,16,256]{2,1,0:T(8,128)S(1)} %get-tuple-element.15), channel_id=1, source_target_pairs={{0,24},{8,0},{16,8},{24,16},{1,25},{9,1},{17,9},{25,17},{2,26},{10... | collective-permute-start | bytes 196616 | tf_op jit(solution)/shard_map/ppermute | solution.py:264
  9.6 2.2 %copy-start.7 = (f32[4096]{0:T(1024)S(1)}, f32[4096]{0:T(1024)}, u32[]{:S(2)}) copy-start(f32[4096]{0:T(1024)} %param.12) | copy-start | bytes 49156
  9.6 2.2 %copy-start.8 = (f32[4096]{0:T(1024)S(1)}, f32[4096]{0:T(1024)}, u32[]{:S(2)}) copy-start(f32[4096]{0:T(1024)} %param.11) | copy-start | bytes 49156
  9.7 3.6 %collective-permute-start = (f32[64]{0:T(128)S(1)}, f32[64]{0:T(128)S(1)}, u32[]{:S(2)}, u32[]{:S(2)}) collective-permute-start(f32[64]{0:T(128)S(1)} %broadcast_select_fusion.1), channel_id=1, source_target_pairs={{0,4},{4,0},{1,5},{5,1},{2,6},{6,2},{3,7},{7,3},{8,12},{12,8},{9,1... | collective-permute-start | bytes 776 | tf_op jit(solution)/shard_map/ppermute | solution.py:19
  14.0 0.6 %copy-start.1 = (f32[4,16,256]{2,1,0:T(8,128)}, f32[4,16,256]{2,1,0:T(8,128)S(1)}, u32[]{:S(2)}) copy-start(f32[4,16,256]{2,1,0:T(8,128)S(1)} %collective-permute-done.1.refs_6_) | copy-start | bytes 196612
  14.0 0.6 %copy-start.2 = (f32[4,16,256]{2,1,0:T(8,128)}, f32[4,16,256]{2,1,0:T(8,128)S(1)}, u32[]{:S(2)}) copy-start(f32[4,16,256]{2,1,0:T(8,128)S(1)} %collective-permute-done.2.refs_7_) | copy-start | bytes 196612
  14.0 0.7 %copy-start.3 = (f32[4,16,256]{2,1,0:T(8,128)}, f32[4,16,256]{2,1,0:T(8,128)S(1)}, u32[]{:S(2)}) copy-start(f32[4,16,256]{2,1,0:T(8,128)S(1)} %collective-permute-done.3.refs_8_) | copy-start | bytes 196612
  18.1 5.9 %collective-permute-start.4 = (f32[24,256]{1,0:T(8,128)}, f32[24,256]{1,0:T(8,128)S(1)}, u32[]{:S(2)}, u32[]{:S(2)}) collective-permute-start(f32[24,256]{1,0:T(8,128)} %get-tuple-element.10), channel_id=1, source_target_pairs={{0,8},{8,16},{16,24},{24,0},{1,9},{9,17},{17,25},{25,1},{2,10},{10... | collective-permute-start | bytes 73736 | tf_op jit(solution)/shard_map/ppermute | solution.py:280
  18.8 5.2 %collective-permute-start.5 = (f32[24,256]{1,0:T(8,128)}, f32[24,256]{1,0:T(8,128)S(1)}, u32[]{:S(2)}, u32[]{:S(2)}) collective-permute-start(f32[24,256]{1,0:T(8,128)} %get-tuple-element.11), channel_id=1, source_target_pairs={{0,16},{8,24},{16,0},{24,8},{1,17},{9,25},{17,1},{25,9},{2,18},{10... | collective-permute-start | bytes 73736 | tf_op jit(solution)/shard_map/ppermute | solution.py:280
  20.6 4.0 %collective-permute-start.6 = (f32[24,256]{1,0:T(8,128)}, f32[24,256]{1,0:T(8,128)S(1)}, u32[]{:S(2)}, u32[]{:S(2)}) collective-permute-start(f32[24,256]{1,0:T(8,128)} %get-tuple-element.12), channel_id=1, source_target_pairs={{0,24},{8,0},{16,8},{24,16},{1,25},{9,1},{17,9},{25,17},{2,26},{10... | collective-permute-start | bytes 73736 | tf_op jit(solution)/shard_map/ppermute | solution.py:280
  24.0 0.6 %copy-start.4 = (f32[24,256]{1,0:T(8,128)}, f32[24,256]{1,0:T(8,128)S(1)}, u32[]{:S(2)}) copy-start(f32[24,256]{1,0:T(8,128)S(1)} %collective-permute-done.4.refs_1_) | copy-start | bytes 73732
  24.0 0.6 %copy-start.5 = (f32[24,256]{1,0:T(8,128)}, f32[24,256]{1,0:T(8,128)S(1)}, u32[]{:S(2)}) copy-start(f32[24,256]{1,0:T(8,128)S(1)} %collective-permute-done.5.refs_2_) | copy-start | bytes 73732
  24.7 0.6 %copy-start.6 = (f32[24,256]{1,0:T(8,128)}, f32[24,256]{1,0:T(8,128)S(1)}, u32[]{:S(2)}) copy-start(f32[24,256]{1,0:T(8,128)S(1)} %collective-permute-done.6.refs_3_) | copy-start | bytes 73732

commit v15 on v14

--- a/solution.py
+++ b/solution.py
@@ -108,18 +108,16 @@
             pivots = diagonal - offdiag * offdiag * inv
             ratios = offdiag * inv
             rr = ratios * ratios
-            od_r = offdiag * ratios
-            t0 = rr * t0 + 2.0 * prior - 4.0 * od_r
-            t1 = rr * t1 + prior - 2.0 * od_r
+            t0 = rr * t0 + 2.0 * prior - 4.0 * offdiag * ratios
+            t1 = rr * t1 + prior - 2.0 * offdiag * ratios
             t2 = rr * t2 + qs * rough - two_ls2 * offdiag * ratios
             t3 = rr * t3 + nugget
             solved = obs - ratios * solved
             inv = 1.0 / pivots
-            half_inv = 0.5 * inv
-            c0 = c0 + t0 * half_inv
-            c1 = c1 + t1 * half_inv
-            c2 = c2 + t2 * half_inv
-            c3 = c3 + t3 * half_inv
+            c0 = c0 + 0.5 * t0 * inv
+            c1 = c1 + 0.5 * t1 * inv
+            c2 = c2 + 0.5 * t2 * inv
+            c3 = c3 + 0.5 * t3 * inv
             logs = logs + jnp.log(pivots)
             piv_ref[block, pl.ds(t, 1), :] = inv
             slv_ref[block, pl.ds(t, 1), :] = solved
@@ -141,10 +139,8 @@
             nugget = ns * weight
             offdiag = mps * coup
             values = (slv_ref[block, pl.ds(t, 1), :] - following) * piv_ref[block, pl.ds(t, 1), :]
-            pvv = prior * values * values
-            vf = values * following
-            q0 = q0 + 2.0 * pvv + 4.0 * vf
-            q1 = q1 + pvv + 2.0 * vf
+            q0 = q0 + 2.0 * prior * values * values + 4.0 * values * following
+            q1 = q1 + prior * values * values + 2.0 * values * following
             q2 = q2 + qs * rough * values * values + two_ls2 * values * following
             q3 = q3 + nugget * values * values
             out_ref[block, pl.ds(t, 1), :] = values

time: 33.9 us -> 33.9 us (level)
  no operation moved by 1% of the time
where the time goes in v15:
time: 33.9 us; the launch traced here: 33.6 us
  starting transfers between devices  12.4 us (37%)
  blocking collectives  5.61 us (17%)
  Pallas kernels  4.85 us (14%)
  local copies, waits for them, and re-layouts  3.94 us (12%)
  waiting for transfers between devices  3.45 us (10%)
  other arithmetic  2.63 us (8%)
  between operations  0.75 us (2%)
    ppermute x3, starting transfers between devices, per_device_body(): lax.ppermute(pieces[shift], 'tm', [(i, (i + shift) % time_count) for i in...  6.99 us
    all_gather x1, blocking collectives, per_device_body(): stats_full = lax.all_gather(stats_quarter, 'hyp', axis=1, tiled=True)  5.61 us
    ppermute x3, starting transfers between devices, per_device_body(): lax.ppermute(payload[shift], 'tm', [(i, (i + shift) % time_count) for i i...  3.88 us
    pallas_call x1, Pallas kernels, run_chain(): pl.pallas_call(functools.partial(chain_kernel, aligned=nodes.shape[1] !=...  3.39 us
    ppermute x3, waiting for transfers between devices, per_device_body(): lax.ppermute(payload[shift], 'tm', [(i, (i + shift) % time_count) for i i...  2.69 us
    ppermute x1, starting transfers between devices, with_halo(): got = lax.ppermute(send, axis, [(0, 1), (1, 0)])  1.53 us
    pallas_call x1, Pallas kernels, run_place(): pl.pallas_call(place_kernel, out_shape=(jax.ShapeDtypeStruct((rows, block...  1.46 us
    unnamed x20, local copies, waits for them, and re-layouts  1.29 us
  transfers between devices with their start and end apart: 7, of which 3 were waited for; matrix products, arithmetic and copies ran while one was open for 6% of the time, Pallas kernels for 0%

profile of v15, /device:TPU:0, one launch (start us, length us, event | category | flops | bytes accessed | tf_op | source)
XLA Modules:
  0.0 33.6 jit_solution(1691826297125037922)
XLA Ops:
  0.7 1.3 %pad_maximum_fusion = f32[4,16,4096]{2,1,0:T(8,128)S(1)} fusion(f32[1,16,4096]{2,1,0:T(8,128)} %bitcast.10, f32[1,16,4096]{2,1,0:T(8,128)} %bitcast.11, f32[1,16,4096]{2,1,0:T(8,128)} %bitcast.12, f32[1,16,4096]{2,1,0:T(8,128)} %bitcast.13), kind=kLoop, calls=%fused_computation | loop fusion | flops 786432 | bytes 2097152 | tf_op jit(solution)/shard_map/stack | solution.py:249
  1.9 0.0 copy-start.9
  1.9 0.0 copy-start
  2.0 0.7 %constant_dynamic-slice_fusion = (f32[4,16,256]{2,1,0:T(8,128)S(1)}, f32[4,16,256]{2,1,0:T(8,128)S(1)}, f32[4,16,256]{2,1,0:T(8,128)S(1)}, f32[4,16,256]{2,1,0:T(8,128)}) fusion(f32[4,16,4096]{2,1,0:T(8,128)S(1)} %pad_maximum_fusion, s32[]{:T(128)S(6)} %select_n.42, s32[]{:T(128)S(6)} %select_n.41, s32[]{:T(128)S(6)} %select_n.40, s32[]{:T(128)S(6)} %select_n.39), kind=kLoop, calls=%fused_computation.3 | loop fusion | bytes 524304 | tf_op jit(solution)/shard_map/dynamic_slice | solution.py:251
  2.6 3.1 %collective-permute-start.1 = (f32[4,16,256]{2,1,0:T(8,128)S(1)}, f32[4,16,256]{2,1,0:T(8,128)S(1)}, u32[]{:S(2)}, u32[]{:S(2)}) collective-permute-start(f32[4,16,256]{2,1,0:T(8,128)S(1)} %get-tuple-element.17), channel_id=1, source_target_pairs={{0,8},{8,16},{16,24},{24,0},{1,9},{9,17},{17,25},{25,1},{2,10},{10... | collective-permute-start | bytes 196616 | tf_op jit(solution)/shard_map/ppermute | solution.py:260
  5.7 2.6 %collective-permute-start.2 = (f32[4,16,256]{2,1,0:T(8,128)S(1)}, f32[4,16,256]{2,1,0:T(8,128)S(1)}, u32[]{:S(2)}, u32[]{:S(2)}) collective-permute-start(f32[4,16,256]{2,1,0:T(8,128)S(1)} %get-tuple-element.16), channel_id=1, source_target_pairs={{0,16},{8,24},{16,0},{24,8},{1,17},{9,25},{17,1},{25,9},{2,18},{10... | collective-permute-start | bytes 196616 | tf_op jit(solution)/shard_map/ppermute | solution.py:260
  8.3 1.3 %collective-permute-start.3 = (f32[4,16,256]{2,1,0:T(8,128)S(1)}, f32[4,16,256]{2,1,0:T(8,128)S(1)}, u32[]{:S(2)}, u32[]{:S(2)}) collective-permute-start(f32[4,16,256]{2,1,0:T(8,128)S(1)} %get-tuple-element.15), channel_id=1, source_target_pairs={{0,24},{8,0},{16,8},{24,16},{1,25},{9,1},{17,9},{25,17},{2,26},{10... | collective-permute-start | bytes 196616 | tf_op jit(solution)/shard_map/ppermute | solution.py:260
  9.6 0.1 broadcast_select_fusion.1
  9.7 1.5 %collective-permute-start = (f32[64]{0:T(128)S(1)}, f32[64]{0:T(128)S(1)}, u32[]{:S(2)}, u32[]{:S(2)}) collective-permute-start(f32[64]{0:T(128)S(1)} %broadcast_select_fusion.1), channel_id=1, source_target_pairs={{0,4},{4,0},{1,5},{5,1},{2,6},{6,2},{3,7},{7,3},{8,12},{12,8},{9,1... | collective-permute-start | bytes 776 | tf_op jit(solution)/shard_map/ppermute | solution.py:19
  11.2 0.6 %pad_add_fusion.refs_0_.place_ref = s32[2]{0:T(128)} fusion(s32[1]{0:T(128)} %bitcast.1, s32[1]{0:T(128)} %bitcast), kind=kLoop, calls=%fused_computation.10 | loop fusion | flops 2 | bytes 16 | tf_op jit(solution)/shard_map/stack | solution.py:267
  11.8 0.7 %pad_maximum_fusion.1.refs_3_ = f32[6,4096]{1,0:T(8,128)} fusion(f32[4,4096]{1,0:T(4,128)S(1)} %copy-done, f32[1,4096]{1,0:T(1,128)S(1)} %bitcast.15, f32[1,4096]{1,0:T(1,128)S(1)} %bitcast.16), kind=kLoop, calls=%fused_computation.1 | loop fusion | flops 49152 | bytes 196608 | tf_op jit(solution)/shard_map/concatenate | solution.py:269
  12.5 0.8 %collective-permute-done = f32[64]{0:T(128)S(1)} collective-permute-done((f32[64]{0:T(128)S(1)}, f32[64]{0:T(128)S(1)}, u32[]{:S(2)}, u32[]{:S(2)}) %collective-permute-start) | collective-permute-done | bytes 288 | tf_op jit(solution)/shard_map/ppermute | solution.py:19
  13.3 0.1 concatenate.6
  13.4 0.1 dynamic_slice.15
  13.4 0.6 %broadcast_in_dim.9.refs_2_ = f32[1,384]{1,0:T(1,128)} reshape(f32[384]{0:T(512)S(1)} %dynamic_slice.15) | data formatting | bytes 3072 | tf_op jit(solution)/shard_map/broadcast_in_dim | solution.py:268
  14.0 0.0 collective-permute-done.1.refs_6_
  14.0 0.0 collective-permute-done.2.refs_7_
  14.0 0.0 collective-permute-done.3.refs_8_
  14.1 0.6 %copy-done.1 = f32[4,16,256]{2,1,0:T(8,128)} copy-done((f32[4,16,256]{2,1,0:T(8,128)}, f32[4,16,256]{2,1,0:T(8,128)S(1)}, u32[]{:S(2)}) %copy-start.1) | copy-done | bytes 65560
  14.6 0.0 copy-done.2
  14.7 0.0 copy-done.3
  14.7 3.4 %shard_map.121 = (f32[24,256]{1,0:T(8,128)}, f32[24,256]{1,0:T(8,128)}, f32[24,256]{1,0:T(8,128)}, f32[24,256]{1,0:T(8,128)}) custom-call(s32[2]{0:T(128)} %pad_add_fusion.refs_0_.place_ref, f32[4]{0:T(128)} %refs_1_.1, f32[1,384]{1,0:T(1,128)} %broadcast_in_dim.9.refs_2_, f32[6,4096]{1,0:T(8,128)} %pad_maximum_fusion.1.refs_3_, s32[4,4096]{1,0:T(4,128)} %refs_4_.1, ...), custom_call_target="tpu_custom_call" | custom-call | tf_op jit(solution)/shard_map/pallas_call | solution.py:175
  18.1 0.7 %collective-permute-start.4 = (f32[24,256]{1,0:T(8,128)}, f32[24,256]{1,0:T(8,128)S(1)}, u32[]{:S(2)}, u32[]{:S(2)}) collective-permute-start(f32[24,256]{1,0:T(8,128)} %get-tuple-element.10), channel_id=1, source_target_pairs={{0,8},{8,16},{16,24},{24,0},{1,9},{9,17},{17,25},{25,1},{2,10},{10... | collective-permute-start | bytes 73736 | tf_op jit(solution)/shard_map/ppermute | solution.py:276
  18.8 1.8 %collective-permute-start.5 = (f32[24,256]{1,0:T(8,128)}, f32[24,256]{1,0:T(8,128)S(1)}, u32[]{:S(2)}, u32[]{:S(2)}) collective-permute-start(f32[24,256]{1,0:T(8,128)} %get-tuple-element.11), channel_id=1, source_target_pairs={{0,16},{8,24},{16,0},{24,8},{1,17},{9,25},{17,1},{25,9},{2,18},{10... | collective-permute-start | bytes 73736 | tf_op jit(solution)/shard_map/ppermute | solution.py:276
  20.6 1.3 %collective-permute-start.6 = (f32[24,256]{1,0:T(8,128)}, f32[24,256]{1,0:T(8,128)S(1)}, u32[]{:S(2)}, u32[]{:S(2)}) collective-permute-start(f32[24,256]{1,0:T(8,128)} %get-tuple-element.12), channel_id=1, source_target_pairs={{0,24},{8,0},{16,8},{24,16},{1,25},{9,1},{17,9},{25,17},{2,26},{10... | collective-permute-start | bytes 73736 | tf_op jit(solution)/shard_map/ppermute | solution.py:276
  22.0 2.0 %collective-permute-done.4.refs_1_ = f32[24,256]{1,0:T(8,128)S(1)} collective-permute-done((f32[24,256]{1,0:T(8,128)}, f32[24,256]{1,0:T(8,128)S(1)}, u32[]{:S(2)}, u32[]{:S(2)}) %collective-permute-start.4) | collective-permute-done | bytes 24608 | tf_op jit(solution)/shard_map/ppermute | solution.py:276
  24.0 0.6 %collective-permute-done.6.refs_3_ = f32[24,256]{1,0:T(8,128)S(1)} collective-permute-done((f32[24,256]{1,0:T(8,128)}, f32[24,256]{1,0:T(8,128)S(1)}, u32[]{:S(2)}, u32[]{:S(2)}) %collective-permute-start.6) | collective-permute-done | bytes 24608 | tf_op jit(solution)/shard_map/ppermute | solution.py:276
  24.7 0.6 %copy-done.6 = f32[24,256]{1,0:T(8,128)} copy-done((f32[24,256]{1,0:T(8,128)}, f32[24,256]{1,0:T(8,128)S(1)}, u32[]{:S(2)}) %copy-start.6) | copy-done | bytes 24600
  25.3 1.5 %shard_map.122 = (f32[16,1024]{1,0:T(8,128)}, f32[8,1024]{1,0:T(8,128)}) custom-call(s32[2]{0:T(128)} %pad_add_fusion.refs_0_.place_ref, f32[24,256]{1,0:T(8,128)} %get-tuple-element.9.refs_0_, f32[24,256]{1,0:T(8,128)} %copy-done.4, f32[24,256]{1,0:T(8,128)} %copy-done.5, f32[24,256]{1,0:T(8,128)} %copy-done.6), custom_call_target="tpu_custom_call" | custom-call | tf_op jit(solution)/shard_map/pallas_call | solution.py:213
  26.7 5.6 %all_gather.3 = f32[5,4096]{1,0:T(8,128)S(1)} all-gather(f32[5,1024]{1,0:T(8,128)} %bitcast.14), channel_id=1, replica_groups=mesh['tm'=4,'space'=2,'hyp'=4] {'hyp'}, dimensions={1}, use_global_device_ids=true | all-gather | bytes 102400 | tf_op jit(solution)/shard_map/all_gather | solution.py:294
  32.4 0.6 %slice.23 = f32[4,4096]{1,0:T(4,128)} slice(f32[5,4096]{1,0:T(8,128)S(1)} %all_gather.3), slice={[1:5], [0:4096]} | slice | bytes 131072 | tf_op jit(solution)/shard_map/slice | solution.py:295
  33.0 0.6 %slice.22 = f32[1,4096]{1,0:T(1,128)} slice(f32[5,4096]{1,0:T(8,128)S(1)} %all_gather.3), slice={[0:1], [0:4096]} | slice | bytes 32768 | tf_op jit(solution)/shard_map/slice | solution.py:295
  (17 shorter events, 0.0 us)
Async XLA Ops:
  1.9 7.7 %copy-start.9 = (f32[4096]{0:T(1024)S(1)}, f32[4096]{0:T(1024)}, u32[]{:S(2)}) copy-start(f32[4096]{0:T(1024)} %param.10) | copy-start | bytes 49156
  1.9 9.9 %copy-start = (f32[4,4096]{1,0:T(4,128)S(1)}, f32[4,4096]{1,0:T(4,128)}, u32[]{:S(2)}) copy-start(f32[4,4096]{1,0:T(4,128)} %param.13) | copy-start | bytes 196612
  2.6 11.4 %collective-permute-start.1 = (f32[4,16,256]{2,1,0:T(8,128)S(1)}, f32[4,16,256]{2,1,0:T(8,128)S(1)}, u32[]{:S(2)}, u32[]{:S(2)}) collective-permute-start(f32[4,16,256]{2,1,0:T(8,128)S(1)} %get-tuple-element.17), channel_id=1, source_target_pairs={{0,8},{8,16},{16,24},{24,0},{1,9},{9,17},{17,25},{25,1},{2,10},{10... | collective-permute-start | bytes 196616 | tf_op jit(solution)/shard_map/ppermute | solution.py:260
  5.7 8.3 %collective-permute-start.2 = (f32[4,16,256]{2,1,0:T(8,128)S(1)}, f32[4,16,256]{2,1,0:T(8,128)S(1)}, u32[]{:S(2)}, u32[]{:S(2)}) collective-permute-start(f32[4,16,256]{2,1,0:T(8,128)S(1)} %get-tuple-element.16), channel_id=1, source_target_pairs={{0,16},{8,24},{16,0},{24,8},{1,17},{9,25},{17,1},{25,9},{2,18},{10... | collective-permute-start | bytes 196616 | tf_op jit(solution)/shard_map/ppermute | solution.py:260
  8.3 5.8 %collective-permute-start.3 = (f32[4,16,256]{2,1,0:T(8,128)S(1)}, f32[4,16,256]{2,1,0:T(8,128)S(1)}, u32[]{:S(2)}, u32[]{:S(2)}) collective-permute-start(f32[4,16,256]{2,1,0:T(8,128)S(1)} %get-tuple-element.15), channel_id=1, source_target_pairs={{0,24},{8,0},{16,8},{24,16},{1,25},{9,1},{17,9},{25,17},{2,26},{10... | collective-permute-start | bytes 196616 | tf_op jit(solution)/shard_map/ppermute | solution.py:260
  9.6 2.2 %copy-start.7 = (f32[4096]{0:T(1024)S(1)}, f32[4096]{0:T(1024)}, u32[]{:S(2)}) copy-start(f32[4096]{0:T(1024)} %param.12) | copy-start | bytes 49156
  9.6 2.2 %copy-start.8 = (f32[4096]{0:T(1024)S(1)}, f32[4096]{0:T(1024)}, u32[]{:S(2)}) copy-start(f32[4096]{0:T(1024)} %param.11) | copy-start | bytes 49156
  9.7 3.6 %collective-permute-start = (f32[64]{0:T(128)S(1)}, f32[64]{0:T(128)S(1)}, u32[]{:S(2)}, u32[]{:S(2)}) collective-permute-start(f32[64]{0:T(128)S(1)} %broadcast_select_fusion.1), channel_id=1, source_target_pairs={{0,4},{4,0},{1,5},{5,1},{2,6},{6,2},{3,7},{7,3},{8,12},{12,8},{9,1... | collective-permute-start | bytes 776 | tf_op jit(solution)/shard_map/ppermute | solution.py:19
  14.0 0.6 %copy-start.1 = (f32[4,16,256]{2,1,0:T(8,128)}, f32[4,16,256]{2,1,0:T(8,128)S(1)}, u32[]{:S(2)}) copy-start(f32[4,16,256]{2,1,0:T(8,128)S(1)} %collective-permute-done.1.refs_6_) | copy-start | bytes 196612
  14.0 0.6 %copy-start.2 = (f32[4,16,256]{2,1,0:T(8,128)}, f32[4,16,256]{2,1,0:T(8,128)S(1)}, u32[]{:S(2)}) copy-start(f32[4,16,256]{2,1,0:T(8,128)S(1)} %collective-permute-done.2.refs_7_) | copy-start | bytes 196612
  14.0 0.7 %copy-start.3 = (f32[4,16,256]{2,1,0:T(8,128)}, f32[4,16,256]{2,1,0:T(8,128)S(1)}, u32[]{:S(2)}) copy-start(f32[4,16,256]{2,1,0:T(8,128)S(1)} %collective-permute-done.3.refs_8_) | copy-start | bytes 196612
  18.1 5.9 %collective-permute-start.4 = (f32[24,256]{1,0:T(8,128)}, f32[24,256]{1,0:T(8,128)S(1)}, u32[]{:S(2)}, u32[]{:S(2)}) collective-permute-start(f32[24,256]{1,0:T(8,128)} %get-tuple-element.10), channel_id=1, source_target_pairs={{0,8},{8,16},{16,24},{24,0},{1,9},{9,17},{17,25},{25,1},{2,10},{10... | collective-permute-start | bytes 73736 | tf_op jit(solution)/shard_map/ppermute | solution.py:276
  18.8 5.2 %collective-permute-start.5 = (f32[24,256]{1,0:T(8,128)}, f32[24,256]{1,0:T(8,128)S(1)}, u32[]{:S(2)}, u32[]{:S(2)}) collective-permute-start(f32[24,256]{1,0:T(8,128)} %get-tuple-element.11), channel_id=1, source_target_pairs={{0,16},{8,24},{16,0},{24,8},{1,17},{9,25},{17,1},{25,9},{2,18},{10... | collective-permute-start | bytes 73736 | tf_op jit(solution)/shard_map/ppermute | solution.py:276
  20.6 4.0 %collective-permute-start.6 = (f32[24,256]{1,0:T(8,128)}, f32[24,256]{1,0:T(8,128)S(1)}, u32[]{:S(2)}, u32[]{:S(2)}) collective-permute-start(f32[24,256]{1,0:T(8,128)} %get-tuple-element.12), channel_id=1, source_target_pairs={{0,24},{8,0},{16,8},{24,16},{1,25},{9,1},{17,9},{25,17},{2,26},{10... | collective-permute-start | bytes 73736 | tf_op jit(solution)/shard_map/ppermute | solution.py:276
  24.0 0.6 %copy-start.4 = (f32[24,256]{1,0:T(8,128)}, f32[24,256]{1,0:T(8,128)S(1)}, u32[]{:S(2)}) copy-start(f32[24,256]{1,0:T(8,128)S(1)} %collective-permute-done.4.refs_1_) | copy-start | bytes 73732
  24.0 0.6 %copy-start.5 = (f32[24,256]{1,0:T(8,128)}, f32[24,256]{1,0:T(8,128)S(1)}, u32[]{:S(2)}) copy-start(f32[24,256]{1,0:T(8,128)S(1)} %collective-permute-done.5.refs_2_) | copy-start | bytes 73732
  24.7 0.6 %copy-start.6 = (f32[24,256]{1,0:T(8,128)}, f32[24,256]{1,0:T(8,128)S(1)}, u32[]{:S(2)}) copy-start(f32[24,256]{1,0:T(8,128)S(1)} %collective-permute-done.6.refs_3_) | copy-start | bytes 73732

commit v16 on v15

--- a/solution.py
+++ b/solution.py
@@ -256,14 +256,15 @@
         )
         for shift in range(time_count)
     ]
-    arrived = [pieces[0]] + [
-        lax.ppermute(
-            pieces[shift],
-            "tm",
-            [(i, (i + shift) % time_count) for i in range(time_count)],
+    arrived = [pieces[0]]
+    for shift in range(1, time_count):
+        arrived.append(
+            lax.ppermute(
+                pieces[shift],
+                "tm",
+                [(i, (i + shift) % time_count) for i in range(time_count)],
+            )
         )
-        for shift in range(1, time_count)
-    ]
     place = jnp.stack([time_place, first]).astype(jnp.int32)
     window = lax.dynamic_slice_in_dim(padded, first, chunk + 2 * BAND)[None]
     nodes = jnp.concatenate([node_mass[None], rho_base[None], edge_weight], axis=0)

time: 33.9 us -> 33.9 us (level)
  no operation moved by 1% of the time
where the time goes in v16:
time: 33.9 us; the launch traced here: 33.6 us
  starting transfers between devices  12.4 us (37%)
  blocking collectives  5.61 us (17%)
  Pallas kernels  4.85 us (14%)
  local copies, waits for them, and re-layouts  3.94 us (12%)
  waiting for transfers between devices  3.45 us (10%)
  other arithmetic  2.63 us (8%)
  between operations  0.75 us (2%)
    ppermute x3, starting transfers between devices, per_device_body(): lax.ppermute(pieces[shift], 'tm', [(i, (i + shift) % time_count) for i in...  6.99 us
    all_gather x1, blocking collectives, per_device_body(): stats_full = lax.all_gather(stats_quarter, 'hyp', axis=1, tiled=True)  5.61 us
    ppermute x3, starting transfers between devices, per_device_body(): lax.ppermute(payload[shift], 'tm', [(i, (i + shift) % time_count) for i i...  3.88 us
    pallas_call x1, Pallas kernels, run_chain(): pl.pallas_call(functools.partial(chain_kernel, aligned=nodes.shape[1] !=...  3.39 us
    ppermute x3, waiting for transfers between devices, per_device_body(): lax.ppermute(payload[shift], 'tm', [(i, (i + shift) % time_count) for i i...  2.69 us
    ppermute x1, starting transfers between devices, with_halo(): got = lax.ppermute(send, axis, [(0, 1), (1, 0)])  1.53 us
    pallas_call x1, Pallas kernels, run_place(): pl.pallas_call(place_kernel, out_shape=(jax.ShapeDtypeStruct((rows, block...  1.46 us
    unnamed x20, local copies, waits for them, and re-layouts  1.29 us
  transfers between devices with their start and end apart: 7, of which 3 were waited for; matrix products, arithmetic and copies ran while one was open for 6% of the time, Pallas kernels for 0%

profile of v16, /device:TPU:0, one launch (start us, length us, event | category | flops | bytes accessed | tf_op | source)
XLA Modules:
  0.0 33.6 jit_solution(1691826297125037922)
XLA Ops:
  0.7 1.3 %pad_maximum_fusion = f32[4,16,4096]{2,1,0:T(8,128)S(1)} fusion(f32[1,16,4096]{2,1,0:T(8,128)} %bitcast.10, f32[1,16,4096]{2,1,0:T(8,128)} %bitcast.11, f32[1,16,4096]{2,1,0:T(8,128)} %bitcast.12, f32[1,16,4096]{2,1,0:T(8,128)} %bitcast.13), kind=kLoop, calls=%fused_computation | loop fusion | flops 786432 | bytes 2097152 | tf_op jit(solution)/shard_map/stack | solution.py:249
  1.9 0.0 copy-start.9
  1.9 0.0 copy-start
  2.0 0.7 %constant_dynamic-slice_fusion = (f32[4,16,256]{2,1,0:T(8,128)S(1)}, f32[4,16,256]{2,1,0:T(8,128)S(1)}, f32[4,16,256]{2,1,0:T(8,128)S(1)}, f32[4,16,256]{2,1,0:T(8,128)}) fusion(f32[4,16,4096]{2,1,0:T(8,128)S(1)} %pad_maximum_fusion, s32[]{:T(128)S(6)} %select_n.42, s32[]{:T(128)S(6)} %select_n.41, s32[]{:T(128)S(6)} %select_n.40, s32[]{:T(128)S(6)} %select_n.39), kind=kLoop, calls=%fused_computation.3 | loop fusion | bytes 524304 | tf_op jit(solution)/shard_map/dynamic_slice | solution.py:251
  2.6 3.1 %collective-permute-start.1 = (f32[4,16,256]{2,1,0:T(8,128)S(1)}, f32[4,16,256]{2,1,0:T(8,128)S(1)}, u32[]{:S(2)}, u32[]{:S(2)}) collective-permute-start(f32[4,16,256]{2,1,0:T(8,128)S(1)} %get-tuple-element.17), channel_id=1, source_target_pairs={{0,8},{8,16},{16,24},{24,0},{1,9},{9,17},{17,25},{25,1},{2,10},{10... | collective-permute-start | bytes 196616 | tf_op jit(solution)/shard_map/ppermute | solution.py:262
  5.7 2.6 %collective-permute-start.2 = (f32[4,16,256]{2,1,0:T(8,128)S(1)}, f32[4,16,256]{2,1,0:T(8,128)S(1)}, u32[]{:S(2)}, u32[]{:S(2)}) collective-permute-start(f32[4,16,256]{2,1,0:T(8,128)S(1)} %get-tuple-element.16), channel_id=1, source_target_pairs={{0,16},{8,24},{16,0},{24,8},{1,17},{9,25},{17,1},{25,9},{2,18},{10... | collective-permute-start | bytes 196616 | tf_op jit(solution)/shard_map/ppermute | solution.py:262
  8.3 1.3 %collective-permute-start.3 = (f32[4,16,256]{2,1,0:T(8,128)S(1)}, f32[4,16,256]{2,1,0:T(8,128)S(1)}, u32[]{:S(2)}, u32[]{:S(2)}) collective-permute-start(f32[4,16,256]{2,1,0:T(8,128)S(1)} %get-tuple-element.15), channel_id=1, source_target_pairs={{0,24},{8,0},{16,8},{24,16},{1,25},{9,1},{17,9},{25,17},{2,26},{10... | collective-permute-start | bytes 196616 | tf_op jit(solution)/shard_map/ppermute | solution.py:262
  9.6 0.1 broadcast_select_fusion.1
  9.7 1.5 %collective-permute-start = (f32[64]{0:T(128)S(1)}, f32[64]{0:T(128)S(1)}, u32[]{:S(2)}, u32[]{:S(2)}) collective-permute-start(f32[64]{0:T(128)S(1)} %broadcast_select_fusion.1), channel_id=1, source_target_pairs={{0,4},{4,0},{1,5},{5,1},{2,6},{6,2},{3,7},{7,3},{8,12},{12,8},{9,1... | collective-permute-start | bytes 776 | tf_op jit(solution)/shard_map/ppermute | solution.py:19
  11.2 0.6 %pad_add_fusion.refs_0_.place_ref = s32[2]{0:T(128)} fusion(s32[1]{0:T(128)} %bitcast.1, s32[1]{0:T(128)} %bitcast), kind=kLoop, calls=%fused_computation.10 | loop fusion | flops 2 | bytes 16 | tf_op jit(solution)/shard_map/stack | solution.py:268
  11.8 0.7 %pad_maximum_fusion.1.refs_3_ = f32[6,4096]{1,0:T(8,128)} fusion(f32[4,4096]{1,0:T(4,128)S(1)} %copy-done, f32[1,4096]{1,0:T(1,128)S(1)} %bitcast.15, f32[1,4096]{1,0:T(1,128)S(1)} %bitcast.16), kind=kLoop, calls=%fused_computation.1 | loop fusion | flops 49152 | bytes 196608 | tf_op jit(solution)/shard_map/concatenate | solution.py:270
  12.5 0.8 %collective-permute-done = f32[64]{0:T(128)S(1)} collective-permute-done((f32[64]{0:T(128)S(1)}, f32[64]{0:T(128)S(1)}, u32[]{:S(2)}, u32[]{:S(2)}) %collective-permute-start) | collective-permute-done | bytes 288 | tf_op jit(solution)/shard_map/ppermute | solution.py:19
  13.3 0.1 concatenate.6
  13.4 0.1 dynamic_slice.15
  13.4 0.6 %broadcast_in_dim.9.refs_2_ = f32[1,384]{1,0:T(1,128)} reshape(f32[384]{0:T(512)S(1)} %dynamic_slice.15) | data formatting | bytes 3072 | tf_op jit(solution)/shard_map/broadcast_in_dim | solution.py:269
  14.0 0.0 collective-permute-done.1.refs_6_
  14.0 0.0 collective-permute-done.2.refs_7_
  14.0 0.0 collective-permute-done.3.refs_8_
  14.1 0.6 %copy-done.1 = f32[4,16,256]{2,1,0:T(8,128)} copy-done((f32[4,16,256]{2,1,0:T(8,128)}, f32[4,16,256]{2,1,0:T(8,128)S(1)}, u32[]{:S(2)}) %copy-start.1) | copy-done | bytes 65560
  14.6 0.0 copy-done.2
  14.7 0.0 copy-done.3
  14.7 3.4 %shard_map.121 = (f32[24,256]{1,0:T(8,128)}, f32[24,256]{1,0:T(8,128)}, f32[24,256]{1,0:T(8,128)}, f32[24,256]{1,0:T(8,128)}) custom-call(s32[2]{0:T(128)} %pad_add_fusion.refs_0_.place_ref, f32[4]{0:T(128)} %refs_1_.1, f32[1,384]{1,0:T(1,128)} %broadcast_in_dim.9.refs_2_, f32[6,4096]{1,0:T(8,128)} %pad_maximum_fusion.1.refs_3_, s32[4,4096]{1,0:T(4,128)} %refs_4_.1, ...), custom_call_target="tpu_custom_call" | custom-call | tf_op jit(solution)/shard_map/pallas_call | solution.py:175
  18.1 0.7 %collective-permute-start.4 = (f32[24,256]{1,0:T(8,128)}, f32[24,256]{1,0:T(8,128)S(1)}, u32[]{:S(2)}, u32[]{:S(2)}) collective-permute-start(f32[24,256]{1,0:T(8,128)} %get-tuple-element.10), channel_id=1, source_target_pairs={{0,8},{8,16},{16,24},{24,0},{1,9},{9,17},{17,25},{25,1},{2,10},{10... | collective-permute-start | bytes 73736 | tf_op jit(solution)/shard_map/ppermute | solution.py:277
  18.8 1.8 %collective-permute-start.5 = (f32[24,256]{1,0:T(8,128)}, f32[24,256]{1,0:T(8,128)S(1)}, u32[]{:S(2)}, u32[]{:S(2)}) collective-permute-start(f32[24,256]{1,0:T(8,128)} %get-tuple-element.11), channel_id=1, source_target_pairs={{0,16},{8,24},{16,0},{24,8},{1,17},{9,25},{17,1},{25,9},{2,18},{10... | collective-permute-start | bytes 73736 | tf_op jit(solution)/shard_map/ppermute | solution.py:277
  20.6 1.3 %collective-permute-start.6 = (f32[24,256]{1,0:T(8,128)}, f32[24,256]{1,0:T(8,128)S(1)}, u32[]{:S(2)}, u32[]{:S(2)}) collective-permute-start(f32[24,256]{1,0:T(8,128)} %get-tuple-element.12), channel_id=1, source_target_pairs={{0,24},{8,0},{16,8},{24,16},{1,25},{9,1},{17,9},{25,17},{2,26},{10... | collective-permute-start | bytes 73736 | tf_op jit(solution)/shard_map/ppermute | solution.py:277
  22.0 2.0 %collective-permute-done.4.refs_1_ = f32[24,256]{1,0:T(8,128)S(1)} collective-permute-done((f32[24,256]{1,0:T(8,128)}, f32[24,256]{1,0:T(8,128)S(1)}, u32[]{:S(2)}, u32[]{:S(2)}) %collective-permute-start.4) | collective-permute-done | bytes 24608 | tf_op jit(solution)/shard_map/ppermute | solution.py:277
  24.0 0.6 %collective-permute-done.6.refs_3_ = f32[24,256]{1,0:T(8,128)S(1)} collective-permute-done((f32[24,256]{1,0:T(8,128)}, f32[24,256]{1,0:T(8,128)S(1)}, u32[]{:S(2)}, u32[]{:S(2)}) %collective-permute-start.6) | collective-permute-done | bytes 24608 | tf_op jit(solution)/shard_map/ppermute | solution.py:277
  24.7 0.6 %copy-done.6 = f32[24,256]{1,0:T(8,128)} copy-done((f32[24,256]{1,0:T(8,128)}, f32[24,256]{1,0:T(8,128)S(1)}, u32[]{:S(2)}) %copy-start.6) | copy-done | bytes 24600
  25.3 1.5 %shard_map.122 = (f32[16,1024]{1,0:T(8,128)}, f32[8,1024]{1,0:T(8,128)}) custom-call(s32[2]{0:T(128)} %pad_add_fusion.refs_0_.place_ref, f32[24,256]{1,0:T(8,128)} %get-tuple-element.9.refs_0_, f32[24,256]{1,0:T(8,128)} %copy-done.4, f32[24,256]{1,0:T(8,128)} %copy-done.5, f32[24,256]{1,0:T(8,128)} %copy-done.6), custom_call_target="tpu_custom_call" | custom-call | tf_op jit(solution)/shard_map/pallas_call | solution.py:213
  26.7 5.6 %all_gather.3 = f32[5,4096]{1,0:T(8,128)S(1)} all-gather(f32[5,1024]{1,0:T(8,128)} %bitcast.14), channel_id=1, replica_groups=mesh['tm'=4,'space'=2,'hyp'=4] {'hyp'}, dimensions={1}, use_global_device_ids=true | all-gather | bytes 102400 | tf_op jit(solution)/shard_map/all_gather | solution.py:295
  32.4 0.6 %slice.23 = f32[4,4096]{1,0:T(4,128)} slice(f32[5,4096]{1,0:T(8,128)S(1)} %all_gather.3), slice={[1:5], [0:4096]} | slice | bytes 131072 | tf_op jit(solution)/shard_map/slice | solution.py:296
  33.0 0.6 %slice.22 = f32[1,4096]{1,0:T(1,128)} slice(f32[5,4096]{1,0:T(8,128)S(1)} %all_gather.3), slice={[0:1], [0:4096]} | slice | bytes 32768 | tf_op jit(solution)/shard_map/slice | solution.py:296
  (17 shorter events, 0.0 us)
Async XLA Ops:
  1.9 7.7 %copy-start.9 = (f32[4096]{0:T(1024)S(1)}, f32[4096]{0:T(1024)}, u32[]{:S(2)}) copy-start(f32[4096]{0:T(1024)} %param.10) | copy-start | bytes 49156
  1.9 9.9 %copy-start = (f32[4,4096]{1,0:T(4,128)S(1)}, f32[4,4096]{1,0:T(4,128)}, u32[]{:S(2)}) copy-start(f32[4,4096]{1,0:T(4,128)} %param.13) | copy-start | bytes 196612
  2.6 11.4 %collective-permute-start.1 = (f32[4,16,256]{2,1,0:T(8,128)S(1)}, f32[4,16,256]{2,1,0:T(8,128)S(1)}, u32[]{:S(2)}, u32[]{:S(2)}) collective-permute-start(f32[4,16,256]{2,1,0:T(8,128)S(1)} %get-tuple-element.17), channel_id=1, source_target_pairs={{0,8},{8,16},{16,24},{24,0},{1,9},{9,17},{17,25},{25,1},{2,10},{10... | collective-permute-start | bytes 196616 | tf_op jit(solution)/shard_map/ppermute | solution.py:262
  5.7 8.3 %collective-permute-start.2 = (f32[4,16,256]{2,1,0:T(8,128)S(1)}, f32[4,16,256]{2,1,0:T(8,128)S(1)}, u32[]{:S(2)}, u32[]{:S(2)}) collective-permute-start(f32[4,16,256]{2,1,0:T(8,128)S(1)} %get-tuple-element.16), channel_id=1, source_target_pairs={{0,16},{8,24},{16,0},{24,8},{1,17},{9,25},{17,1},{25,9},{2,18},{10... | collective-permute-start | bytes 196616 | tf_op jit(solution)/shard_map/ppermute | solution.py:262
  8.3 5.8 %collective-permute-start.3 = (f32[4,16,256]{2,1,0:T(8,128)S(1)}, f32[4,16,256]{2,1,0:T(8,128)S(1)}, u32[]{:S(2)}, u32[]{:S(2)}) collective-permute-start(f32[4,16,256]{2,1,0:T(8,128)S(1)} %get-tuple-element.15), channel_id=1, source_target_pairs={{0,24},{8,0},{16,8},{24,16},{1,25},{9,1},{17,9},{25,17},{2,26},{10... | collective-permute-start | bytes 196616 | tf_op jit(solution)/shard_map/ppermute | solution.py:262
  9.6 2.2 %copy-start.7 = (f32[4096]{0:T(1024)S(1)}, f32[4096]{0:T(1024)}, u32[]{:S(2)}) copy-start(f32[4096]{0:T(1024)} %param.12) | copy-start | bytes 49156
  9.6 2.2 %copy-start.8 = (f32[4096]{0:T(1024)S(1)}, f32[4096]{0:T(1024)}, u32[]{:S(2)}) copy-start(f32[4096]{0:T(1024)} %param.11) | copy-start | bytes 49156
  9.7 3.6 %collective-permute-start = (f32[64]{0:T(128)S(1)}, f32[64]{0:T(128)S(1)}, u32[]{:S(2)}, u32[]{:S(2)}) collective-permute-start(f32[64]{0:T(128)S(1)} %broadcast_select_fusion.1), channel_id=1, source_target_pairs={{0,4},{4,0},{1,5},{5,1},{2,6},{6,2},{3,7},{7,3},{8,12},{12,8},{9,1... | collective-permute-start | bytes 776 | tf_op jit(solution)/shard_map/ppermute | solution.py:19
  14.0 0.6 %copy-start.1 = (f32[4,16,256]{2,1,0:T(8,128)}, f32[4,16,256]{2,1,0:T(8,128)S(1)}, u32[]{:S(2)}) copy-start(f32[4,16,256]{2,1,0:T(8,128)S(1)} %collective-permute-done.1.refs_6_) | copy-start | bytes 196612
  14.0 0.6 %copy-start.2 = (f32[4,16,256]{2,1,0:T(8,128)}, f32[4,16,256]{2,1,0:T(8,128)S(1)}, u32[]{:S(2)}) copy-start(f32[4,16,256]{2,1,0:T(8,128)S(1)} %collective-permute-done.2.refs_7_) | copy-start | bytes 196612
  14.0 0.7 %copy-start.3 = (f32[4,16,256]{2,1,0:T(8,128)}, f32[4,16,256]{2,1,0:T(8,128)S(1)}, u32[]{:S(2)}) copy-start(f32[4,16,256]{2,1,0:T(8,128)S(1)} %collective-permute-done.3.refs_8_) | copy-start | bytes 196612
  18.1 5.9 %collective-permute-start.4 = (f32[24,256]{1,0:T(8,128)}, f32[24,256]{1,0:T(8,128)S(1)}, u32[]{:S(2)}, u32[]{:S(2)}) collective-permute-start(f32[24,256]{1,0:T(8,128)} %get-tuple-element.10), channel_id=1, source_target_pairs={{0,8},{8,16},{16,24},{24,0},{1,9},{9,17},{17,25},{25,1},{2,10},{10... | collective-permute-start | bytes 73736 | tf_op jit(solution)/shard_map/ppermute | solution.py:277
  18.8 5.2 %collective-permute-start.5 = (f32[24,256]{1,0:T(8,128)}, f32[24,256]{1,0:T(8,128)S(1)}, u32[]{:S(2)}, u32[]{:S(2)}) collective-permute-start(f32[24,256]{1,0:T(8,128)} %get-tuple-element.11), channel_id=1, source_target_pairs={{0,16},{8,24},{16,0},{24,8},{1,17},{9,25},{17,1},{25,9},{2,18},{10... | collective-permute-start | bytes 73736 | tf_op jit(solution)/shard_map/ppermute | solution.py:277
  20.6 4.0 %collective-permute-start.6 = (f32[24,256]{1,0:T(8,128)}, f32[24,256]{1,0:T(8,128)S(1)}, u32[]{:S(2)}, u32[]{:S(2)}) collective-permute-start(f32[24,256]{1,0:T(8,128)} %get-tuple-element.12), channel_id=1, source_target_pairs={{0,24},{8,0},{16,8},{24,16},{1,25},{9,1},{17,9},{25,17},{2,26},{10... | collective-permute-start | bytes 73736 | tf_op jit(solution)/shard_map/ppermute | solution.py:277
  24.0 0.6 %copy-start.4 = (f32[24,256]{1,0:T(8,128)}, f32[24,256]{1,0:T(8,128)S(1)}, u32[]{:S(2)}) copy-start(f32[24,256]{1,0:T(8,128)S(1)} %collective-permute-done.4.refs_1_) | copy-start | bytes 73732
  24.0 0.6 %copy-start.5 = (f32[24,256]{1,0:T(8,128)}, f32[24,256]{1,0:T(8,128)S(1)}, u32[]{:S(2)}) copy-start(f32[24,256]{1,0:T(8,128)S(1)} %collective-permute-done.5.refs_2_) | copy-start | bytes 73732
  24.7 0.6 %copy-start.6 = (f32[24,256]{1,0:T(8,128)}, f32[24,256]{1,0:T(8,128)S(1)}, u32[]{:S(2)}) copy-start(f32[24,256]{1,0:T(8,128)S(1)} %collective-permute-done.6.refs_3_) | copy-start | bytes 73732
